TPU v7x, 1024 devices: a whole 8x8x8 slice. The times are simulated.
1024 devices in a mesh: ctx: 64 (over x, y), head: 16 (over z, core).
Axes of the slice: x: 8, y: 8, z: 8, core: 2. Of those that a mesh axis runs over, the one named last changes fastest.
Arguments:
- queries: bfloat16 [8192, 4096], P(('ctx', 'head')), may hold values from -6 to 6
- keys: bfloat16 [8192, 4096], P(('ctx', 'head')), may hold values from -6 to 6
- values: bfloat16 [8192, 8192], P(('ctx', 'head')), may hold values from -6 to 6
- grad_out: bfloat16 [8192, 8192], P('ctx', 'head'), may hold values from -6 to 6
- log_decay: float32 [16, 8192], P('head', 'ctx'), may hold values from -1 to 0
- doc_lengths: int32 [32], replicated, may hold values from 1 to 2048, 8192 in all
Outputs:
- retained: bfloat16 [8192, 8192], P('ctx', 'head')
- query_gradient: bfloat16 [8192, 4096], P('ctx', 'head')
- grad_k: bfloat16 [8192, 4096], P('ctx', 'head')
- value_gradient: bfloat16 [8192, 8192], P('ctx', 'head')
Inputs may be any that keep to these rules, and one draw needn't show every extreme that they name: `doc_lengths`: the 32 lengths sum to 8192; the largest is exactly 2048.
All inputs are finite; a program needn't handle non-finite values.
Results may differ from a plain program's by a relative error of at most 0.0056.
Values may be sent and summed in bfloat16 or wider, within the bound.
No kernel may reach another device: no remote copies, remote signals or barrier semaphores. Data moves between devices by JAX's collectives and lax.ppermute only.
A program may use at most 32 MiB of HBM per device.

v0:
```python
import jax
import jax.numpy as jnp
from jax import lax
from jax.sharding import PartitionSpec as P

BLOCK = 128


def passed_along(block, axis, distance):
    devices = range(lax.axis_size(axis))
    route = [(i - distance, i) for i in devices if i - distance in devices]
    return lax.ppermute(block, axis, route)


def document_ids(doc_lengths, first_place, span_length):
    starts = jnp.cumsum(doc_lengths, dtype=jnp.int32) - doc_lengths
    places = first_place - 1 + jnp.arange(span_length + 1, dtype=jnp.int32)
    return jnp.sum((starts[None, :] <= places[:, None]).astype(jnp.int32), axis=1) - 1


def decay_tables(log_rates, doc_ids, block_size, score_scaling):
    block_count = log_rates.shape[0] // block_size
    cumulated = jnp.cumsum(log_rates.reshape(block_count, block_size), axis=1)
    before = doc_ids[0 : block_count * block_size : block_size]
    own_ids = doc_ids[1:].reshape(block_count, block_size)
    carried = (own_ids == before[:, None]).astype(jnp.float32)
    last_ids = own_ids[:, block_size - 1]
    tail_mask = (own_ids == last_ids[:, None]).astype(jnp.float32)
    block_decay = jnp.exp(cumulated[:, block_size - 1]) * carried[:, block_size - 1]
    row_index = lax.broadcasted_iota(jnp.int32, (block_size, block_size), 0)
    column_index = lax.broadcasted_iota(jnp.int32, (block_size, block_size), 1)
    inside = (own_ids[:, :, None] == own_ids[:, None, :]) & (row_index >= column_index)[None]
    decay_gaps = cumulated[:, :, None] - cumulated[:, None, :]
    weights = jnp.where(inside, jnp.exp(jnp.where(inside, decay_gaps, 0.0)), 0.0) * score_scaling
    per_head_decay_rate = jnp.exp(cumulated) * carried
    tail_decay = jnp.exp(cumulated[:, block_size - 1 :] - cumulated) * tail_mask
    return (weights, per_head_decay_rate, tail_decay, block_decay)


def chain_combine(earlier, follower):
    return (earlier[0] * follower[0], follower[0] * earlier[1] + follower[1])


def offset_list(shard_total):
    return [1] + [1 << level for level in range((shard_total - 1).bit_length())]


def per_device(queries, keys, values, grad_out, log_decay, doc_lengths):
    query_rows, key_rows, value_rows = (
        lax.all_to_all(queries, "head", split_axis=1, concat_axis=0, tiled=True),
        lax.all_to_all(keys, "head", split_axis=1, concat_axis=0, tiled=True),
        lax.all_to_all(values, "head", split_axis=1, concat_axis=0, tiled=True),
    )
    tok_dev, key_dim = key_rows.shape
    value_dim = value_rows.shape[1]
    block_count = tok_dev // BLOCK
    score_scaling = (key_dim * BLOCK) ** (-0.5)
    shard_total = lax.axis_size("ctx")
    doc_ids = document_ids(doc_lengths, lax.axis_index("ctx") * tok_dev, tok_dev)
    weights, per_head_decay_rate, tail_decay, block_decay = decay_tables(
        log_decay[0], doc_ids, BLOCK, score_scaling
    )
    query_block_list = query_rows.reshape(block_count, BLOCK, key_dim)
    key_blocks = key_rows.reshape(block_count, BLOCK, key_dim)
    value_block_list = value_rows.reshape(block_count, BLOCK, value_dim)
    gradient_block_list = grad_out.reshape(block_count, BLOCK, value_dim)
    zero_state = jnp.zeros((key_dim, value_dim), jnp.float32)
    keyed_blocks = (key_blocks * tail_decay[:, :, None]).astype(jnp.bfloat16)
    updates = jnp.einsum(
        "ncd,nce->nde", keyed_blocks, value_block_list, preferred_element_type=jnp.float32
    )
    local_starts = []
    running = zero_state
    factor = jnp.float32(1.0)
    block_index = 0
    local_starts.append(running)
    carry_gains = factor
    running = block_decay[block_index] * running + updates[block_index]
    factor = factor * block_decay[block_index]
    shard_decay = factor
    current = (shard_decay, running)
    for position, offset in enumerate(offset_list(shard_total)):
        pulled = passed_along((current[0], current[1]), "ctx", offset)
        current = pulled if position == 0 else chain_combine(pulled, current)
    incoming = current[1]
    states = jnp.stack([carry_gains * incoming])
    queried = (query_block_list * (per_head_decay_rate * score_scaling)[:, :, None]).astype(
        jnp.bfloat16
    )
    back_updates = jnp.einsum(
        "ncd,nce->nde", queried, gradient_block_list, preferred_element_type=jnp.float32
    )
    local_ends = [zero_state] * block_count
    back_gains = [jnp.float32(1.0)] * block_count
    running = zero_state
    factor = jnp.float32(1.0)
    for block_index in reversed(range(block_count)):
        local_ends[block_index] = running
        back_gains[block_index] = factor
        running = block_decay[block_index] * running + back_updates[block_index]
        factor = factor * block_decay[block_index]
    current = (shard_decay, running)
    for position, offset in enumerate(offset_list(shard_total)):
        pulled = passed_along((current[0], current[1]), "ctx", -offset)
        current = pulled if position == 0 else chain_combine(pulled, current)
    arriving = current[1]
    ends = jnp.stack([back_gains[0] * arriving])
    lowered_state = states.astype(jnp.bfloat16)
    back_low = ends.astype(jnp.bfloat16)
    scores = jnp.einsum(
        "nid,njd->nij", query_block_list, key_blocks, preferred_element_type=jnp.float32
    )
    attention_weights = (scores * weights).astype(jnp.bfloat16)
    retained = (
        jnp.einsum(
            "xho,xoy->xhy", query_block_list, lowered_state, preferred_element_type=jnp.float32
        )
        * (per_head_decay_rate * score_scaling)[:, :, None]
    )
    retained = retained + jnp.einsum(
        "bcv,bvd->bcd", attention_weights, value_block_list, preferred_element_type=jnp.float32
    )
    score_gradient = jnp.einsum(
        "ysb,ytb->yst", gradient_block_list, value_block_list, preferred_element_type=jnp.float32
    )
    gprobs = (score_gradient * weights).astype(jnp.bfloat16)
    query_gradient = (
        jnp.einsum(
            "srj,sqj->srq", gradient_block_list, lowered_state, preferred_element_type=jnp.float32
        )
        * (per_head_decay_rate * score_scaling)[:, :, None]
    )
    query_gradient = query_gradient + jnp.einsum(
        "nij,njd->nid", gprobs, key_blocks, preferred_element_type=jnp.float32
    )
    grad_k = (
        jnp.einsum("nje,nde->njd", value_block_list, back_low, preferred_element_type=jnp.float32)
        * tail_decay[:, :, None]
    )
    grad_k = grad_k + jnp.einsum(
        "nij,nid->njd", gprobs, query_block_list, preferred_element_type=jnp.float32
    )
    value_gradient = (
        jnp.einsum("njd,nde->nje", key_blocks, back_low, preferred_element_type=jnp.float32)
        * tail_decay[:, :, None]
    )
    value_gradient = value_gradient + jnp.einsum(
        "glu,glx->gux", attention_weights, gradient_block_list, preferred_element_type=jnp.float32
    )
    return (
        retained.reshape(tok_dev, value_dim).astype(jnp.bfloat16),
        query_gradient.reshape(tok_dev, key_dim).astype(jnp.bfloat16),
        grad_k.reshape(tok_dev, key_dim).astype(jnp.bfloat16),
        value_gradient.reshape(tok_dev, value_dim).astype(jnp.bfloat16),
    )


def solution(mesh):
    placed = (
        P(("ctx", "head"), None),
        P(("ctx", "head"), None),
        P(("ctx", "head"), None),
        P("ctx", "head"),
        P("head", "ctx"),
        P(),
    )
    return jax.shard_map(
        per_device,
        mesh=mesh,
        in_specs=placed,
        out_specs=(P("ctx", "head"), P("ctx", "head"), P("ctx", "head"), P("ctx", "head")),
        check_vma=False,
    )
```

profile of v0, /device:TPU:42, one launch (start us, length us, event | category | flops | bytes accessed | tf_op | source)
XLA Modules:
  0.0 311.3 jit_solution(16730720940128088570)
XLA Ops:
  0.6 16.9 %all-to-all-start.2 = ((bf16[8,16,256]{2,0,1:T(8,128)(2,1)}), bf16[8,16,256]{2,0,1:T(8,128)(2,1)S(1)}, u32[]{:S(2)}, u32[]{:S(2)}) async-start(bf16[8,16,256]{2,0,1:T(8,128)(2,1)} %bitcast.87), calls=%async_computation.2 | async-start | bytes 131072 | tf_op jit(solution)/shard_map/all_to_all | solution.py:50
  17.6 0.6 copy-done.2
  18.4 0.1 reduce
  18.7 0.5 slice.19
  19.2 0.6 slice.22
  19.9 0.3 reduce_window_sum.20
  20.2 0.6 slice.21
  20.8 0.7 compare_bitcast_fusion
  21.5 0.6 slice.20
  23.4 2.0 fusion.32
  25.4 7.2 %all-to-all-start = ((bf16[8,16,256]{2,0,1:T(8,128)(2,1)}), bf16[8,16,256]{2,0,1:T(8,128)(2,1)S(1)}, u32[]{:S(2)}, u32[]{:S(2)}) async-start(bf16[8,16,256]{2,0,1:T(8,128)(2,1)} %bitcast.4), calls=%async_computation | async-start | bytes 131072 | tf_op jit(solution)/shard_map/all_to_all | solution.py:51
  32.6 0.3 convolution_add_fusion
  33.0 2.2 collective-permute-start.19
  35.2 5.2 %all-to-all-done = bf16[8,16,256]{2,0,1:T(8,128)(2,1)S(1)} async-done(((bf16[8,16,256]{2,0,1:T(8,128)(2,1)}), bf16[8,16,256]{2,0,1:T(8,128)(2,1)S(1)}, u32[]{:S(2)}, u32[]{:S(2)}) %all-to-all-start) | async-done | bytes 65568 | tf_op jit(solution)/shard_map/all_to_all | solution.py:51
  40.4 11.2 %all_to_all.48 = bf16[8,16,512]{2,0,1:T(8,128)(2,1)S(1)} all-to-all(bf16[8,16,512]{2,0,1:T(8,128)(2,1)S(1)} %bitcast.86), channel_id=1, replica_groups=mesh['ctx'=64,'head'=16] {'head'}, dimensions={1} | all-to-all | bytes 262144 | tf_op jit(solution)/shard_map/all_to_all | solution.py:52
  51.6 0.3 convolution_add_fusion.1
  52.0 3.6 %collective-permute-start.6 = (f32[256,512]{1,0:T(8,128)S(1)}, f32[256,512]{1,0:T(8,128)S(1)}, u32[]{:S(2)}, u32[]{:S(2)}) collective-permute-start(f32[256,512]{1,0:T(8,128)S(1)} %convolution_add_fusion.1), channel_id=1, source_target_pairs={{0,16},{16,32},{32,48},{48,64},{64,80},{80,96},{96,112},{112,128},... | collective-permute-start | bytes 1572872 | tf_op jit(solution)/shard_map/ppermute | solution.py:12
  55.6 2.2 collective-permute-start.20
  57.8 12.0 %collective-permute-start.13 = (f32[]{:T(128)}, f32[]{:T(128)}, u32[]{:S(2)}, u32[]{:S(2)}) collective-permute-start(f32[]{:T(128)} %bitcast.3), channel_id=1, source_target_pairs={{16,0},{32,16},{48,32},{64,48},{80,64},{96,80},{112,96},{128,112},... | collective-permute-start | bytes 20 | tf_op jit(solution)/shard_map/ppermute | solution.py:12
  69.8 4.7 %collective-permute-start.7 = (f32[256,512]{1,0:T(8,128)S(1)}, f32[256,512]{1,0:T(8,128)S(1)}, u32[]{:S(2)}, u32[]{:S(2)}) collective-permute-start(f32[256,512]{1,0:T(8,128)S(1)} %collective-permute-done.6), channel_id=1, source_target_pairs={{0,16},{16,32},{32,48},{48,64},{64,80},{80,96},{96,112},{112,128},... | collective-permute-start | bytes 1572872 | tf_op jit(solution)/shard_map/ppermute | solution.py:12
  74.6 0.8 multiply_add_fusion.4
  75.4 5.1 %collective-permute-start.21 = (f32[256,512]{1,0:T(8,128)S(1)}, f32[256,512]{1,0:T(8,128)S(1)}, u32[]{:S(2)}, u32[]{:S(2)}) collective-permute-start(f32[256,512]{1,0:T(8,128)S(1)} %multiply_add_fusion.4), channel_id=1, source_target_pairs={{32,0},{48,16},{64,32},{80,48},{96,64},{112,80},{128,96},{144,112}... | collective-permute-start | bytes 1572872 | tf_op jit(solution)/shard_map/ppermute | solution.py:12
  80.5 5.4 %collective-permute-start = (f32[]{:T(128)}, f32[]{:T(128)}, u32[]{:S(2)}, u32[]{:S(2)}) collective-permute-start(f32[]{:T(128)} %bitcast.3), channel_id=1, source_target_pairs={{0,16},{16,32},{32,48},{48,64},{64,80},{80,96},{96,112},{112,128},... | collective-permute-start | bytes 20 | tf_op jit(solution)/shard_map/ppermute | solution.py:12
  85.9 3.8 %collective-permute-start.14 = (f32[]{:T(128)}, f32[]{:T(128)}, u32[]{:S(2)}, u32[]{:S(2)}) collective-permute-start(f32[]{:T(128)} %collective-permute-done.13), channel_id=1, source_target_pairs={{16,0},{32,16},{48,32},{64,48},{80,64},{96,80},{112,96},{128,112},... | collective-permute-start | bytes 20 | tf_op jit(solution)/shard_map/ppermute | solution.py:12
  89.7 13.5 %collective-permute-done.14 = f32[]{:T(128)} collective-permute-done((f32[]{:T(128)}, f32[]{:T(128)}, u32[]{:S(2)}, u32[]{:S(2)}) %collective-permute-start.14) | collective-permute-done | bytes 36 | tf_op jit(solution)/shard_map/ppermute | solution.py:12
  104.5 0.7 multiply_add_fusion.9
  105.3 4.1 %collective-permute-start.8 = (f32[256,512]{1,0:T(8,128)S(1)}, f32[256,512]{1,0:T(8,128)S(1)}, u32[]{:S(2)}, u32[]{:S(2)}) collective-permute-start(f32[256,512]{1,0:T(8,128)S(1)} %multiply_add_fusion.9), channel_id=1, source_target_pairs={{0,32},{16,48},{32,64},{48,80},{64,96},{80,112},{96,128},{112,144}... | collective-permute-start | bytes 1572872 | tf_op jit(solution)/shard_map/ppermute | solution.py:12
  109.5 4.7 %collective-permute-start.22 = (f32[256,512]{1,0:T(8,128)S(1)}, f32[256,512]{1,0:T(8,128)S(1)}, u32[]{:S(2)}, u32[]{:S(2)}) collective-permute-start(f32[256,512]{1,0:T(8,128)S(1)} %multiply_add_fusion.3), channel_id=1, source_target_pairs={{64,0},{80,16},{96,32},{112,48},{128,64},{144,80},{160,96},{176,11... | collective-permute-start | bytes 1572872 | tf_op jit(solution)/shard_map/ppermute | solution.py:12
  114.2 5.4 %collective-permute-start.1 = (f32[]{:T(128)}, f32[]{:T(128)}, u32[]{:S(2)}, u32[]{:S(2)}) collective-permute-start(f32[]{:T(128)} %collective-permute-done), channel_id=1, source_target_pairs={{0,16},{16,32},{32,48},{48,64},{64,80},{80,96},{96,112},{112,128},... | collective-permute-start | bytes 20 | tf_op jit(solution)/shard_map/ppermute | solution.py:12
  119.6 3.2 %collective-permute-start.15 = (f32[]{:T(128)}, f32[]{:T(128)}, u32[]{:S(2)}, u32[]{:S(2)}) collective-permute-start(f32[]{:T(128)} %mul.268), channel_id=1, source_target_pairs={{32,0},{48,16},{64,32},{80,48},{96,64},{112,80},{128,96},{144,112}... | collective-permute-start | bytes 20 | tf_op jit(solution)/shard_map/ppermute | solution.py:12
  122.8 32.4 %collective-permute-done.1 = f32[]{:T(128)} collective-permute-done((f32[]{:T(128)}, f32[]{:T(128)}, u32[]{:S(2)}, u32[]{:S(2)}) %collective-permute-start.1) | collective-permute-done | bytes 36 | tf_op jit(solution)/shard_map/ppermute | solution.py:12
  157.3 22.1 %collective-permute-start.9 = (f32[256,512]{1,0:T(8,128)S(1)}, f32[256,512]{1,0:T(8,128)S(1)}, u32[]{:S(2)}, u32[]{:S(2)}) collective-permute-start(f32[256,512]{1,0:T(8,128)S(1)} %multiply_add_fusion.8), channel_id=1, source_target_pairs={{0,64},{16,80},{32,96},{48,112},{64,128},{80,144},{96,160},{112,17... | collective-permute-start | bytes 1572872 | tf_op jit(solution)/shard_map/ppermute | solution.py:12
  179.4 3.6 %collective-permute-start.23 = (f32[256,512]{1,0:T(8,128)S(1)}, f32[256,512]{1,0:T(8,128)S(1)}, u32[]{:S(2)}, u32[]{:S(2)}) collective-permute-start(f32[256,512]{1,0:T(8,128)S(1)} %multiply_add_fusion.2), channel_id=1, source_target_pairs={{128,0},{144,16},{160,32},{176,48},{192,64},{208,80},{224,96},{240... | collective-permute-start | bytes 1572872 | tf_op jit(solution)/shard_map/ppermute | solution.py:12
  183.0 7.8 %collective-permute-start.2 = (f32[]{:T(128)}, f32[]{:T(128)}, u32[]{:S(2)}, u32[]{:S(2)}) collective-permute-start(f32[]{:T(128)} %mul.234), channel_id=1, source_target_pairs={{0,32},{16,48},{32,64},{48,80},{64,96},{80,112},{96,128},{112,144}... | collective-permute-start | bytes 20 | tf_op jit(solution)/shard_map/ppermute | solution.py:12
  190.8 4.5 %collective-permute-start.16 = (f32[]{:T(128)}, f32[]{:T(128)}, u32[]{:S(2)}, u32[]{:S(2)}) collective-permute-start(f32[]{:T(128)} %mul.269), channel_id=1, source_target_pairs={{64,0},{80,16},{96,32},{112,48},{128,64},{144,80},{160,96},{176,11... | collective-permute-start | bytes 20 | tf_op jit(solution)/shard_map/ppermute | solution.py:12
  195.9 7.8 %collective-permute-start.3 = (f32[]{:T(128)}, f32[]{:T(128)}, u32[]{:S(2)}, u32[]{:S(2)}) collective-permute-start(f32[]{:T(128)} %mul.235), channel_id=1, source_target_pairs={{0,64},{16,80},{32,96},{48,112},{64,128},{80,144},{96,160},{112,17... | collective-permute-start | bytes 20 | tf_op jit(solution)/shard_map/ppermute | solution.py:12
  204.4 4.8 %collective-permute-start.17 = (f32[]{:T(128)}, f32[]{:T(128)}, u32[]{:S(2)}, u32[]{:S(2)}) collective-permute-start(f32[]{:T(128)} %mul.270), channel_id=1, source_target_pairs={{128,0},{144,16},{160,32},{176,48},{192,64},{208,80},{224,96},{240... | collective-permute-start | bytes 20 | tf_op jit(solution)/shard_map/ppermute | solution.py:12
  209.8 3.6 %collective-permute-start.4 = (f32[]{:T(128)}, f32[]{:T(128)}, u32[]{:S(2)}, u32[]{:S(2)}) collective-permute-start(f32[]{:T(128)} %mul.236), channel_id=1, source_target_pairs={{0,128},{16,144},{32,160},{48,176},{64,192},{80,208},{96,224},{112... | collective-permute-start | bytes 20 | tf_op jit(solution)/shard_map/ppermute | solution.py:12
  214.0 9.5 %collective-permute-start.18 = (f32[]{:T(128)}, f32[]{:T(128)}, u32[]{:S(2)}, u32[]{:S(2)}) collective-permute-start(f32[]{:T(128)} %mul.271), channel_id=1, source_target_pairs={{256,0},{272,16},{288,32},{304,48},{320,64},{336,80},{352,96},{368... | collective-permute-start | bytes 20 | tf_op jit(solution)/shard_map/ppermute | solution.py:12
  224.3 3.2 %collective-permute-start.5 = (f32[]{:T(128)}, f32[]{:T(128)}, u32[]{:S(2)}, u32[]{:S(2)}) collective-permute-start(f32[]{:T(128)} %mul.237), channel_id=1, source_target_pairs={{0,256},{16,272},{32,288},{48,304},{64,320},{80,336},{96,352},{112... | collective-permute-start | bytes 20 | tf_op jit(solution)/shard_map/ppermute | solution.py:12
  228.0 6.4 %collective-permute-done.5 = f32[]{:T(128)} collective-permute-done((f32[]{:T(128)}, f32[]{:T(128)}, u32[]{:S(2)}, u32[]{:S(2)}) %collective-permute-start.5) | collective-permute-done | bytes 36 | tf_op jit(solution)/shard_map/ppermute | solution.py:12
  235.2 1.9 collective-permute-start.10
  237.3 7.2 %collective-permute-start.24 = (f32[256,512]{1,0:T(8,128)S(1)}, f32[256,512]{1,0:T(8,128)S(1)}, u32[]{:S(2)}, u32[]{:S(2)}) collective-permute-start(f32[256,512]{1,0:T(8,128)S(1)} %multiply_add_fusion.1), channel_id=1, source_target_pairs={{256,0},{272,16},{288,32},{304,48},{320,64},{336,80},{352,96},{368... | collective-permute-start | bytes 1572872 | tf_op jit(solution)/shard_map/ppermute | solution.py:12
  244.5 0.2 fusion.10
  244.7 0.2 fusion.11
  244.9 4.3 %collective-permute-done.10 = f32[256,512]{1,0:T(8,128)S(1)} collective-permute-done((f32[256,512]{1,0:T(8,128)S(1)}, f32[256,512]{1,0:T(8,128)S(1)}, u32[]{:S(2)}, u32[]{:S(2)}) %collective-permute-start.10) | collective-permute-done | bytes 524320 | tf_op jit(solution)/shard_map/ppermute | solution.py:12
  249.3 1.9 collective-permute-start.11
  251.2 18.2 %collective-permute-done.24 = f32[256,512]{1,0:T(8,128)S(1)} collective-permute-done((f32[256,512]{1,0:T(8,128)S(1)}, f32[256,512]{1,0:T(8,128)S(1)}, u32[]{:S(2)}, u32[]{:S(2)}) %collective-permute-start.24) | collective-permute-done | bytes 524320 | tf_op jit(solution)/shard_map/ppermute | solution.py:12
  269.6 1.3 collective-permute-start.25
  270.9 0.2 fusion.24
  271.1 0.2 fusion.21
  271.4 1.3 collective-permute-start.12
  272.7 5.2 %collective-permute-done.25 = f32[256,512]{1,0:T(8,128)S(1)} collective-permute-done((f32[256,512]{1,0:T(8,128)S(1)}, f32[256,512]{1,0:T(8,128)S(1)}, u32[]{:S(2)}, u32[]{:S(2)}) %collective-permute-start.25) | collective-permute-done | bytes 524320 | tf_op jit(solution)/shard_map/ppermute | solution.py:12
  278.0 0.3 fusion
  278.3 0.2 fusion.3
  278.5 0.8 copy.36
  279.3 0.2 fusion.9
  279.6 0.7 copy.35
  280.3 28.7 %collective-permute-done.12 = f32[256,512]{1,0:T(8,128)S(1)} collective-permute-done((f32[256,512]{1,0:T(8,128)S(1)}, f32[256,512]{1,0:T(8,128)S(1)}, u32[]{:S(2)}, u32[]{:S(2)}) %collective-permute-start.12) | collective-permute-done | bytes 524320 | tf_op jit(solution)/shard_map/ppermute | solution.py:12
  309.1 0.3 fusion.1
  309.3 0.2 fusion.2
  309.6 0.8 copy.33
  310.4 0.2 fusion.8
  310.6 0.7 copy.34
  (44 shorter events, 1.4 us)
Async XLA Ops:
  0.6 32.0 %copy-start = (bf16[128,512]{1,0:T(8,128)(2,1)S(1)}, bf16[128,512]{1,0:T(8,128)(2,1)}, u32[]{:S(2)}) copy-start(bf16[128,512]{1,0:T(8,128)(2,1)} %param.9) | copy-start | bytes 393220
  0.6 24.7 %all-to-all-start.2 = ((bf16[8,16,256]{2,0,1:T(8,128)(2,1)}), bf16[8,16,256]{2,0,1:T(8,128)(2,1)S(1)}, u32[]{:S(2)}, u32[]{:S(2)}) async-start(bf16[8,16,256]{2,0,1:T(8,128)(2,1)} %bitcast.87), calls=%async_computation.2 | async-start | bytes 131072 | tf_op jit(solution)/shard_map/all_to_all | solution.py:50
  17.6 0.7 copy-start.2
  19.2 0.7 copy-start.3
  25.4 15.0 %all-to-all-start = ((bf16[8,16,256]{2,0,1:T(8,128)(2,1)}), bf16[8,16,256]{2,0,1:T(8,128)(2,1)S(1)}, u32[]{:S(2)}, u32[]{:S(2)}) async-start(bf16[8,16,256]{2,0,1:T(8,128)(2,1)} %bitcast.4), calls=%async_computation | async-start | bytes 131072 | tf_op jit(solution)/shard_map/all_to_all | solution.py:51
  32.6 7.8 %copy-start.1 = (bf16[8,8192]{1,0:T(8,128)(2,1)S(1)}, bf16[8,8192]{1,0:T(8,128)(2,1)}, u32[]{:S(2)}) copy-start(bf16[8,8192]{1,0:T(8,128)(2,1)} %param.8) | copy-start | bytes 393220
  33.0 22.6 %collective-permute-start.19 = (f32[256,512]{1,0:T(8,128)S(1)}, f32[256,512]{1,0:T(8,128)S(1)}, u32[]{:S(2)}, u32[]{:S(2)}) collective-permute-start(f32[256,512]{1,0:T(8,128)S(1)} %convolution_add_fusion), channel_id=1, source_target_pairs={{16,0},{32,16},{48,32},{64,48},{80,64},{96,80},{112,96},{128,112},... | collective-permute-start | bytes 1572872 | tf_op jit(solution)/shard_map/ppermute | solution.py:12
  52.0 17.8 %collective-permute-start.6 = (f32[256,512]{1,0:T(8,128)S(1)}, f32[256,512]{1,0:T(8,128)S(1)}, u32[]{:S(2)}, u32[]{:S(2)}) collective-permute-start(f32[256,512]{1,0:T(8,128)S(1)} %convolution_add_fusion.1), channel_id=1, source_target_pairs={{0,16},{16,32},{32,48},{48,64},{64,80},{80,96},{96,112},{112,128},... | collective-permute-start | bytes 1572872 | tf_op jit(solution)/shard_map/ppermute | solution.py:12
  55.6 19.0 %collective-permute-start.20 = (f32[256,512]{1,0:T(8,128)S(1)}, f32[256,512]{1,0:T(8,128)S(1)}, u32[]{:S(2)}, u32[]{:S(2)}) collective-permute-start(f32[256,512]{1,0:T(8,128)S(1)} %collective-permute-done.19), channel_id=1, source_target_pairs={{16,0},{32,16},{48,32},{64,48},{80,64},{96,80},{112,96},{128,112},... | collective-permute-start | bytes 1572872 | tf_op jit(solution)/shard_map/ppermute | solution.py:12
  57.8 16.7 %collective-permute-start.13 = (f32[]{:T(128)}, f32[]{:T(128)}, u32[]{:S(2)}, u32[]{:S(2)}) collective-permute-start(f32[]{:T(128)} %bitcast.3), channel_id=1, source_target_pairs={{16,0},{32,16},{48,32},{64,48},{80,64},{96,80},{112,96},{128,112},... | collective-permute-start | bytes 20 | tf_op jit(solution)/shard_map/ppermute | solution.py:12
  69.8 34.7 %collective-permute-start.7 = (f32[256,512]{1,0:T(8,128)S(1)}, f32[256,512]{1,0:T(8,128)S(1)}, u32[]{:S(2)}, u32[]{:S(2)}) collective-permute-start(f32[256,512]{1,0:T(8,128)S(1)} %collective-permute-done.6), channel_id=1, source_target_pairs={{0,16},{16,32},{32,48},{48,64},{64,80},{80,96},{96,112},{112,128},... | collective-permute-start | bytes 1572872 | tf_op jit(solution)/shard_map/ppermute | solution.py:12
  75.4 34.0 %collective-permute-start.21 = (f32[256,512]{1,0:T(8,128)S(1)}, f32[256,512]{1,0:T(8,128)S(1)}, u32[]{:S(2)}, u32[]{:S(2)}) collective-permute-start(f32[256,512]{1,0:T(8,128)S(1)} %multiply_add_fusion.4), channel_id=1, source_target_pairs={{32,0},{48,16},{64,32},{80,48},{96,64},{112,80},{128,96},{144,112}... | collective-permute-start | bytes 1572872 | tf_op jit(solution)/shard_map/ppermute | solution.py:12
  80.5 24.0 %collective-permute-start = (f32[]{:T(128)}, f32[]{:T(128)}, u32[]{:S(2)}, u32[]{:S(2)}) collective-permute-start(f32[]{:T(128)} %bitcast.3), channel_id=1, source_target_pairs={{0,16},{16,32},{32,48},{48,64},{64,80},{80,96},{96,112},{112,128},... | collective-permute-start | bytes 20 | tf_op jit(solution)/shard_map/ppermute | solution.py:12
  85.9 17.3 %collective-permute-start.14 = (f32[]{:T(128)}, f32[]{:T(128)}, u32[]{:S(2)}, u32[]{:S(2)}) collective-permute-start(f32[]{:T(128)} %collective-permute-done.13), channel_id=1, source_target_pairs={{16,0},{32,16},{48,32},{64,48},{80,64},{96,80},{112,96},{128,112},... | collective-permute-start | bytes 20 | tf_op jit(solution)/shard_map/ppermute | solution.py:12
  105.3 51.9 %collective-permute-start.8 = (f32[256,512]{1,0:T(8,128)S(1)}, f32[256,512]{1,0:T(8,128)S(1)}, u32[]{:S(2)}, u32[]{:S(2)}) collective-permute-start(f32[256,512]{1,0:T(8,128)S(1)} %multiply_add_fusion.9), channel_id=1, source_target_pairs={{0,32},{16,48},{32,64},{48,80},{64,96},{80,112},{96,128},{112,144}... | collective-permute-start | bytes 1572872 | tf_op jit(solution)/shard_map/ppermute | solution.py:12
  109.5 69.9 %collective-permute-start.22 = (f32[256,512]{1,0:T(8,128)S(1)}, f32[256,512]{1,0:T(8,128)S(1)}, u32[]{:S(2)}, u32[]{:S(2)}) collective-permute-start(f32[256,512]{1,0:T(8,128)S(1)} %multiply_add_fusion.3), channel_id=1, source_target_pairs={{64,0},{80,16},{96,32},{112,48},{128,64},{144,80},{160,96},{176,11... | collective-permute-start | bytes 1572872 | tf_op jit(solution)/shard_map/ppermute | solution.py:12
  114.2 41.1 %collective-permute-start.1 = (f32[]{:T(128)}, f32[]{:T(128)}, u32[]{:S(2)}, u32[]{:S(2)}) collective-permute-start(f32[]{:T(128)} %collective-permute-done), channel_id=1, source_target_pairs={{0,16},{16,32},{32,48},{48,64},{64,80},{80,96},{96,112},{112,128},... | collective-permute-start | bytes 20 | tf_op jit(solution)/shard_map/ppermute | solution.py:12
  119.6 37.0 %collective-permute-start.15 = (f32[]{:T(128)}, f32[]{:T(128)}, u32[]{:S(2)}, u32[]{:S(2)}) collective-permute-start(f32[]{:T(128)} %mul.268), channel_id=1, source_target_pairs={{32,0},{48,16},{64,32},{80,48},{96,64},{112,80},{128,96},{144,112}... | collective-permute-start | bytes 20 | tf_op jit(solution)/shard_map/ppermute | solution.py:12
  157.3 77.9 %collective-permute-start.9 = (f32[256,512]{1,0:T(8,128)S(1)}, f32[256,512]{1,0:T(8,128)S(1)}, u32[]{:S(2)}, u32[]{:S(2)}) collective-permute-start(f32[256,512]{1,0:T(8,128)S(1)} %multiply_add_fusion.8), channel_id=1, source_target_pairs={{0,64},{16,80},{32,96},{48,112},{64,128},{80,144},{96,160},{112,17... | collective-permute-start | bytes 1572872 | tf_op jit(solution)/shard_map/ppermute | solution.py:12
  179.4 57.7 %collective-permute-start.23 = (f32[256,512]{1,0:T(8,128)S(1)}, f32[256,512]{1,0:T(8,128)S(1)}, u32[]{:S(2)}, u32[]{:S(2)}) collective-permute-start(f32[256,512]{1,0:T(8,128)S(1)} %multiply_add_fusion.2), channel_id=1, source_target_pairs={{128,0},{144,16},{160,32},{176,48},{192,64},{208,80},{224,96},{240... | collective-permute-start | bytes 1572872 | tf_op jit(solution)/shard_map/ppermute | solution.py:12
  183.0 12.3 %collective-permute-start.2 = (f32[]{:T(128)}, f32[]{:T(128)}, u32[]{:S(2)}, u32[]{:S(2)}) collective-permute-start(f32[]{:T(128)} %mul.234), channel_id=1, source_target_pairs={{0,32},{16,48},{32,64},{48,80},{64,96},{80,112},{96,128},{112,144}... | collective-permute-start | bytes 20 | tf_op jit(solution)/shard_map/ppermute | solution.py:12
  190.8 12.9 %collective-permute-start.16 = (f32[]{:T(128)}, f32[]{:T(128)}, u32[]{:S(2)}, u32[]{:S(2)}) collective-permute-start(f32[]{:T(128)} %mul.269), channel_id=1, source_target_pairs={{64,0},{80,16},{96,32},{112,48},{128,64},{144,80},{160,96},{176,11... | collective-permute-start | bytes 20 | tf_op jit(solution)/shard_map/ppermute | solution.py:12
  195.9 13.3 %collective-permute-start.3 = (f32[]{:T(128)}, f32[]{:T(128)}, u32[]{:S(2)}, u32[]{:S(2)}) collective-permute-start(f32[]{:T(128)} %mul.235), channel_id=1, source_target_pairs={{0,64},{16,80},{32,96},{48,112},{64,128},{80,144},{96,160},{112,17... | collective-permute-start | bytes 20 | tf_op jit(solution)/shard_map/ppermute | solution.py:12
  204.4 9.0 %collective-permute-start.17 = (f32[]{:T(128)}, f32[]{:T(128)}, u32[]{:S(2)}, u32[]{:S(2)}) collective-permute-start(f32[]{:T(128)} %mul.270), channel_id=1, source_target_pairs={{128,0},{144,16},{160,32},{176,48},{192,64},{208,80},{224,96},{240... | collective-permute-start | bytes 20 | tf_op jit(solution)/shard_map/ppermute | solution.py:12
  209.8 13.7 %collective-permute-start.4 = (f32[]{:T(128)}, f32[]{:T(128)}, u32[]{:S(2)}, u32[]{:S(2)}) collective-permute-start(f32[]{:T(128)} %mul.236), channel_id=1, source_target_pairs={{0,128},{16,144},{32,160},{48,176},{64,192},{80,208},{96,224},{112... | collective-permute-start | bytes 20 | tf_op jit(solution)/shard_map/ppermute | solution.py:12
  214.0 13.4 %collective-permute-start.18 = (f32[]{:T(128)}, f32[]{:T(128)}, u32[]{:S(2)}, u32[]{:S(2)}) collective-permute-start(f32[]{:T(128)} %mul.271), channel_id=1, source_target_pairs={{256,0},{272,16},{288,32},{304,48},{320,64},{336,80},{352,96},{368... | collective-permute-start | bytes 20 | tf_op jit(solution)/shard_map/ppermute | solution.py:12
  224.3 10.2 %collective-permute-start.5 = (f32[]{:T(128)}, f32[]{:T(128)}, u32[]{:S(2)}, u32[]{:S(2)}) collective-permute-start(f32[]{:T(128)} %mul.237), channel_id=1, source_target_pairs={{0,256},{16,272},{32,288},{48,304},{64,320},{80,336},{96,352},{112... | collective-permute-start | bytes 20 | tf_op jit(solution)/shard_map/ppermute | solution.py:12
  235.2 14.0 %collective-permute-start.10 = (f32[256,512]{1,0:T(8,128)S(1)}, f32[256,512]{1,0:T(8,128)S(1)}, u32[]{:S(2)}, u32[]{:S(2)}) collective-permute-start(f32[256,512]{1,0:T(8,128)S(1)} %multiply_add_fusion.7), channel_id=1, source_target_pairs={{0,128},{16,144},{32,160},{48,176},{64,192},{80,208},{96,224},{112... | collective-permute-start | bytes 1572872 | tf_op jit(solution)/shard_map/ppermute | solution.py:12
  237.3 32.2 %collective-permute-start.24 = (f32[256,512]{1,0:T(8,128)S(1)}, f32[256,512]{1,0:T(8,128)S(1)}, u32[]{:S(2)}, u32[]{:S(2)}) collective-permute-start(f32[256,512]{1,0:T(8,128)S(1)} %multiply_add_fusion.1), channel_id=1, source_target_pairs={{256,0},{272,16},{288,32},{304,48},{320,64},{336,80},{352,96},{368... | collective-permute-start | bytes 1572872 | tf_op jit(solution)/shard_map/ppermute | solution.py:12
  249.3 22.0 %collective-permute-start.11 = (f32[256,512]{1,0:T(8,128)S(1)}, f32[256,512]{1,0:T(8,128)S(1)}, u32[]{:S(2)}, u32[]{:S(2)}) collective-permute-start(f32[256,512]{1,0:T(8,128)S(1)} %multiply_add_fusion.6), channel_id=1, source_target_pairs={{0,256},{16,272},{32,288},{48,304},{64,320},{80,336},{96,352},{112... | collective-permute-start | bytes 1572872 | tf_op jit(solution)/shard_map/ppermute | solution.py:12
  269.6 8.4 %collective-permute-start.25 = (f32[256,512]{1,0:T(8,128)S(1)}, f32[256,512]{1,0:T(8,128)S(1)}, u32[]{:S(2)}, u32[]{:S(2)}) collective-permute-start(f32[256,512]{1,0:T(8,128)S(1)} %multiply_add_fusion), channel_id=1, source_target_pairs={{512,0},{528,16},{544,32},{560,48},{576,64},{592,80},{608,96},{624... | collective-permute-start | bytes 1572872 | tf_op jit(solution)/shard_map/ppermute | solution.py:12
  271.4 37.5 %collective-permute-start.12 = (f32[256,512]{1,0:T(8,128)S(1)}, f32[256,512]{1,0:T(8,128)S(1)}, u32[]{:S(2)}, u32[]{:S(2)}) collective-permute-start(f32[256,512]{1,0:T(8,128)S(1)} %multiply_add_fusion.5), channel_id=1, source_target_pairs={{0,512},{16,528},{32,544},{48,560},{64,576},{80,592},{96,608},{112... | collective-permute-start | bytes 1572872 | tf_op jit(solution)/shard_map/ppermute | solution.py:12
where the time goes:
time: 312 us; the launch traced here: 311 us
  starting transfers between devices  161 us (52%)
  waiting for transfers between devices  114 us (37%)
  blocking collectives  11.2 us (4%)
  between operations  10.1 us (3%)
  local copies, waits for them, and re-layouts  6.19 us (2%)
  other arithmetic  5.72 us (2%)
    ppermute x26, starting transfers between devices, passed_along(): return lax.ppermute(block, axis, route)  137 us
    ppermute x26, waiting for transfers between devices, passed_along(): return lax.ppermute(block, axis, route)  109 us
    all_to_all x1, starting transfers between devices, per_device(): lax.all_to_all(queries, 'head', split_axis=1, concat_axis=0, tiled=True)  16.9 us
    all_to_all x1, blocking collectives, per_device(): lax.all_to_all(values, 'head', split_axis=1, concat_axis=0, tiled=True)  11.2 us
    all_to_all x1, starting transfers between devices, per_device(): lax.all_to_all(keys, 'head', split_axis=1, concat_axis=0, tiled=True)  7.22 us
  transfers between devices with their start and end apart: 28, of which 8 were waited for; matrix products, arithmetic and copies ran while one was open for 4% of the time, Pallas kernels for 0%

commit v1 on v0

--- a/solution.py
+++ b/solution.py
@@ -4,6 +4,7 @@
 from jax.sharding import PartitionSpec as P
 
 BLOCK = 128
+WINDOW_BLOCKS = 16
 
 
 def passed_along(block, axis, distance):
@@ -37,74 +38,69 @@
     return (weights, per_head_decay_rate, tail_decay, block_decay)
 
 
-def chain_combine(earlier, follower):
-    return (earlier[0] * follower[0], follower[0] * earlier[1] + follower[1])
+def window_product(all_decays, me, first, size):
+    places = first + jnp.arange(size, dtype=jnp.int32)
+    inside = (places >= 0) & (places < all_decays.shape[0])
+    picked = jnp.where(inside, all_decays[jnp.clip(places, 0, all_decays.shape[0] - 1)], 1.0)
+    return jnp.prod(picked)
 
 
-def offset_list(shard_total):
-    return [1] + [1 << level for level in range((shard_total - 1).bit_length())]
+def windowed_scan(own, all_decays, me, direction):
+    current = passed_along(own, "ctx", direction)
+    offset = 1
+    while offset < WINDOW_BLOCKS:
+        pulled = passed_along(current, "ctx", direction * offset)
+        if direction > 0:
+            gain = window_product(all_decays, me, me - offset, offset)
+        else:
+            gain = window_product(all_decays, me, me + 1, offset)
+        current = gain * pulled + current
+        offset *= 2
+    return current
 
 
 def per_device(queries, keys, values, grad_out, log_decay, doc_lengths):
-    query_rows, key_rows, value_rows = (
-        lax.all_to_all(queries, "head", split_axis=1, concat_axis=0, tiled=True),
-        lax.all_to_all(keys, "head", split_axis=1, concat_axis=0, tiled=True),
-        lax.all_to_all(values, "head", split_axis=1, concat_axis=0, tiled=True),
-    )
-    tok_dev, key_dim = key_rows.shape
-    value_dim = value_rows.shape[1]
+    heads = lax.axis_size("head")
+    rows = queries.shape[0]
+    key_dim = queries.shape[1] // heads
+    value_dim = values.shape[1] // heads
+    packed = jnp.concatenate(
+        [
+            queries.reshape(rows, heads, key_dim),
+            keys.reshape(rows, heads, key_dim),
+            values.reshape(rows, heads, value_dim),
+        ],
+        axis=2,
+    ).reshape(rows, heads * (2 * key_dim + value_dim))
+    gathered = lax.all_to_all(packed, "head", split_axis=1, concat_axis=0, tiled=True)
+    query_rows = gathered[:, :key_dim]
+    key_rows = gathered[:, key_dim : 2 * key_dim]
+    value_rows = gathered[:, 2 * key_dim :]
+    tok_dev = key_rows.shape[0]
     block_count = tok_dev // BLOCK
     score_scaling = (key_dim * BLOCK) ** (-0.5)
-    shard_total = lax.axis_size("ctx")
-    doc_ids = document_ids(doc_lengths, lax.axis_index("ctx") * tok_dev, tok_dev)
+    me = lax.axis_index("ctx")
+    doc_ids = document_ids(doc_lengths, me * tok_dev, tok_dev)
     weights, per_head_decay_rate, tail_decay, block_decay = decay_tables(
         log_decay[0], doc_ids, BLOCK, score_scaling
     )
+    all_decays = lax.all_gather(block_decay[0], "ctx")
     query_block_list = query_rows.reshape(block_count, BLOCK, key_dim)
     key_blocks = key_rows.reshape(block_count, BLOCK, key_dim)
     value_block_list = value_rows.reshape(block_count, BLOCK, value_dim)
     gradient_block_list = grad_out.reshape(block_count, BLOCK, value_dim)
-    zero_state = jnp.zeros((key_dim, value_dim), jnp.float32)
     keyed_blocks = (key_blocks * tail_decay[:, :, None]).astype(jnp.bfloat16)
     updates = jnp.einsum(
         "ncd,nce->nde", keyed_blocks, value_block_list, preferred_element_type=jnp.float32
     )
-    local_starts = []
-    running = zero_state
-    factor = jnp.float32(1.0)
-    block_index = 0
-    local_starts.append(running)
-    carry_gains = factor
-    running = block_decay[block_index] * running + updates[block_index]
-    factor = factor * block_decay[block_index]
-    shard_decay = factor
-    current = (shard_decay, running)
-    for position, offset in enumerate(offset_list(shard_total)):
-        pulled = passed_along((current[0], current[1]), "ctx", offset)
-        current = pulled if position == 0 else chain_combine(pulled, current)
-    incoming = current[1]
-    states = jnp.stack([carry_gains * incoming])
     queried = (query_block_list * (per_head_decay_rate * score_scaling)[:, :, None]).astype(
         jnp.bfloat16
     )
     back_updates = jnp.einsum(
         "ncd,nce->nde", queried, gradient_block_list, preferred_element_type=jnp.float32
     )
-    local_ends = [zero_state] * block_count
-    back_gains = [jnp.float32(1.0)] * block_count
-    running = zero_state
-    factor = jnp.float32(1.0)
-    for block_index in reversed(range(block_count)):
-        local_ends[block_index] = running
-        back_gains[block_index] = factor
-        running = block_decay[block_index] * running + back_updates[block_index]
-        factor = factor * block_decay[block_index]
-    current = (shard_decay, running)
-    for position, offset in enumerate(offset_list(shard_total)):
-        pulled = passed_along((current[0], current[1]), "ctx", -offset)
-        current = pulled if position == 0 else chain_combine(pulled, current)
-    arriving = current[1]
-    ends = jnp.stack([back_gains[0] * arriving])
+    states = windowed_scan(updates[0], all_decays, me, 1)[None]
+    ends = windowed_scan(back_updates[0], all_decays, me, -1)[None]
     lowered_state = states.astype(jnp.bfloat16)
     back_low = ends.astype(jnp.bfloat16)
     scores = jnp.einsum(

time: 312 us -> 303 us (0.971)
  the two profiles are of different devices: /device:TPU:42 before, /device:TPU:210 now
where the time goes in v1:
time: 303 us; the launch traced here: 302 us
  blocking collectives  120 us (40%)
  starting transfers between devices  101 us (33%)
  waiting for transfers between devices  49.3 us (16%)
  other arithmetic  13.5 us (4%)
  local copies, waits for them, and re-layouts  10.3 us (3%)
  matrix products  4.56 us (2%)
  between operations  3.61 us (1%)
    all_gather x1, blocking collectives, per_device(): all_decays = lax.all_gather(block_decay[0], 'ctx')  120 us
    ppermute x10, starting transfers between devices, passed_along(): return lax.ppermute(block, axis, route)  85.4 us
    ppermute x10, waiting for transfers between devices, passed_along(): return lax.ppermute(block, axis, route)  49.3 us
    all_to_all x1, starting transfers between devices, per_device(): lax.all_to_all(packed, 'head', split_axis=1, concat_axis=0, tiled=True)  15.4 us
  transfers between devices with their start and end apart: 11, of which 8 were waited for; matrix products, arithmetic and copies ran while one was open for 8% of the time, Pallas kernels for 0%

profile of v1, /device:TPU:210, one launch (start us, length us, event | category | flops | bytes accessed | tf_op | source)
XLA Modules:
  0.0 302.3 jit_solution(2195433282748773694)
XLA Ops:
  0.6 1.7 pad_maximum_fusion
  2.3 15.4 %all-to-all-start = ((bf16[8,16,1024]{2,0,1:T(8,128)(2,1)}), bf16[8,16,1024]{2,0,1:T(8,128)(2,1)S(1)}, u32[]{:S(2)}, u32[]{:S(2)}) async-start(bf16[8,16,1024]{2,0,1:T(8,128)(2,1)} %pad_maximum_fusion), calls=%async_computation | async-start | bytes 524288 | tf_op jit(solution)/shard_map/all_to_all | solution.py:75
  17.8 0.6 copy-done.1
  18.6 0.1 reduce
  18.8 0.5 slice.29
  19.4 0.7 compare_bitcast_fusion
  20.2 0.6 slice.30
  20.9 0.3 reduce_window_sum.20
  21.2 0.6 slice.31
  22.5 0.6 slice.33
  23.1 1.3 dynamic-slice.8
  25.0 0.7 bitcast_dynamic-update-slice_fusion
  25.7 120.2 %all-reduce = f32[64]{0:T(128)S(1)} all-reduce(f32[64]{0:T(128)S(1)} %bitcast_dynamic-update-slice_fusion), channel_id=2, replica_groups=mesh['ctx'=64,'head'=16] {'ctx'}, use_global_device_ids=true, to_apply=%add | all-reduce | flops 64 | bytes 512 | tf_op jit(solution)/shard_map/all_gather | solution.py:87
  145.9 0.6 gather_fusion.5
  146.5 0.6 gather_fusion.4
  147.2 0.6 gather_fusion.3
  147.8 0.6 gather_fusion.2
  148.5 0.6 gather_fusion.1
  149.1 2.0 fusion.32
  151.1 0.3 fusion.18
  151.5 6.0 %collective-permute-start.5 = (f32[256,512]{1,0:T(8,128)S(1)}, f32[256,512]{1,0:T(8,128)S(1)}, u32[]{:S(2)}, u32[]{:S(2)}) collective-permute-start(f32[256,512]{1,0:T(8,128)S(1)} %fusion.18), channel_id=1, source_target_pairs={{16,0},{32,16},{48,32},{64,48},{80,64},{96,80},{112,96},{128,112},... | collective-permute-start | bytes 1572872 | tf_op jit(solution)/shard_map/ppermute | solution.py:13
  157.5 0.6 gather_fusion
  158.2 0.6 fusion.45
  160.1 0.6 fusion.39
  160.7 0.3 fusion.16
  161.0 1.9 collective-permute-start
  162.9 5.5 %collective-permute-done.5 = f32[256,512]{1,0:T(8,128)S(1)} collective-permute-done((f32[256,512]{1,0:T(8,128)S(1)}, f32[256,512]{1,0:T(8,128)S(1)}, u32[]{:S(2)}, u32[]{:S(2)}) %collective-permute-start.5) | collective-permute-done | bytes 524320 | tf_op jit(solution)/shard_map/ppermute | solution.py:13
  168.4 5.9 %collective-permute-start.6 = (f32[256,512]{1,0:T(8,128)S(1)}, f32[256,512]{1,0:T(8,128)S(1)}, u32[]{:S(2)}, u32[]{:S(2)}) collective-permute-start(f32[256,512]{1,0:T(8,128)S(1)} %collective-permute-done.5), channel_id=1, source_target_pairs={{16,0},{32,16},{48,32},{64,48},{80,64},{96,80},{112,96},{128,112},... | collective-permute-start | bytes 1572872 | tf_op jit(solution)/shard_map/ppermute | solution.py:13
  174.3 0.7 fusion.40
  175.0 0.7 fusion.41
  175.7 0.6 fusion.42
  176.3 0.6 fusion.43
  177.0 0.6 fusion.44
  177.6 5.4 %collective-permute-done = f32[256,512]{1,0:T(8,128)S(1)} collective-permute-done((f32[256,512]{1,0:T(8,128)S(1)}, f32[256,512]{1,0:T(8,128)S(1)}, u32[]{:S(2)}, u32[]{:S(2)}) %collective-permute-start) | collective-permute-done | bytes 524320 | tf_op jit(solution)/shard_map/ppermute | solution.py:13
  183.0 1.9 collective-permute-start.1
  184.9 6.6 %collective-permute-done.6 = f32[256,512]{1,0:T(8,128)S(1)} collective-permute-done((f32[256,512]{1,0:T(8,128)S(1)}, f32[256,512]{1,0:T(8,128)S(1)}, u32[]{:S(2)}, u32[]{:S(2)}) %collective-permute-start.6) | collective-permute-done | bytes 524320 | tf_op jit(solution)/shard_map/ppermute | solution.py:13
  191.6 25.2 %collective-permute-start.7 = (f32[256,512]{1,0:T(8,128)S(1)}, f32[256,512]{1,0:T(8,128)S(1)}, u32[]{:S(2)}, u32[]{:S(2)}) collective-permute-start(f32[256,512]{1,0:T(8,128)S(1)} %multiply_add_fusion.2), channel_id=1, source_target_pairs={{32,0},{48,16},{64,32},{80,48},{96,64},{112,80},{128,96},{144,112}... | collective-permute-start | bytes 1572872 | tf_op jit(solution)/shard_map/ppermute | solution.py:13
  216.8 0.2 fusion.11
  217.0 0.2 fusion.27
  217.3 1.9 collective-permute-start.2
  219.3 4.6 %collective-permute-done.7 = f32[256,512]{1,0:T(8,128)S(1)} collective-permute-done((f32[256,512]{1,0:T(8,128)S(1)}, f32[256,512]{1,0:T(8,128)S(1)}, u32[]{:S(2)}, u32[]{:S(2)}) %collective-permute-start.7) | collective-permute-done | bytes 524320 | tf_op jit(solution)/shard_map/ppermute | solution.py:13
  223.8 0.6 multiply_add_fusion.1
  224.5 21.0 %collective-permute-start.8 = (f32[256,512]{1,0:T(8,128)S(1)}, f32[256,512]{1,0:T(8,128)S(1)}, u32[]{:S(2)}, u32[]{:S(2)}) collective-permute-start(f32[256,512]{1,0:T(8,128)S(1)} %multiply_add_fusion.1), channel_id=1, source_target_pairs={{64,0},{80,16},{96,32},{112,48},{128,64},{144,80},{160,96},{176,11... | collective-permute-start | bytes 1572872 | tf_op jit(solution)/shard_map/ppermute | solution.py:13
  245.5 0.2 fusion.10
  245.7 0.2 fusion.46
  245.9 0.5 collective-permute-done.2
  246.4 0.7 multiply_add_fusion.4
  247.1 1.9 collective-permute-start.3
  249.1 7.7 %collective-permute-done.8 = f32[256,512]{1,0:T(8,128)S(1)} collective-permute-done((f32[256,512]{1,0:T(8,128)S(1)}, f32[256,512]{1,0:T(8,128)S(1)}, u32[]{:S(2)}, u32[]{:S(2)}) %collective-permute-start.8) | collective-permute-done | bytes 524320 | tf_op jit(solution)/shard_map/ppermute | solution.py:13
  256.7 0.7 multiply_add_fusion
  257.5 17.6 %collective-permute-start.9 = (f32[256,512]{1,0:T(8,128)S(1)}, f32[256,512]{1,0:T(8,128)S(1)}, u32[]{:S(2)}, u32[]{:S(2)}) collective-permute-start(f32[256,512]{1,0:T(8,128)S(1)} %multiply_add_fusion), channel_id=1, source_target_pairs={{128,0},{144,16},{160,32},{176,48},{192,64},{208,80},{224,96},{240... | collective-permute-start | bytes 1572872 | tf_op jit(solution)/shard_map/ppermute | solution.py:13
  275.1 0.2 fusion.23
  275.3 0.2 fusion.14
  275.5 0.7 multiply_add_fusion.3
  276.2 1.9 collective-permute-start.4
  278.2 3.6 %collective-permute-done.9 = f32[256,512]{1,0:T(8,128)S(1)} collective-permute-done((f32[256,512]{1,0:T(8,128)S(1)}, f32[256,512]{1,0:T(8,128)S(1)}, u32[]{:S(2)}, u32[]{:S(2)}) %collective-permute-start.9) | collective-permute-done | bytes 524320 | tf_op jit(solution)/shard_map/ppermute | solution.py:13
  281.8 0.7 add_convert_fusion
  282.5 0.9 fusion.8
  283.4 0.8 fusion.3
  284.2 15.5 %collective-permute-done.4 = f32[256,512]{1,0:T(8,128)S(1)} collective-permute-done((f32[256,512]{1,0:T(8,128)S(1)}, f32[256,512]{1,0:T(8,128)S(1)}, u32[]{:S(2)}, u32[]{:S(2)}) %collective-permute-start.4) | collective-permute-done | bytes 524320 | tf_op jit(solution)/shard_map/ppermute | solution.py:13
  299.7 0.7 add_convert_fusion.1
  300.4 0.2 fusion.7
  300.7 0.7 copy.21
  301.4 0.8 fusion.2
  (30 shorter events, 0.6 us)
Async XLA Ops:
  0.6 150.5 %copy-start = (bf16[128,512]{1,0:T(8,128)(2,1)S(1)}, bf16[128,512]{1,0:T(8,128)(2,1)}, u32[]{:S(2)}) copy-start(bf16[128,512]{1,0:T(8,128)(2,1)} %param.9) | copy-start | bytes 393220
  2.3 148.8 %all-to-all-start = ((bf16[8,16,1024]{2,0,1:T(8,128)(2,1)}), bf16[8,16,1024]{2,0,1:T(8,128)(2,1)S(1)}, u32[]{:S(2)}, u32[]{:S(2)}) async-start(bf16[8,16,1024]{2,0,1:T(8,128)(2,1)} %pad_maximum_fusion), calls=%async_computation | async-start | bytes 524288 | tf_op jit(solution)/shard_map/all_to_all | solution.py:75
  17.8 0.7 copy-start.1
  20.2 0.7 copy-start.2
  151.5 17.0 %collective-permute-start.5 = (f32[256,512]{1,0:T(8,128)S(1)}, f32[256,512]{1,0:T(8,128)S(1)}, u32[]{:S(2)}, u32[]{:S(2)}) collective-permute-start(f32[256,512]{1,0:T(8,128)S(1)} %fusion.18), channel_id=1, source_target_pairs={{16,0},{32,16},{48,32},{64,48},{80,64},{96,80},{112,96},{128,112},... | collective-permute-start | bytes 1572872 | tf_op jit(solution)/shard_map/ppermute | solution.py:13
  161.0 22.0 %collective-permute-start = (f32[256,512]{1,0:T(8,128)S(1)}, f32[256,512]{1,0:T(8,128)S(1)}, u32[]{:S(2)}, u32[]{:S(2)}) collective-permute-start(f32[256,512]{1,0:T(8,128)S(1)} %fusion.16), channel_id=1, source_target_pairs={{0,16},{16,32},{32,48},{48,64},{64,80},{80,96},{96,112},{112,128},... | collective-permute-start | bytes 1572872 | tf_op jit(solution)/shard_map/ppermute | solution.py:13
  168.4 23.1 %collective-permute-start.6 = (f32[256,512]{1,0:T(8,128)S(1)}, f32[256,512]{1,0:T(8,128)S(1)}, u32[]{:S(2)}, u32[]{:S(2)}) collective-permute-start(f32[256,512]{1,0:T(8,128)S(1)} %collective-permute-done.5), channel_id=1, source_target_pairs={{16,0},{32,16},{48,32},{64,48},{80,64},{96,80},{112,96},{128,112},... | collective-permute-start | bytes 1572872 | tf_op jit(solution)/shard_map/ppermute | solution.py:13
  183.0 34.2 %collective-permute-start.1 = (f32[256,512]{1,0:T(8,128)S(1)}, f32[256,512]{1,0:T(8,128)S(1)}, u32[]{:S(2)}, u32[]{:S(2)}) collective-permute-start(f32[256,512]{1,0:T(8,128)S(1)} %collective-permute-done), channel_id=1, source_target_pairs={{0,16},{16,32},{32,48},{48,64},{64,80},{80,96},{96,112},{112,128},... | collective-permute-start | bytes 1572872 | tf_op jit(solution)/shard_map/ppermute | solution.py:13
  191.6 32.2 %collective-permute-start.7 = (f32[256,512]{1,0:T(8,128)S(1)}, f32[256,512]{1,0:T(8,128)S(1)}, u32[]{:S(2)}, u32[]{:S(2)}) collective-permute-start(f32[256,512]{1,0:T(8,128)S(1)} %multiply_add_fusion.2), channel_id=1, source_target_pairs={{32,0},{48,16},{64,32},{80,48},{96,64},{112,80},{128,96},{144,112}... | collective-permute-start | bytes 1572872 | tf_op jit(solution)/shard_map/ppermute | solution.py:13
  217.3 29.1 %collective-permute-start.2 = (f32[256,512]{1,0:T(8,128)S(1)}, f32[256,512]{1,0:T(8,128)S(1)}, u32[]{:S(2)}, u32[]{:S(2)}) collective-permute-start(f32[256,512]{1,0:T(8,128)S(1)} %multiply_add_fusion.5), channel_id=1, source_target_pairs={{0,32},{16,48},{32,64},{48,80},{64,96},{80,112},{96,128},{112,144}... | collective-permute-start | bytes 1572872 | tf_op jit(solution)/shard_map/ppermute | solution.py:13
  224.5 32.2 %collective-permute-start.8 = (f32[256,512]{1,0:T(8,128)S(1)}, f32[256,512]{1,0:T(8,128)S(1)}, u32[]{:S(2)}, u32[]{:S(2)}) collective-permute-start(f32[256,512]{1,0:T(8,128)S(1)} %multiply_add_fusion.1), channel_id=1, source_target_pairs={{64,0},{80,16},{96,32},{112,48},{128,64},{144,80},{160,96},{176,11... | collective-permute-start | bytes 1572872 | tf_op jit(solution)/shard_map/ppermute | solution.py:13
  247.1 28.4 %collective-permute-start.3 = (f32[256,512]{1,0:T(8,128)S(1)}, f32[256,512]{1,0:T(8,128)S(1)}, u32[]{:S(2)}, u32[]{:S(2)}) collective-permute-start(f32[256,512]{1,0:T(8,128)S(1)} %multiply_add_fusion.4), channel_id=1, source_target_pairs={{0,64},{16,80},{32,96},{48,112},{64,128},{80,144},{96,160},{112,17... | collective-permute-start | bytes 1572872 | tf_op jit(solution)/shard_map/ppermute | solution.py:13
  257.5 24.3 %collective-permute-start.9 = (f32[256,512]{1,0:T(8,128)S(1)}, f32[256,512]{1,0:T(8,128)S(1)}, u32[]{:S(2)}, u32[]{:S(2)}) collective-permute-start(f32[256,512]{1,0:T(8,128)S(1)} %multiply_add_fusion), channel_id=1, source_target_pairs={{128,0},{144,16},{160,32},{176,48},{192,64},{208,80},{224,96},{240... | collective-permute-start | bytes 1572872 | tf_op jit(solution)/shard_map/ppermute | solution.py:13
  276.2 23.4 %collective-permute-start.4 = (f32[256,512]{1,0:T(8,128)S(1)}, f32[256,512]{1,0:T(8,128)S(1)}, u32[]{:S(2)}, u32[]{:S(2)}) collective-permute-start(f32[256,512]{1,0:T(8,128)S(1)} %multiply_add_fusion.3), channel_id=1, source_target_pairs={{0,128},{16,144},{32,160},{48,176},{64,192},{80,208},{96,224},{112... | collective-permute-start | bytes 1572872 | tf_op jit(solution)/shard_map/ppermute | solution.py:13

commit v2 on v1

--- a/solution.py
+++ b/solution.py
@@ -38,25 +38,19 @@
     return (weights, per_head_decay_rate, tail_decay, block_decay)
 
 
-def window_product(all_decays, me, first, size):
-    places = first + jnp.arange(size, dtype=jnp.int32)
-    inside = (places >= 0) & (places < all_decays.shape[0])
-    picked = jnp.where(inside, all_decays[jnp.clip(places, 0, all_decays.shape[0] - 1)], 1.0)
-    return jnp.prod(picked)
-
-
-def windowed_scan(own, all_decays, me, direction):
-    current = passed_along(own, "ctx", direction)
+def windowed_scan(own, own_decay, direction):
+    rows, cols = own.shape
+    gain_rows = jnp.broadcast_to(own_decay, (8, cols)).astype(own.dtype)
+    message = jnp.concatenate([own, gain_rows], axis=0)
+    keep = (lax.broadcasted_iota(jnp.int32, (rows + 8, 1), 0) < rows).astype(own.dtype)
+    current = passed_along(message, "ctx", direction)
     offset = 1
     while offset < WINDOW_BLOCKS:
         pulled = passed_along(current, "ctx", direction * offset)
-        if direction > 0:
-            gain = window_product(all_decays, me, me - offset, offset)
-        else:
-            gain = window_product(all_decays, me, me + 1, offset)
-        current = gain * pulled + current
+        gain = current[rows, 0]
+        current = gain * pulled + current * keep
         offset *= 2
-    return current
+    return current[:rows]
 
 
 def per_device(queries, keys, values, grad_out, log_decay, doc_lengths):
@@ -84,7 +78,6 @@
     weights, per_head_decay_rate, tail_decay, block_decay = decay_tables(
         log_decay[0], doc_ids, BLOCK, score_scaling
     )
-    all_decays = lax.all_gather(block_decay[0], "ctx")
     query_block_list = query_rows.reshape(block_count, BLOCK, key_dim)
     key_blocks = key_rows.reshape(block_count, BLOCK, key_dim)
     value_block_list = value_rows.reshape(block_count, BLOCK, value_dim)
@@ -99,8 +92,8 @@
     back_updates = jnp.einsum(
         "ncd,nce->nde", queried, gradient_block_list, preferred_element_type=jnp.float32
     )
-    states = windowed_scan(updates[0], all_decays, me, 1)[None]
-    ends = windowed_scan(back_updates[0], all_decays, me, -1)[None]
+    states = windowed_scan(updates[0], block_decay[0], 1)[None]
+    ends = windowed_scan(back_updates[0], block_decay[0], -1)[None]
     lowered_state = states.astype(jnp.bfloat16)
     back_low = ends.astype(jnp.bfloat16)
     scores = jnp.einsum(

time: 303 us -> 216 us (0.71)
  the two profiles are of different devices: /device:TPU:210 before, /device:TPU:40 now
where the time goes in v2:
time: 216 us
  waiting for transfers between devices  133 us (62%)
  starting transfers between devices  56.4 us (26%)
  other arithmetic  11 us (5%)
  local copies, waits for them, and re-layouts  8.77 us (4%)
  matrix products  4.55 us (2%)
  between operations  2.21 us (1%)
    ppermute x10, waiting for transfers between devices, passed_along(): return lax.ppermute(block, axis, route)  129 us
    ppermute x10, starting transfers between devices, passed_along(): return lax.ppermute(block, axis, route)  39.7 us
    all_to_all x1, starting transfers between devices, per_device(): lax.all_to_all(packed, 'head', split_axis=1, concat_axis=0, tiled=True)  16.8 us
    add x4, other arithmetic, windowed_scan(): current = gain * pulled + current * keep  4.5 us
  transfers between devices with their start and end apart: 11, of which 8 were waited for; matrix products, arithmetic and copies ran while one was open for 6% of the time, Pallas kernels for 0%

profile of v2, /device:TPU:40, one launch (start us, length us, event | category | flops | bytes accessed | tf_op | source)
XLA Modules:
  0.0 215.7 jit_solution(8779534780503455427)
XLA Ops:
  0.6 0.0 copy-start
  0.6 1.7 pad_maximum_fusion
  2.3 16.8 %all-to-all-start = ((bf16[8,16,1024]{2,0,1:T(8,128)(2,1)}), bf16[8,16,1024]{2,0,1:T(8,128)(2,1)S(1)}, u32[]{:S(2)}, u32[]{:S(2)}) async-start(bf16[8,16,1024]{2,0,1:T(8,128)(2,1)} %pad_maximum_fusion), calls=%async_computation | async-start | bytes 524288 | tf_op jit(solution)/shard_map/all_to_all | solution.py:69
  19.1 0.0 copy-start.2
  19.2 0.6 copy-done.2
  19.8 0.1 copy.18
  19.9 0.1 reduce-window.9
  19.9 0.1 reduce
  20.1 0.1 convert_reduce_fusion
  20.2 0.1 fusion.35
  20.3 0.5 slice.65
  20.8 0.6 slice.62
  21.4 0.1 copy-done.3
  21.4 0.3 reduce_window_sum.20
  21.7 0.6 slice.63
  22.3 0.7 compare_bitcast_fusion
  23.0 0.6 slice.66
  25.0 2.0 fusion.34
  27.0 3.3 %all-to-all-done = bf16[8,16,1024]{2,0,1:T(8,128)(2,1)S(1)} async-done(((bf16[8,16,1024]{2,0,1:T(8,128)(2,1)}), bf16[8,16,1024]{2,0,1:T(8,128)(2,1)S(1)}, u32[]{:S(2)}, u32[]{:S(2)}) %all-to-all-start) | async-done | bytes 262176 | tf_op jit(solution)/shard_map/all_to_all | solution.py:69
  30.3 0.3 fusion.19
  30.7 2.2 %collective-permute-start.5 = (f32[264,512]{1,0:T(8,128)S(1)}, f32[264,512]{1,0:T(8,128)S(1)}, u32[]{:S(2)}, u32[]{:S(2)}) collective-permute-start(f32[264,512]{1,0:T(8,128)S(1)} %concatenate.11), channel_id=1, source_target_pairs={{16,0},{32,16},{48,32},{64,48},{80,64},{96,80},{112,96},{128,112},... | collective-permute-start | bytes 1622024 | tf_op jit(solution)/shard_map/ppermute | solution.py:13
  32.9 0.3 fusion.17
  33.3 3.6 %collective-permute-start = (f32[264,512]{1,0:T(8,128)S(1)}, f32[264,512]{1,0:T(8,128)S(1)}, u32[]{:S(2)}, u32[]{:S(2)}) collective-permute-start(f32[264,512]{1,0:T(8,128)S(1)} %concatenate.10), channel_id=1, source_target_pairs={{0,16},{16,32},{32,48},{48,64},{64,80},{80,96},{96,112},{112,128},... | collective-permute-start | bytes 1622024 | tf_op jit(solution)/shard_map/ppermute | solution.py:13
  36.9 10.7 %collective-permute-done.5 = f32[264,512]{1,0:T(8,128)S(1)} collective-permute-done((f32[264,512]{1,0:T(8,128)S(1)}, f32[264,512]{1,0:T(8,128)S(1)}, u32[]{:S(2)}, u32[]{:S(2)}) %collective-permute-start.5) | collective-permute-done | bytes 540704 | tf_op jit(solution)/shard_map/ppermute | solution.py:13
  47.6 2.2 %collective-permute-start.6 = (f32[264,512]{1,0:T(8,128)S(1)}, f32[264,512]{1,0:T(8,128)S(1)}, u32[]{:S(2)}, u32[]{:S(2)}) collective-permute-start(f32[264,512]{1,0:T(8,128)S(1)} %collective-permute-done.5), channel_id=1, source_target_pairs={{16,0},{32,16},{48,32},{64,48},{80,64},{96,80},{112,96},{128,112},... | collective-permute-start | bytes 1622024 | tf_op jit(solution)/shard_map/ppermute | solution.py:13
  49.8 0.0 copy-start.1
  49.8 0.5 slice.87
  50.4 4.5 %collective-permute-start.1 = (f32[264,512]{1,0:T(8,128)S(1)}, f32[264,512]{1,0:T(8,128)S(1)}, u32[]{:S(2)}, u32[]{:S(2)}) collective-permute-start(f32[264,512]{1,0:T(8,128)S(1)} %collective-permute-done), channel_id=1, source_target_pairs={{0,16},{16,32},{32,48},{48,64},{64,80},{80,96},{96,112},{112,128},... | collective-permute-start | bytes 1622024 | tf_op jit(solution)/shard_map/ppermute | solution.py:13
  54.8 10.0 %collective-permute-done.6 = f32[264,512]{1,0:T(8,128)S(1)} collective-permute-done((f32[264,512]{1,0:T(8,128)S(1)}, f32[264,512]{1,0:T(8,128)S(1)}, u32[]{:S(2)}, u32[]{:S(2)}) %collective-permute-start.6) | collective-permute-done | bytes 540704 | tf_op jit(solution)/shard_map/ppermute | solution.py:13
  64.8 0.8 multiply_add_fusion.2
  65.6 5.9 %collective-permute-start.7 = (f32[264,512]{1,0:T(8,128)S(1)}, f32[264,512]{1,0:T(8,128)S(1)}, u32[]{:S(2)}, u32[]{:S(2)}) collective-permute-start(f32[264,512]{1,0:T(8,128)S(1)} %multiply_add_fusion.2), channel_id=1, source_target_pairs={{32,0},{48,16},{64,32},{80,48},{96,64},{112,80},{128,96},{144,112}... | collective-permute-start | bytes 1622024 | tf_op jit(solution)/shard_map/ppermute | solution.py:13
  71.5 0.5 slice.80
  72.0 0.5 slice.88
  72.5 21.7 %collective-permute-done.7 = f32[264,512]{1,0:T(8,128)S(1)} collective-permute-done((f32[264,512]{1,0:T(8,128)S(1)}, f32[264,512]{1,0:T(8,128)S(1)}, u32[]{:S(2)}, u32[]{:S(2)}) %collective-permute-start.7) | collective-permute-done | bytes 540704 | tf_op jit(solution)/shard_map/ppermute | solution.py:13
  94.3 1.5 multiply_add_fusion.1
  95.8 1.9 collective-permute-start.2
  97.7 11.7 %collective-permute-start.8 = (f32[264,512]{1,0:T(8,128)S(1)}, f32[264,512]{1,0:T(8,128)S(1)}, u32[]{:S(2)}, u32[]{:S(2)}) collective-permute-start(f32[264,512]{1,0:T(8,128)S(1)} %get-tuple-element.18), channel_id=1, source_target_pairs={{64,0},{80,16},{96,32},{112,48},{128,64},{144,80},{160,96},{176,11... | collective-permute-start | bytes 1622024 | tf_op jit(solution)/shard_map/ppermute | solution.py:13
  109.4 0.5 slice.81
  110.0 0.5 slice.89
  110.5 24.4 %collective-permute-done.2 = f32[264,512]{1,0:T(8,128)S(1)} collective-permute-done((f32[264,512]{1,0:T(8,128)S(1)}, f32[264,512]{1,0:T(8,128)S(1)}, u32[]{:S(2)}, u32[]{:S(2)}) %collective-permute-start.2) | collective-permute-done | bytes 540704 | tf_op jit(solution)/shard_map/ppermute | solution.py:13
  134.9 34.0 %collective-permute-done.8 = f32[264,512]{1,0:T(8,128)S(1)} collective-permute-done((f32[264,512]{1,0:T(8,128)S(1)}, f32[264,512]{1,0:T(8,128)S(1)}, u32[]{:S(2)}, u32[]{:S(2)}) %collective-permute-start.8) | collective-permute-done | bytes 540704 | tf_op jit(solution)/shard_map/ppermute | solution.py:13
  168.9 1.5 multiply_add_fusion
  170.4 1.9 collective-permute-start.3
  172.3 0.2 fusion.9
  172.5 0.5 slice.82
  173.0 3.7 %collective-permute-start.9 = (f32[264,512]{1,0:T(8,128)S(1)}, f32[264,512]{1,0:T(8,128)S(1)}, u32[]{:S(2)}, u32[]{:S(2)}) collective-permute-start(f32[264,512]{1,0:T(8,128)S(1)} %get-tuple-element.16), channel_id=1, source_target_pairs={{128,0},{144,16},{160,32},{176,48},{192,64},{208,80},{224,96},{240... | collective-permute-start | bytes 1622024 | tf_op jit(solution)/shard_map/ppermute | solution.py:13
  176.7 15.7 %collective-permute-done.3 = f32[264,512]{1,0:T(8,128)S(1)} collective-permute-done((f32[264,512]{1,0:T(8,128)S(1)}, f32[264,512]{1,0:T(8,128)S(1)}, u32[]{:S(2)}, u32[]{:S(2)}) %collective-permute-start.3) | collective-permute-done | bytes 540704 | tf_op jit(solution)/shard_map/ppermute | solution.py:13
  192.5 0.8 multiply_add_fusion.3
  193.2 1.9 collective-permute-start.4
  195.2 0.2 fusion.8
  195.3 0.2 fusion.28
  195.5 0.2 fusion.24
  195.7 0.5 slice.90
  196.3 0.5 slice.83
  196.8 12.9 %collective-permute-done.4 = f32[264,512]{1,0:T(8,128)S(1)} collective-permute-done((f32[264,512]{1,0:T(8,128)S(1)}, f32[264,512]{1,0:T(8,128)S(1)}, u32[]{:S(2)}, u32[]{:S(2)}) %collective-permute-start.4) | collective-permute-done | bytes 540704 | tf_op jit(solution)/shard_map/ppermute | solution.py:13
  209.6 0.7 slice-done
  210.3 1.5 fusion.11
  211.8 0.2 convolution_multiply_fusion
  212.0 0.9 fusion.6
  212.9 0.2 convolution_multiply_fusion.1
  213.1 0.2 fusion.5
  213.3 0.7 copy.21
  214.0 0.9 fusion.1
  214.9 0.8 fusion
  (13 shorter events, 0.1 us)
Async XLA Ops:
  0.6 29.7 %copy-start = (bf16[128,512]{1,0:T(8,128)(2,1)S(1)}, bf16[128,512]{1,0:T(8,128)(2,1)}, u32[]{:S(2)}) copy-start(bf16[128,512]{1,0:T(8,128)(2,1)} %param.9) | copy-start | bytes 393220
  2.3 27.9 %all-to-all-start = ((bf16[8,16,1024]{2,0,1:T(8,128)(2,1)}), bf16[8,16,1024]{2,0,1:T(8,128)(2,1)S(1)}, u32[]{:S(2)}, u32[]{:S(2)}) async-start(bf16[8,16,1024]{2,0,1:T(8,128)(2,1)} %pad_maximum_fusion), calls=%async_computation | async-start | bytes 524288 | tf_op jit(solution)/shard_map/all_to_all | solution.py:69
  19.1 0.7 copy-start.2
  20.8 0.7 copy-start.3
  30.7 16.9 %collective-permute-start.5 = (f32[264,512]{1,0:T(8,128)S(1)}, f32[264,512]{1,0:T(8,128)S(1)}, u32[]{:S(2)}, u32[]{:S(2)}) collective-permute-start(f32[264,512]{1,0:T(8,128)S(1)} %concatenate.11), channel_id=1, source_target_pairs={{16,0},{32,16},{48,32},{64,48},{80,64},{96,80},{112,96},{128,112},... | collective-permute-start | bytes 1622024 | tf_op jit(solution)/shard_map/ppermute | solution.py:13
  33.3 17.1 %collective-permute-start = (f32[264,512]{1,0:T(8,128)S(1)}, f32[264,512]{1,0:T(8,128)S(1)}, u32[]{:S(2)}, u32[]{:S(2)}) collective-permute-start(f32[264,512]{1,0:T(8,128)S(1)} %concatenate.10), channel_id=1, source_target_pairs={{0,16},{16,32},{32,48},{48,64},{64,80},{80,96},{96,112},{112,128},... | collective-permute-start | bytes 1622024 | tf_op jit(solution)/shard_map/ppermute | solution.py:13
  47.6 17.2 %collective-permute-start.6 = (f32[264,512]{1,0:T(8,128)S(1)}, f32[264,512]{1,0:T(8,128)S(1)}, u32[]{:S(2)}, u32[]{:S(2)}) collective-permute-start(f32[264,512]{1,0:T(8,128)S(1)} %collective-permute-done.5), channel_id=1, source_target_pairs={{16,0},{32,16},{48,32},{64,48},{80,64},{96,80},{112,96},{128,112},... | collective-permute-start | bytes 1622024 | tf_op jit(solution)/shard_map/ppermute | solution.py:13
  49.8 142.6 %copy-start.1 = (f32[264]{0:T(512)}, f32[264]{0:T(512)S(1)}, u32[]{:S(2)}) copy-start(f32[264]{0:T(512)S(1)} %fusion.33) | copy-start | bytes 3172
  50.4 22.2 %collective-permute-start.1 = (f32[264,512]{1,0:T(8,128)S(1)}, f32[264,512]{1,0:T(8,128)S(1)}, u32[]{:S(2)}, u32[]{:S(2)}) collective-permute-start(f32[264,512]{1,0:T(8,128)S(1)} %collective-permute-done), channel_id=1, source_target_pairs={{0,16},{16,32},{32,48},{48,64},{64,80},{80,96},{96,112},{112,128},... | collective-permute-start | bytes 1622024 | tf_op jit(solution)/shard_map/ppermute | solution.py:13
  65.6 28.7 %collective-permute-start.7 = (f32[264,512]{1,0:T(8,128)S(1)}, f32[264,512]{1,0:T(8,128)S(1)}, u32[]{:S(2)}, u32[]{:S(2)}) collective-permute-start(f32[264,512]{1,0:T(8,128)S(1)} %multiply_add_fusion.2), channel_id=1, source_target_pairs={{32,0},{48,16},{64,32},{80,48},{96,64},{112,80},{128,96},{144,112}... | collective-permute-start | bytes 1622024 | tf_op jit(solution)/shard_map/ppermute | solution.py:13
  95.8 39.1 %collective-permute-start.2 = (f32[264,512]{1,0:T(8,128)S(1)}, f32[264,512]{1,0:T(8,128)S(1)}, u32[]{:S(2)}, u32[]{:S(2)}) collective-permute-start(f32[264,512]{1,0:T(8,128)S(1)} %get-tuple-element.19), channel_id=1, source_target_pairs={{0,32},{16,48},{32,64},{48,80},{64,96},{80,112},{96,128},{112,144}... | collective-permute-start | bytes 1622024 | tf_op jit(solution)/shard_map/ppermute | solution.py:13
  97.7 71.2 %collective-permute-start.8 = (f32[264,512]{1,0:T(8,128)S(1)}, f32[264,512]{1,0:T(8,128)S(1)}, u32[]{:S(2)}, u32[]{:S(2)}) collective-permute-start(f32[264,512]{1,0:T(8,128)S(1)} %get-tuple-element.18), channel_id=1, source_target_pairs={{64,0},{80,16},{96,32},{112,48},{128,64},{144,80},{160,96},{176,11... | collective-permute-start | bytes 1622024 | tf_op jit(solution)/shard_map/ppermute | solution.py:13
  170.4 22.1 %collective-permute-start.3 = (f32[264,512]{1,0:T(8,128)S(1)}, f32[264,512]{1,0:T(8,128)S(1)}, u32[]{:S(2)}, u32[]{:S(2)}) collective-permute-start(f32[264,512]{1,0:T(8,128)S(1)} %get-tuple-element.17), channel_id=1, source_target_pairs={{0,64},{16,80},{32,96},{48,112},{64,128},{80,144},{96,160},{112,17... | collective-permute-start | bytes 1622024 | tf_op jit(solution)/shard_map/ppermute | solution.py:13
  173.0 23.8 %collective-permute-start.9 = (f32[264,512]{1,0:T(8,128)S(1)}, f32[264,512]{1,0:T(8,128)S(1)}, u32[]{:S(2)}, u32[]{:S(2)}) collective-permute-start(f32[264,512]{1,0:T(8,128)S(1)} %get-tuple-element.16), channel_id=1, source_target_pairs={{128,0},{144,16},{160,32},{176,48},{192,64},{208,80},{224,96},{240... | collective-permute-start | bytes 1622024 | tf_op jit(solution)/shard_map/ppermute | solution.py:13
  193.2 16.4 %collective-permute-start.4 = (f32[264,512]{1,0:T(8,128)S(1)}, f32[264,512]{1,0:T(8,128)S(1)}, u32[]{:S(2)}, u32[]{:S(2)}) collective-permute-start(f32[264,512]{1,0:T(8,128)S(1)} %multiply_add_fusion.3), channel_id=1, source_target_pairs={{0,128},{16,144},{32,160},{48,176},{64,192},{80,208},{96,224},{112... | collective-permute-start | bytes 1622024 | tf_op jit(solution)/shard_map/ppermute | solution.py:13
  209.6 0.7 slice-start

commit v3 on v2

--- a/solution.py
+++ b/solution.py
@@ -38,19 +38,38 @@
     return (weights, per_head_decay_rate, tail_decay, block_decay)
 
 
-def windowed_scan(own, own_decay, direction):
-    rows, cols = own.shape
-    gain_rows = jnp.broadcast_to(own_decay, (8, cols)).astype(own.dtype)
-    message = jnp.concatenate([own, gain_rows], axis=0)
-    keep = (lax.broadcasted_iota(jnp.int32, (rows + 8, 1), 0) < rows).astype(own.dtype)
-    current = passed_along(message, "ctx", direction)
-    offset = 1
-    while offset < WINDOW_BLOCKS:
-        pulled = passed_along(current, "ctx", direction * offset)
-        gain = current[rows, 0]
-        current = gain * pulled + current * keep
-        offset *= 2
-    return current[:rows]
+RELAY_BLOCKS = WINDOW_BLOCKS // 2
+
+
+def neighbour_decays(own_decay, direction):
+    known = passed_along(own_decay.reshape(1), "ctx", direction)
+    while known.shape[0] < RELAY_BLOCKS:
+        far = passed_along(known, "ctx", direction * known.shape[0])
+        known = jnp.concatenate([known, far])
+    return known
+
+
+def relayed_partial(bundle, decays, split, direction):
+    received = []
+    moving = bundle
+    for _ in range(RELAY_BLOCKS):
+        moving = passed_along(moving, "ctx", direction)
+        received.append(moving)
+    stacked = jnp.stack(received)
+    updates = jnp.einsum(
+        "kcd,kce->kde",
+        stacked[:, :, :split],
+        stacked[:, :, split:],
+        preferred_element_type=jnp.float32,
+    )
+    acc = updates[RELAY_BLOCKS - 1]
+    for k in range(RELAY_BLOCKS - 1, 0, -1):
+        acc = decays[k - 1] * acc + updates[k - 1]
+    gain = decays[0]
+    for k in range(1, RELAY_BLOCKS):
+        gain = gain * decays[k]
+    joined = passed_along(acc, "ctx", direction * RELAY_BLOCKS)
+    return gain * joined + acc
 
 
 def per_device(queries, keys, values, grad_out, log_decay, doc_lengths):
@@ -83,17 +102,15 @@
     value_block_list = value_rows.reshape(block_count, BLOCK, value_dim)
     gradient_block_list = grad_out.reshape(block_count, BLOCK, value_dim)
     keyed_blocks = (key_blocks * tail_decay[:, :, None]).astype(jnp.bfloat16)
-    updates = jnp.einsum(
-        "ncd,nce->nde", keyed_blocks, value_block_list, preferred_element_type=jnp.float32
-    )
     queried = (query_block_list * (per_head_decay_rate * score_scaling)[:, :, None]).astype(
         jnp.bfloat16
     )
-    back_updates = jnp.einsum(
-        "ncd,nce->nde", queried, gradient_block_list, preferred_element_type=jnp.float32
-    )
-    states = windowed_scan(updates[0], block_decay[0], 1)[None]
-    ends = windowed_scan(back_updates[0], block_decay[0], -1)[None]
+    earlier_decays = neighbour_decays(block_decay[0], 1)
+    later_decays = neighbour_decays(block_decay[0], -1)
+    forward_bundle = jnp.concatenate([keyed_blocks[0], value_block_list[0]], axis=1)
+    backward_bundle = jnp.concatenate([queried[0], gradient_block_list[0]], axis=1)
+    states = relayed_partial(forward_bundle, earlier_decays, key_dim, 1)[None]
+    ends = relayed_partial(backward_bundle, later_decays, key_dim, -1)[None]
     lowered_state = states.astype(jnp.bfloat16)
     back_low = ends.astype(jnp.bfloat16)
     scores = jnp.einsum(

time: 216 us -> 215 us (level)
  the two profiles are of different devices: /device:TPU:40 before, /device:TPU:120 now
where the time goes in v3:
time: 215 us; the launch traced here: 213 us
  starting transfers between devices  140 us (65%)
  other arithmetic  30.9 us (14%)
  waiting for transfers between devices  18.1 us (8%)
  between operations  12.5 us (6%)
  local copies, waits for them, and re-layouts  6.51 us (3%)
  matrix products  5.41 us (3%)
    ppermute x26, starting transfers between devices, passed_along(): return lax.ppermute(block, axis, route)  123 us
    ppermute x26, waiting for transfers between devices, passed_along(): return lax.ppermute(block, axis, route)  18.1 us
    all_to_all x1, starting transfers between devices, per_device(): lax.all_to_all(packed, 'head', split_axis=1, concat_axis=0, tiled=True)  16.8 us
    add x2, other arithmetic, relayed_partial(): acc = decays[k - 1] * acc + updates[k - 1]  9.65 us
    concatenate x4, other arithmetic, neighbour_decays(): known = jnp.concatenate([known, far])  5.05 us
    convert_element_type x1, other arithmetic, per_device(): lowered_state = states.astype(jnp.bfloat16)  5.04 us
    convert_element_type x1, other arithmetic, per_device(): back_low = ends.astype(jnp.bfloat16)  4.78 us
  transfers between devices with their start and end apart: 27, of which 11 were waited for; matrix products, arithmetic and copies ran while one was open for 14% of the time, Pallas kernels for 0%

profile of v3, /device:TPU:120, one launch (start us, length us, event | category | flops | bytes accessed | tf_op | source)
XLA Modules:
  0.0 213.3 jit_solution(2374620680692185085)
XLA Ops:
  0.6 0.8 copy.22
  1.6 0.7 sub.35
  2.4 0.5 slice.135
  2.9 1.0 reduce_window_sum.20
  3.8 0.6 slice.137
  4.4 0.7 compare_bitcast_fusion
  5.1 0.6 slice.136
  7.1 4.4 %collective-permute-start.13 = (f32[1]{0:T(128)}, f32[1]{0:T(128)}, u32[]{:S(2)}, u32[]{:S(2)}) collective-permute-start(f32[1]{0:T(128)} %bitcast.8), channel_id=1, source_target_pairs={{16,0},{32,16},{48,32},{64,48},{80,64},{96,80},{112,96},{128,112},... | collective-permute-start | bytes 20 | tf_op jit(solution)/shard_map/ppermute | solution.py:13
  11.5 6.1 %collective-permute-start = (f32[1]{0:T(128)}, f32[1]{0:T(128)}, u32[]{:S(2)}, u32[]{:S(2)}) collective-permute-start(f32[1]{0:T(128)} %bitcast.8), channel_id=1, source_target_pairs={{0,16},{16,32},{32,48},{48,64},{64,80},{80,96},{96,112},{112,128},... | collective-permute-start | bytes 20 | tf_op jit(solution)/shard_map/ppermute | solution.py:13
  17.6 1.7 pad_maximum_fusion
  19.2 16.8 %all-to-all-start = ((bf16[8,16,1024]{2,0,1:T(8,128)(2,1)}), bf16[8,16,1024]{2,0,1:T(8,128)(2,1)S(1)}, u32[]{:S(2)}, u32[]{:S(2)}) async-start(bf16[8,16,1024]{2,0,1:T(8,128)(2,1)} %pad_maximum_fusion), calls=%async_computation | async-start | bytes 524288 | tf_op jit(solution)/shard_map/all_to_all | solution.py:88
  36.1 0.6 slice.145
  36.7 2.0 fusion.41
  38.7 1.9 collective-permute-start.14
  40.6 6.0 %collective-permute-start.1 = (f32[1]{0:T(128)}, f32[1]{0:T(128)}, u32[]{:S(2)}, u32[]{:S(2)}) collective-permute-start(f32[1]{0:T(128)} %collective-permute-done), channel_id=1, source_target_pairs={{0,16},{16,32},{32,48},{48,64},{64,80},{80,96},{96,112},{112,128},... | collective-permute-start | bytes 20 | tf_op jit(solution)/shard_map/ppermute | solution.py:13
  46.7 1.2 pad_maximum_fusion.5
  47.9 1.9 collective-permute-start.15
  49.8 1.3 pad_maximum_fusion.3
  51.1 6.9 %collective-permute-start.2 = (f32[2]{0:T(128)S(1)}, f32[2]{0:T(128)S(1)}, u32[]{:S(2)}, u32[]{:S(2)}) collective-permute-start(f32[2]{0:T(128)S(1)} %pad_maximum_fusion.3), channel_id=1, source_target_pairs={{0,32},{16,48},{32,64},{48,80},{64,96},{80,112},{96,128},{112,144}... | collective-permute-start | bytes 32 | tf_op jit(solution)/shard_map/ppermute | solution.py:13
  60.4 1.2 pad_maximum_fusion.6
  61.6 1.9 collective-permute-start.16
  63.6 1.3 pad_maximum_fusion.4
  64.9 8.7 %collective-permute-start.3 = (f32[4]{0:T(128)S(1)}, f32[4]{0:T(128)S(1)}, u32[]{:S(2)}, u32[]{:S(2)}) collective-permute-start(f32[4]{0:T(128)S(1)} %pad_maximum_fusion.4), channel_id=1, source_target_pairs={{0,64},{16,80},{32,96},{48,112},{64,128},{80,144},{96,160},{112,17... | collective-permute-start | bytes 56 | tf_op jit(solution)/shard_map/ppermute | solution.py:13
  73.6 0.6 fusion.47
  75.5 0.6 fusion.49
  77.4 0.6 fusion.46
  80.5 0.6 fusion.48
  84.6 1.9 collective-permute-start.17
  86.7 6.0 %collective-permute-start.4 = (bf16[128,768]{1,0:T(8,128)(2,1)S(1)}, bf16[128,768]{1,0:T(8,128)(2,1)S(1)}, u32[]{:S(2)}, u32[]{:S(2)}) collective-permute-start(bf16[128,768]{1,0:T(8,128)(2,1)S(1)} %pad_maximum_fusion.1), channel_id=1, source_target_pairs={{0,16},{16,32},{32,48},{48,64},{64,80},{80,96},{96,112},{112,128},... | collective-permute-start | bytes 589832 | tf_op jit(solution)/shard_map/ppermute | solution.py:13
  93.0 1.3 collective-permute-done.17
  94.3 1.9 collective-permute-start.18
  96.2 6.2 %collective-permute-start.5 = (bf16[128,768]{1,0:T(8,128)(2,1)S(1)}, bf16[128,768]{1,0:T(8,128)(2,1)S(1)}, u32[]{:S(2)}, u32[]{:S(2)}) collective-permute-start(bf16[128,768]{1,0:T(8,128)(2,1)S(1)} %collective-permute-done.4), channel_id=1, source_target_pairs={{0,16},{16,32},{32,48},{48,64},{64,80},{80,96},{96,112},{112,128},... | collective-permute-start | bytes 589832 | tf_op jit(solution)/shard_map/ppermute | solution.py:13
  102.5 1.5 collective-permute-done.18
  103.9 1.9 collective-permute-start.19
  105.9 6.2 %collective-permute-start.6 = (bf16[128,768]{1,0:T(8,128)(2,1)S(1)}, bf16[128,768]{1,0:T(8,128)(2,1)S(1)}, u32[]{:S(2)}, u32[]{:S(2)}) collective-permute-start(bf16[128,768]{1,0:T(8,128)(2,1)S(1)} %collective-permute-done.5), channel_id=1, source_target_pairs={{0,16},{16,32},{32,48},{48,64},{64,80},{80,96},{96,112},{112,128},... | collective-permute-start | bytes 589832 | tf_op jit(solution)/shard_map/ppermute | solution.py:13
  112.1 1.5 collective-permute-done.19
  113.6 1.9 collective-permute-start.20
  115.5 6.2 %collective-permute-start.7 = (bf16[128,768]{1,0:T(8,128)(2,1)S(1)}, bf16[128,768]{1,0:T(8,128)(2,1)S(1)}, u32[]{:S(2)}, u32[]{:S(2)}) collective-permute-start(bf16[128,768]{1,0:T(8,128)(2,1)S(1)} %collective-permute-done.6), channel_id=1, source_target_pairs={{0,16},{16,32},{32,48},{48,64},{64,80},{80,96},{96,112},{112,128},... | collective-permute-start | bytes 589832 | tf_op jit(solution)/shard_map/ppermute | solution.py:13
  121.8 1.5 collective-permute-done.20
  123.2 1.9 collective-permute-start.21
  125.2 6.2 %collective-permute-start.8 = (bf16[128,768]{1,0:T(8,128)(2,1)S(1)}, bf16[128,768]{1,0:T(8,128)(2,1)S(1)}, u32[]{:S(2)}, u32[]{:S(2)}) collective-permute-start(bf16[128,768]{1,0:T(8,128)(2,1)S(1)} %collective-permute-done.7), channel_id=1, source_target_pairs={{0,16},{16,32},{32,48},{48,64},{64,80},{80,96},{96,112},{112,128},... | collective-permute-start | bytes 589832 | tf_op jit(solution)/shard_map/ppermute | solution.py:13
  131.4 1.9 collective-permute-done.21
  133.3 1.9 collective-permute-start.22
  135.3 6.5 %collective-permute-start.9 = (bf16[128,768]{1,0:T(8,128)(2,1)S(1)}, bf16[128,768]{1,0:T(8,128)(2,1)S(1)}, u32[]{:S(2)}, u32[]{:S(2)}) collective-permute-start(bf16[128,768]{1,0:T(8,128)(2,1)S(1)} %collective-permute-done.8), channel_id=1, source_target_pairs={{0,16},{16,32},{32,48},{48,64},{64,80},{80,96},{96,112},{112,128},... | collective-permute-start | bytes 589832 | tf_op jit(solution)/shard_map/ppermute | solution.py:13
  141.8 2.8 %collective-permute-done.22 = bf16[128,768]{1,0:T(8,128)(2,1)S(1)} collective-permute-done((bf16[128,768]{1,0:T(8,128)(2,1)S(1)}, bf16[128,768]{1,0:T(8,128)(2,1)S(1)}, u32[]{:S(2)}, u32[]{:S(2)}) %collective-permute-start.22) | collective-permute-done | bytes 196640 | tf_op jit(solution)/shard_map/ppermute | solution.py:13
  144.6 1.9 collective-permute-start.23
  146.8 6.5 %collective-permute-start.10 = (bf16[128,768]{1,0:T(8,128)(2,1)S(1)}, bf16[128,768]{1,0:T(8,128)(2,1)S(1)}, u32[]{:S(2)}, u32[]{:S(2)}) collective-permute-start(bf16[128,768]{1,0:T(8,128)(2,1)S(1)} %collective-permute-done.9), channel_id=1, source_target_pairs={{0,16},{16,32},{32,48},{48,64},{64,80},{80,96},{96,112},{112,128},... | collective-permute-start | bytes 589832 | tf_op jit(solution)/shard_map/ppermute | solution.py:13
  153.3 2.4 %collective-permute-done.23 = bf16[128,768]{1,0:T(8,128)(2,1)S(1)} collective-permute-done((bf16[128,768]{1,0:T(8,128)(2,1)S(1)}, bf16[128,768]{1,0:T(8,128)(2,1)S(1)}, u32[]{:S(2)}, u32[]{:S(2)}) %collective-permute-start.23) | collective-permute-done | bytes 196640 | tf_op jit(solution)/shard_map/ppermute | solution.py:13
  155.7 1.9 collective-permute-start.24
  157.7 6.5 %collective-permute-start.11 = (bf16[128,768]{1,0:T(8,128)(2,1)S(1)}, bf16[128,768]{1,0:T(8,128)(2,1)S(1)}, u32[]{:S(2)}, u32[]{:S(2)}) collective-permute-start(bf16[128,768]{1,0:T(8,128)(2,1)S(1)} %collective-permute-done.10), channel_id=1, source_target_pairs={{0,16},{16,32},{32,48},{48,64},{64,80},{80,96},{96,112},{112,128},... | collective-permute-start | bytes 589832 | tf_op jit(solution)/shard_map/ppermute | solution.py:13
  164.2 1.1 collective-permute-done.24
  165.4 0.7 fusion.12
  166.2 4.7 %fusion.16 = f32[256,512]{1,0:T(8,128)S(1)} fusion(f32[8,256,512]{2,1,0:T(8,128)S(1)} %fusion.12, f32[]{:T(128)} %bitcast.33, f32[]{:T(128)} %bitcast.34, f32[]{:T(128)} %bitcast.35, f32[]{:T(128)} %bitcast.36, f32[]{:T(128)} %bitcast.37, f32[]{:T(128)} %bitcast.39, f32[]{:T(128)} %bitcast.38), kind=kLoop, calls=%fused_computation.23 | loop fusion | flops 1835008 | bytes 4718620 | tf_op jit(solution)/shard_map/add | solution.py:67
  170.9 17.5 %collective-permute-start.25 = (f32[256,512]{1,0:T(8,128)S(1)}, f32[256,512]{1,0:T(8,128)S(1)}, u32[]{:S(2)}, u32[]{:S(2)}) collective-permute-start(f32[256,512]{1,0:T(8,128)S(1)} %fusion.16), channel_id=1, source_target_pairs={{128,0},{144,16},{160,32},{176,48},{192,64},{208,80},{224,96},{240... | collective-permute-start | bytes 1572872 | tf_op jit(solution)/shard_map/ppermute | solution.py:13
  188.4 0.7 fusion.14
  189.1 5.0 %fusion.24 = f32[256,512]{1,0:T(8,128)S(1)} fusion(f32[8,256,512]{2,1,0:T(8,128)S(1)} %fusion.14, f32[]{:T(128)} %bitcast.9, f32[]{:T(128)} %bitcast.10, f32[]{:T(128)} %bitcast.11, f32[]{:T(128)} %bitcast.12, f32[]{:T(128)} %bitcast.13, f32[]{:T(128)} %bitcast.15, f32[]{:T(128)} %bitcast.14), kind=kLoop, calls=%fused_computation.39 | loop fusion | flops 1835008 | bytes 4718620 | tf_op jit(solution)/shard_map/add | solution.py:67
  194.1 1.9 collective-permute-start.12
  196.0 4.8 %add_convert_fusion = bf16[256,512]{1,0:T(8,128)(2,1)S(1)} fusion(f32[256,512]{1,0:T(8,128)S(1)} %collective-permute-done.25, f32[]{:T(128)S(6)} %mul.279, f32[8,256,512]{2,1,0:T(8,128)S(1)} %fusion.12, f32[]{:T(128)} %bitcast.39, f32[]{:T(128)} %bitcast.38, f32[]{:T(128)} %bitcast.37, f32[]{:T(128)} %bitcast.36, f32[]{:T(128)} %bitcast.35, f32[]{:T(128)} %bitcast.34, ...), kind=kLoop, calls=%fused_computation.54 | loop fusion | flops 2228224 | bytes 4980768 | tf_op jit(solution)/shard_map/convert_element_type | solution.py:115
  200.8 0.9 fusion.8
  201.7 0.8 fusion.3
  202.5 3.9 %collective-permute-done.12 = f32[256,512]{1,0:T(8,128)S(1)} collective-permute-done((f32[256,512]{1,0:T(8,128)S(1)}, f32[256,512]{1,0:T(8,128)S(1)}, u32[]{:S(2)}, u32[]{:S(2)}) %collective-permute-start.12) | collective-permute-done | bytes 524320 | tf_op jit(solution)/shard_map/ppermute | solution.py:13
  206.4 5.0 %add_convert_fusion.1 = bf16[256,512]{1,0:T(8,128)(2,1)S(1)} fusion(f32[256,512]{1,0:T(8,128)S(1)} %collective-permute-done.12, f32[]{:T(128)S(6)} %mul.242, f32[8,256,512]{2,1,0:T(8,128)S(1)} %fusion.14, f32[]{:T(128)} %bitcast.15, f32[]{:T(128)} %bitcast.14, f32[]{:T(128)} %bitcast.13, f32[]{:T(128)} %bitcast.12, f32[]{:T(128)} %bitcast.11, f32[]{:T(128)} %bitcast.10, ...), kind=kLoop, calls=%fused_computation.55 | loop fusion | flops 2228224 | bytes 4980768 | tf_op jit(solution)/shard_map/convert_element_type | solution.py:114
  211.7 0.7 copy.27
  212.4 0.8 fusion.2
  (53 shorter events, 2.5 us)
Async XLA Ops:
  0.6 83.2 %copy-start = (bf16[128,512]{1,0:T(8,128)(2,1)S(1)}, bf16[128,512]{1,0:T(8,128)(2,1)}, u32[]{:S(2)}) copy-start(bf16[128,512]{1,0:T(8,128)(2,1)} %param.9) | copy-start | bytes 393220
  7.1 31.6 %collective-permute-start.13 = (f32[1]{0:T(128)}, f32[1]{0:T(128)}, u32[]{:S(2)}, u32[]{:S(2)}) collective-permute-start(f32[1]{0:T(128)} %bitcast.8), channel_id=1, source_target_pairs={{16,0},{32,16},{48,32},{64,48},{80,64},{96,80},{112,96},{128,112},... | collective-permute-start | bytes 20 | tf_op jit(solution)/shard_map/ppermute | solution.py:13
  11.5 29.1 %collective-permute-start = (f32[1]{0:T(128)}, f32[1]{0:T(128)}, u32[]{:S(2)}, u32[]{:S(2)}) collective-permute-start(f32[1]{0:T(128)} %bitcast.8), channel_id=1, source_target_pairs={{0,16},{16,32},{32,48},{48,64},{64,80},{80,96},{96,112},{112,128},... | collective-permute-start | bytes 20 | tf_op jit(solution)/shard_map/ppermute | solution.py:13
  19.2 64.4 %all-to-all-start = ((bf16[8,16,1024]{2,0,1:T(8,128)(2,1)}), bf16[8,16,1024]{2,0,1:T(8,128)(2,1)S(1)}, u32[]{:S(2)}, u32[]{:S(2)}) async-start(bf16[8,16,1024]{2,0,1:T(8,128)(2,1)} %pad_maximum_fusion), calls=%async_computation | async-start | bytes 524288 | tf_op jit(solution)/shard_map/all_to_all | solution.py:88
  38.7 8.0 %collective-permute-start.14 = (f32[1]{0:T(128)}, f32[1]{0:T(128)}, u32[]{:S(2)}, u32[]{:S(2)}) collective-permute-start(f32[1]{0:T(128)} %collective-permute-done.13), channel_id=1, source_target_pairs={{16,0},{32,16},{48,32},{64,48},{80,64},{96,80},{112,96},{128,112},... | collective-permute-start | bytes 20 | tf_op jit(solution)/shard_map/ppermute | solution.py:13
  40.6 9.2 %collective-permute-start.1 = (f32[1]{0:T(128)}, f32[1]{0:T(128)}, u32[]{:S(2)}, u32[]{:S(2)}) collective-permute-start(f32[1]{0:T(128)} %collective-permute-done), channel_id=1, source_target_pairs={{0,16},{16,32},{32,48},{48,64},{64,80},{80,96},{96,112},{112,128},... | collective-permute-start | bytes 20 | tf_op jit(solution)/shard_map/ppermute | solution.py:13
  47.9 12.6 %collective-permute-start.15 = (f32[2]{0:T(128)S(1)}, f32[2]{0:T(128)S(1)}, u32[]{:S(2)}, u32[]{:S(2)}) collective-permute-start(f32[2]{0:T(128)S(1)} %pad_maximum_fusion.5), channel_id=1, source_target_pairs={{32,0},{48,16},{64,32},{80,48},{96,64},{112,80},{128,96},{144,112}... | collective-permute-start | bytes 32 | tf_op jit(solution)/shard_map/ppermute | solution.py:13
  51.1 12.4 %collective-permute-start.2 = (f32[2]{0:T(128)S(1)}, f32[2]{0:T(128)S(1)}, u32[]{:S(2)}, u32[]{:S(2)}) collective-permute-start(f32[2]{0:T(128)S(1)} %pad_maximum_fusion.3), channel_id=1, source_target_pairs={{0,32},{16,48},{32,64},{48,80},{64,96},{80,112},{96,128},{112,144}... | collective-permute-start | bytes 32 | tf_op jit(solution)/shard_map/ppermute | solution.py:13
  61.6 15.7 %collective-permute-start.16 = (f32[4]{0:T(128)S(1)}, f32[4]{0:T(128)S(1)}, u32[]{:S(2)}, u32[]{:S(2)}) collective-permute-start(f32[4]{0:T(128)S(1)} %pad_maximum_fusion.6), channel_id=1, source_target_pairs={{64,0},{80,16},{96,32},{112,48},{128,64},{144,80},{160,96},{176,11... | collective-permute-start | bytes 56 | tf_op jit(solution)/shard_map/ppermute | solution.py:13
  64.9 15.6 %collective-permute-start.3 = (f32[4]{0:T(128)S(1)}, f32[4]{0:T(128)S(1)}, u32[]{:S(2)}, u32[]{:S(2)}) collective-permute-start(f32[4]{0:T(128)S(1)} %pad_maximum_fusion.4), channel_id=1, source_target_pairs={{0,64},{16,80},{32,96},{48,112},{64,128},{80,144},{96,160},{112,17... | collective-permute-start | bytes 56 | tf_op jit(solution)/shard_map/ppermute | solution.py:13
  84.6 9.7 %collective-permute-start.17 = (bf16[128,768]{1,0:T(8,128)(2,1)S(1)}, bf16[128,768]{1,0:T(8,128)(2,1)S(1)}, u32[]{:S(2)}, u32[]{:S(2)}) collective-permute-start(bf16[128,768]{1,0:T(8,128)(2,1)S(1)} %pad_maximum_fusion.2), channel_id=1, source_target_pairs={{16,0},{32,16},{48,32},{64,48},{80,64},{96,80},{112,96},{128,112},... | collective-permute-start | bytes 589832 | tf_op jit(solution)/shard_map/ppermute | solution.py:13
  86.7 9.5 %collective-permute-start.4 = (bf16[128,768]{1,0:T(8,128)(2,1)S(1)}, bf16[128,768]{1,0:T(8,128)(2,1)S(1)}, u32[]{:S(2)}, u32[]{:S(2)}) collective-permute-start(bf16[128,768]{1,0:T(8,128)(2,1)S(1)} %pad_maximum_fusion.1), channel_id=1, source_target_pairs={{0,16},{16,32},{32,48},{48,64},{64,80},{80,96},{96,112},{112,128},... | collective-permute-start | bytes 589832 | tf_op jit(solution)/shard_map/ppermute | solution.py:13
  94.3 9.7 %collective-permute-start.18 = (bf16[128,768]{1,0:T(8,128)(2,1)S(1)}, bf16[128,768]{1,0:T(8,128)(2,1)S(1)}, u32[]{:S(2)}, u32[]{:S(2)}) collective-permute-start(bf16[128,768]{1,0:T(8,128)(2,1)S(1)} %collective-permute-done.17), channel_id=1, source_target_pairs={{16,0},{32,16},{48,32},{64,48},{80,64},{96,80},{112,96},{128,112},... | collective-permute-start | bytes 589832 | tf_op jit(solution)/shard_map/ppermute | solution.py:13
  96.2 9.7 %collective-permute-start.5 = (bf16[128,768]{1,0:T(8,128)(2,1)S(1)}, bf16[128,768]{1,0:T(8,128)(2,1)S(1)}, u32[]{:S(2)}, u32[]{:S(2)}) collective-permute-start(bf16[128,768]{1,0:T(8,128)(2,1)S(1)} %collective-permute-done.4), channel_id=1, source_target_pairs={{0,16},{16,32},{32,48},{48,64},{64,80},{80,96},{96,112},{112,128},... | collective-permute-start | bytes 589832 | tf_op jit(solution)/shard_map/ppermute | solution.py:13
  103.9 9.7 %collective-permute-start.19 = (bf16[128,768]{1,0:T(8,128)(2,1)S(1)}, bf16[128,768]{1,0:T(8,128)(2,1)S(1)}, u32[]{:S(2)}, u32[]{:S(2)}) collective-permute-start(bf16[128,768]{1,0:T(8,128)(2,1)S(1)} %collective-permute-done.18), channel_id=1, source_target_pairs={{16,0},{32,16},{48,32},{64,48},{80,64},{96,80},{112,96},{128,112},... | collective-permute-start | bytes 589832 | tf_op jit(solution)/shard_map/ppermute | solution.py:13
  105.9 9.7 %collective-permute-start.6 = (bf16[128,768]{1,0:T(8,128)(2,1)S(1)}, bf16[128,768]{1,0:T(8,128)(2,1)S(1)}, u32[]{:S(2)}, u32[]{:S(2)}) collective-permute-start(bf16[128,768]{1,0:T(8,128)(2,1)S(1)} %collective-permute-done.5), channel_id=1, source_target_pairs={{0,16},{16,32},{32,48},{48,64},{64,80},{80,96},{96,112},{112,128},... | collective-permute-start | bytes 589832 | tf_op jit(solution)/shard_map/ppermute | solution.py:13
  113.6 9.7 %collective-permute-start.20 = (bf16[128,768]{1,0:T(8,128)(2,1)S(1)}, bf16[128,768]{1,0:T(8,128)(2,1)S(1)}, u32[]{:S(2)}, u32[]{:S(2)}) collective-permute-start(bf16[128,768]{1,0:T(8,128)(2,1)S(1)} %collective-permute-done.19), channel_id=1, source_target_pairs={{16,0},{32,16},{48,32},{64,48},{80,64},{96,80},{112,96},{128,112},... | collective-permute-start | bytes 589832 | tf_op jit(solution)/shard_map/ppermute | solution.py:13
  115.5 9.7 %collective-permute-start.7 = (bf16[128,768]{1,0:T(8,128)(2,1)S(1)}, bf16[128,768]{1,0:T(8,128)(2,1)S(1)}, u32[]{:S(2)}, u32[]{:S(2)}) collective-permute-start(bf16[128,768]{1,0:T(8,128)(2,1)S(1)} %collective-permute-done.6), channel_id=1, source_target_pairs={{0,16},{16,32},{32,48},{48,64},{64,80},{80,96},{96,112},{112,128},... | collective-permute-start | bytes 589832 | tf_op jit(solution)/shard_map/ppermute | solution.py:13
  123.2 10.1 %collective-permute-start.21 = (bf16[128,768]{1,0:T(8,128)(2,1)S(1)}, bf16[128,768]{1,0:T(8,128)(2,1)S(1)}, u32[]{:S(2)}, u32[]{:S(2)}) collective-permute-start(bf16[128,768]{1,0:T(8,128)(2,1)S(1)} %collective-permute-done.20), channel_id=1, source_target_pairs={{16,0},{32,16},{48,32},{64,48},{80,64},{96,80},{112,96},{128,112},... | collective-permute-start | bytes 589832 | tf_op jit(solution)/shard_map/ppermute | solution.py:13
  125.2 10.1 %collective-permute-start.8 = (bf16[128,768]{1,0:T(8,128)(2,1)S(1)}, bf16[128,768]{1,0:T(8,128)(2,1)S(1)}, u32[]{:S(2)}, u32[]{:S(2)}) collective-permute-start(bf16[128,768]{1,0:T(8,128)(2,1)S(1)} %collective-permute-done.7), channel_id=1, source_target_pairs={{0,16},{16,32},{32,48},{48,64},{64,80},{80,96},{96,112},{112,128},... | collective-permute-start | bytes 589832 | tf_op jit(solution)/shard_map/ppermute | solution.py:13
  133.3 11.2 %collective-permute-start.22 = (bf16[128,768]{1,0:T(8,128)(2,1)S(1)}, bf16[128,768]{1,0:T(8,128)(2,1)S(1)}, u32[]{:S(2)}, u32[]{:S(2)}) collective-permute-start(bf16[128,768]{1,0:T(8,128)(2,1)S(1)} %collective-permute-done.21), channel_id=1, source_target_pairs={{16,0},{32,16},{48,32},{64,48},{80,64},{96,80},{112,96},{128,112},... | collective-permute-start | bytes 589832 | tf_op jit(solution)/shard_map/ppermute | solution.py:13
  135.3 11.5 %collective-permute-start.9 = (bf16[128,768]{1,0:T(8,128)(2,1)S(1)}, bf16[128,768]{1,0:T(8,128)(2,1)S(1)}, u32[]{:S(2)}, u32[]{:S(2)}) collective-permute-start(bf16[128,768]{1,0:T(8,128)(2,1)S(1)} %collective-permute-done.8), channel_id=1, source_target_pairs={{0,16},{16,32},{32,48},{48,64},{64,80},{80,96},{96,112},{112,128},... | collective-permute-start | bytes 589832 | tf_op jit(solution)/shard_map/ppermute | solution.py:13
  144.6 11.2 %collective-permute-start.23 = (bf16[128,768]{1,0:T(8,128)(2,1)S(1)}, bf16[128,768]{1,0:T(8,128)(2,1)S(1)}, u32[]{:S(2)}, u32[]{:S(2)}) collective-permute-start(bf16[128,768]{1,0:T(8,128)(2,1)S(1)} %collective-permute-done.22), channel_id=1, source_target_pairs={{16,0},{32,16},{48,32},{64,48},{80,64},{96,80},{112,96},{128,112},... | collective-permute-start | bytes 589832 | tf_op jit(solution)/shard_map/ppermute | solution.py:13
  146.8 10.9 %collective-permute-start.10 = (bf16[128,768]{1,0:T(8,128)(2,1)S(1)}, bf16[128,768]{1,0:T(8,128)(2,1)S(1)}, u32[]{:S(2)}, u32[]{:S(2)}) collective-permute-start(bf16[128,768]{1,0:T(8,128)(2,1)S(1)} %collective-permute-done.9), channel_id=1, source_target_pairs={{0,16},{16,32},{32,48},{48,64},{64,80},{80,96},{96,112},{112,128},... | collective-permute-start | bytes 589832 | tf_op jit(solution)/shard_map/ppermute | solution.py:13
  155.7 9.7 %collective-permute-start.24 = (bf16[128,768]{1,0:T(8,128)(2,1)S(1)}, bf16[128,768]{1,0:T(8,128)(2,1)S(1)}, u32[]{:S(2)}, u32[]{:S(2)}) collective-permute-start(bf16[128,768]{1,0:T(8,128)(2,1)S(1)} %collective-permute-done.23), channel_id=1, source_target_pairs={{16,0},{32,16},{48,32},{64,48},{80,64},{96,80},{112,96},{128,112},... | collective-permute-start | bytes 589832 | tf_op jit(solution)/shard_map/ppermute | solution.py:13
  157.7 30.6 %collective-permute-start.11 = (bf16[128,768]{1,0:T(8,128)(2,1)S(1)}, bf16[128,768]{1,0:T(8,128)(2,1)S(1)}, u32[]{:S(2)}, u32[]{:S(2)}) collective-permute-start(bf16[128,768]{1,0:T(8,128)(2,1)S(1)} %collective-permute-done.10), channel_id=1, source_target_pairs={{0,16},{16,32},{32,48},{48,64},{64,80},{80,96},{96,112},{112,128},... | collective-permute-start | bytes 589832 | tf_op jit(solution)/shard_map/ppermute | solution.py:13
  170.9 25.2 %collective-permute-start.25 = (f32[256,512]{1,0:T(8,128)S(1)}, f32[256,512]{1,0:T(8,128)S(1)}, u32[]{:S(2)}, u32[]{:S(2)}) collective-permute-start(f32[256,512]{1,0:T(8,128)S(1)} %fusion.16), channel_id=1, source_target_pairs={{128,0},{144,16},{160,32},{176,48},{192,64},{208,80},{224,96},{240... | collective-permute-start | bytes 1572872 | tf_op jit(solution)/shard_map/ppermute | solution.py:13
  194.1 12.3 %collective-permute-start.12 = (f32[256,512]{1,0:T(8,128)S(1)}, f32[256,512]{1,0:T(8,128)S(1)}, u32[]{:S(2)}, u32[]{:S(2)}) collective-permute-start(f32[256,512]{1,0:T(8,128)S(1)} %fusion.24), channel_id=1, source_target_pairs={{0,128},{16,144},{32,160},{48,176},{64,192},{80,208},{96,224},{112... | collective-permute-start | bytes 1572872 | tf_op jit(solution)/shard_map/ppermute | solution.py:13

commit v4 on v2

--- a/solution.py
+++ b/solution.py
@@ -38,19 +38,45 @@
     return (weights, per_head_decay_rate, tail_decay, block_decay)
 
 
-def windowed_scan(own, own_decay, direction):
-    rows, cols = own.shape
-    gain_rows = jnp.broadcast_to(own_decay, (8, cols)).astype(own.dtype)
-    message = jnp.concatenate([own, gain_rows], axis=0)
-    keep = (lax.broadcasted_iota(jnp.int32, (rows + 8, 1), 0) < rows).astype(own.dtype)
-    current = passed_along(message, "ctx", direction)
-    offset = 1
-    while offset < WINDOW_BLOCKS:
-        pulled = passed_along(current, "ctx", direction * offset)
-        gain = current[rows, 0]
-        current = gain * pulled + current * keep
-        offset *= 2
-    return current[:rows]
+RELAY_BLOCKS = WINDOW_BLOCKS // 2
+GAIN_ROWS = 8
+
+
+def pieces_of(decay):
+    high = lax.reduce_precision(decay, exponent_bits=8, mantissa_bits=7)
+    rest = decay - high
+    middle = lax.reduce_precision(rest, exponent_bits=8, mantissa_bits=7)
+    return jnp.stack([high, middle, rest - middle])
+
+
+def relayed_partial(left, right, own_decay, direction):
+    rows = left.shape[0]
+    split = left.shape[1]
+    cols = split + right.shape[1]
+    parts = jnp.zeros((GAIN_ROWS, cols), jnp.float32).at[:3, :].set(pieces_of(own_decay)[:, None])
+    moving = jnp.concatenate(
+        [jnp.concatenate([left, right], axis=1), parts.astype(jnp.bfloat16)], axis=0
+    )
+    acc = None
+    gain = None
+    for _ in range(RELAY_BLOCKS):
+        moving = passed_along(moving, "ctx", direction)
+        update = jnp.einsum(
+            "cd,ce->de",
+            moving[:rows, :split],
+            moving[:rows, split:],
+            preferred_element_type=jnp.float32,
+        )
+        coded = moving[rows : rows + 3, 0].astype(jnp.float32)
+        decay = (coded[0] + coded[1]) + coded[2]
+        if acc is None:
+            acc = update
+            gain = decay
+        else:
+            acc = acc + gain * update
+            gain = gain * decay
+    joined = passed_along(acc, "ctx", direction * RELAY_BLOCKS)
+    return gain * joined + acc
 
 
 def per_device(queries, keys, values, grad_out, log_decay, doc_lengths):
@@ -83,17 +109,11 @@
     value_block_list = value_rows.reshape(block_count, BLOCK, value_dim)
     gradient_block_list = grad_out.reshape(block_count, BLOCK, value_dim)
     keyed_blocks = (key_blocks * tail_decay[:, :, None]).astype(jnp.bfloat16)
-    updates = jnp.einsum(
-        "ncd,nce->nde", keyed_blocks, value_block_list, preferred_element_type=jnp.float32
-    )
     queried = (query_block_list * (per_head_decay_rate * score_scaling)[:, :, None]).astype(
         jnp.bfloat16
     )
-    back_updates = jnp.einsum(
-        "ncd,nce->nde", queried, gradient_block_list, preferred_element_type=jnp.float32
-    )
-    states = windowed_scan(updates[0], block_decay[0], 1)[None]
-    ends = windowed_scan(back_updates[0], block_decay[0], -1)[None]
+    states = relayed_partial(keyed_blocks[0], value_block_list[0], block_decay[0], 1)[None]
+    ends = relayed_partial(queried[0], gradient_block_list[0], block_decay[0], -1)[None]
     lowered_state = states.astype(jnp.bfloat16)
     back_low = ends.astype(jnp.bfloat16)
     scores = jnp.einsum(

time: 216 us -> 194 us (0.90)
  the two profiles are of different devices: /device:TPU:40 before, /device:TPU:6 now
where the time goes in v4:
time: 194 us; the launch traced here: 192 us
  starting transfers between devices  101 us (52%)
  between operations  36.9 us (19%)
  waiting for transfers between devices  21.5 us (11%)
  local copies, waits for them, and re-layouts  13.6 us (7%)
  matrix products  11.6 us (6%)
  other arithmetic  8.22 us (4%)
    ppermute x18, starting transfers between devices, passed_along(): return lax.ppermute(block, axis, route)  83.8 us
    ppermute x18, waiting for transfers between devices, passed_along(): return lax.ppermute(block, axis, route)  21.5 us
    all_to_all x1, starting transfers between devices, per_device(): lax.all_to_all(packed, 'head', split_axis=1, concat_axis=0, tiled=True)  16.8 us
    slice x16, local copies, waits for them, and re-layouts, relayed_partial(): decay = coded[0] + coded[1] + coded[2]  8.87 us
    dot_general x16, matrix products, relayed_partial(): jnp.einsum('cd,ce->de', moving[:rows, :split], moving[:rows, split:], pre...  7.73 us
  transfers between devices with their start and end apart: 19, of which 15 were waited for; matrix products, arithmetic and copies ran while one was open for 12% of the time, Pallas kernels for 0%

profile of v4, /device:TPU:6, one launch (start us, length us, event | category | flops | bytes accessed | tf_op | source)
XLA Modules:
  0.0 192.4 jit_solution(2865253683221500840)
XLA Ops:
  0.6 1.7 pad_maximum_fusion
  2.3 16.8 %all-to-all-start = ((bf16[8,16,1024]{2,0,1:T(8,128)(2,1)}), bf16[8,16,1024]{2,0,1:T(8,128)(2,1)S(1)}, u32[]{:S(2)}, u32[]{:S(2)}) async-start(bf16[8,16,1024]{2,0,1:T(8,128)(2,1)} %pad_maximum_fusion), calls=%async_computation | async-start | bytes 524288 | tf_op jit(solution)/shard_map/all_to_all | solution.py:95
  19.1 0.6 copy-done.1
  21.1 0.6 slice.392
  21.7 0.7 compare_bitcast_fusion
  22.4 0.6 slice.395
  28.0 0.6 slice.391
  28.7 2.0 %fusion.69 = (f32[128]{0:T(128)S(1)}, f32[128]{0:T(128)S(1)}) fusion(s32[]{:T(128)} %bitcast.11, f32[1,128]{1,0:T(1,128)S(1)} %reduce_window_sum.20, s32[129]{0:T(256)S(1)} %broadcast_add_fusion, f32[]{:T(128)} %bitcast.9, s32[]{:T(128)} %bitcast.8), kind=kLoop, calls=%fused_computation.119 | loop fusion | flops 768 | bytes 2060 | tf_op jit(solution)/shard_map/mul | solution.py:127
  31.1 0.7 copy-done
  32.5 3.6 %collective-permute-start = (bf16[136,768]{1,0:T(8,128)(2,1)S(1)}, bf16[136,768]{1,0:T(8,128)(2,1)S(1)}, u32[]{:S(2)}, u32[]{:S(2)}) collective-permute-start(bf16[136,768]{1,0:T(8,128)(2,1)S(1)} %get-tuple-element.91), channel_id=1, source_target_pairs={{0,16},{16,32},{32,48},{48,64},{64,80},{80,96},{96,112},{112,128},... | collective-permute-start | bytes 626696 | tf_op jit(solution)/shard_map/ppermute | solution.py:13
  36.3 4.5 %collective-permute-start.9 = (bf16[136,768]{1,0:T(8,128)(2,1)S(1)}, bf16[136,768]{1,0:T(8,128)(2,1)S(1)}, u32[]{:S(2)}, u32[]{:S(2)}) collective-permute-start(bf16[136,768]{1,0:T(8,128)(2,1)S(1)} %get-tuple-element.90), channel_id=1, source_target_pairs={{16,0},{32,16},{48,32},{64,48},{80,64},{96,80},{112,96},{128,112},... | collective-permute-start | bytes 626696 | tf_op jit(solution)/shard_map/ppermute | solution.py:13
  40.9 3.4 %collective-permute-done = bf16[136,768]{1,0:T(8,128)(2,1)S(1)} collective-permute-done((bf16[136,768]{1,0:T(8,128)(2,1)S(1)}, bf16[136,768]{1,0:T(8,128)(2,1)S(1)}, u32[]{:S(2)}, u32[]{:S(2)}) %collective-permute-start) | collective-permute-done | bytes 208928 | tf_op jit(solution)/shard_map/ppermute | solution.py:13
  44.3 0.5 fusion.89
  44.9 0.9 collective-permute-done.9
  45.7 0.6 fusion.81
  50.4 3.2 %collective-permute-start.1 = (bf16[136,768]{1,0:T(8,128)(2,1)S(1)}, bf16[136,768]{1,0:T(8,128)(2,1)}, u32[]{:S(2)}, u32[]{:S(2)}) collective-permute-start(bf16[136,768]{1,0:T(8,128)(2,1)S(1)} %collective-permute-done), channel_id=1, source_target_pairs={{0,16},{16,32},{32,48},{48,64},{64,80},{80,96},{96,112},{112,128},... | collective-permute-start | bytes 626696 | tf_op jit(solution)/shard_map/ppermute | solution.py:13
  53.7 5.2 %collective-permute-start.10 = (bf16[136,768]{1,0:T(8,128)(2,1)S(1)}, bf16[136,768]{1,0:T(8,128)(2,1)S(1)}, u32[]{:S(2)}, u32[]{:S(2)}) collective-permute-start(bf16[136,768]{1,0:T(8,128)(2,1)S(1)} %collective-permute-done.9), channel_id=1, source_target_pairs={{16,0},{32,16},{48,32},{64,48},{80,64},{96,80},{112,96},{128,112},... | collective-permute-start | bytes 626696 | tf_op jit(solution)/shard_map/ppermute | solution.py:13
  59.1 2.8 %collective-permute-done.1 = bf16[136,768]{1,0:T(8,128)(2,1)} collective-permute-done((bf16[136,768]{1,0:T(8,128)(2,1)S(1)}, bf16[136,768]{1,0:T(8,128)(2,1)}, u32[]{:S(2)}, u32[]{:S(2)}) %collective-permute-start.1) | collective-permute-done | bytes 208928 | tf_op jit(solution)/shard_map/ppermute | solution.py:13
  61.9 0.7 slice_convert_fusion.14
  62.6 0.5 fusion.88
  63.1 0.6 fusion.80
  67.5 4.5 %collective-permute-start.2 = (bf16[136,768]{1,0:T(8,128)(2,1)}, bf16[136,768]{1,0:T(8,128)(2,1)S(1)}, u32[]{:S(2)}, u32[]{:S(2)}) collective-permute-start(bf16[136,768]{1,0:T(8,128)(2,1)} %collective-permute-done.1), channel_id=1, source_target_pairs={{0,16},{16,32},{32,48},{48,64},{64,80},{80,96},{96,112},{112,128},... | collective-permute-start | bytes 626696 | tf_op jit(solution)/shard_map/ppermute | solution.py:13
  72.0 3.8 %collective-permute-start.11 = (bf16[136,768]{1,0:T(8,128)(2,1)S(1)}, bf16[136,768]{1,0:T(8,128)(2,1)S(1)}, u32[]{:S(2)}, u32[]{:S(2)}) collective-permute-start(bf16[136,768]{1,0:T(8,128)(2,1)S(1)} %collective-permute-done.10), channel_id=1, source_target_pairs={{16,0},{32,16},{48,32},{64,48},{80,64},{96,80},{112,96},{128,112},... | collective-permute-start | bytes 626696 | tf_op jit(solution)/shard_map/ppermute | solution.py:13
  75.8 1.2 fusion
  77.3 0.8 collective-permute-done.2
  78.1 0.5 fusion.87
  78.6 1.1 collective-permute-done.11
  79.7 0.6 fusion.79
  84.2 3.6 %collective-permute-start.3 = (bf16[136,768]{1,0:T(8,128)(2,1)S(1)}, bf16[136,768]{1,0:T(8,128)(2,1)}, u32[]{:S(2)}, u32[]{:S(2)}) collective-permute-start(bf16[136,768]{1,0:T(8,128)(2,1)S(1)} %collective-permute-done.2), channel_id=1, source_target_pairs={{0,16},{16,32},{32,48},{48,64},{64,80},{80,96},{96,112},{112,128},... | collective-permute-start | bytes 626696 | tf_op jit(solution)/shard_map/ppermute | solution.py:13
  87.8 4.3 %collective-permute-start.12 = (bf16[136,768]{1,0:T(8,128)(2,1)S(1)}, bf16[136,768]{1,0:T(8,128)(2,1)S(1)}, u32[]{:S(2)}, u32[]{:S(2)}) collective-permute-start(bf16[136,768]{1,0:T(8,128)(2,1)S(1)} %collective-permute-done.11), channel_id=1, source_target_pairs={{16,0},{32,16},{48,32},{64,48},{80,64},{96,80},{112,96},{128,112},... | collective-permute-start | bytes 626696 | tf_op jit(solution)/shard_map/ppermute | solution.py:13
  92.6 1.4 collective-permute-done.3
  94.1 0.7 slice_convert_fusion.12
  94.7 0.5 fusion.86
  95.5 0.6 fusion.78
  100.0 3.4 %collective-permute-start.4 = (bf16[136,768]{1,0:T(8,128)(2,1)}, bf16[136,768]{1,0:T(8,128)(2,1)S(1)}, u32[]{:S(2)}, u32[]{:S(2)}) collective-permute-start(bf16[136,768]{1,0:T(8,128)(2,1)} %collective-permute-done.3), channel_id=1, source_target_pairs={{0,16},{16,32},{32,48},{48,64},{64,80},{80,96},{96,112},{112,128},... | collective-permute-start | bytes 626696 | tf_op jit(solution)/shard_map/ppermute | solution.py:13
  103.4 4.9 %collective-permute-start.13 = (bf16[136,768]{1,0:T(8,128)(2,1)S(1)}, bf16[136,768]{1,0:T(8,128)(2,1)S(1)}, u32[]{:S(2)}, u32[]{:S(2)}) collective-permute-start(bf16[136,768]{1,0:T(8,128)(2,1)S(1)} %collective-permute-done.12), channel_id=1, source_target_pairs={{16,0},{32,16},{48,32},{64,48},{80,64},{96,80},{112,96},{128,112},... | collective-permute-start | bytes 626696 | tf_op jit(solution)/shard_map/ppermute | solution.py:13
  108.3 1.2 fusion.2
  109.8 0.6 collective-permute-done.4
  110.4 0.5 fusion.85
  110.9 0.7 collective-permute-done.13
  111.6 0.6 fusion.77
  116.1 3.0 %collective-permute-start.5 = (bf16[136,768]{1,0:T(8,128)(2,1)S(1)}, bf16[136,768]{1,0:T(8,128)(2,1)}, u32[]{:S(2)}, u32[]{:S(2)}) collective-permute-start(bf16[136,768]{1,0:T(8,128)(2,1)S(1)} %collective-permute-done.4), channel_id=1, source_target_pairs={{0,16},{16,32},{32,48},{48,64},{64,80},{80,96},{96,112},{112,128},... | collective-permute-start | bytes 626696 | tf_op jit(solution)/shard_map/ppermute | solution.py:13
  119.1 5.4 %collective-permute-start.14 = (bf16[136,768]{1,0:T(8,128)(2,1)S(1)}, bf16[136,768]{1,0:T(8,128)(2,1)S(1)}, u32[]{:S(2)}, u32[]{:S(2)}) collective-permute-start(bf16[136,768]{1,0:T(8,128)(2,1)S(1)} %collective-permute-done.13), channel_id=1, source_target_pairs={{16,0},{32,16},{48,32},{64,48},{80,64},{96,80},{112,96},{128,112},... | collective-permute-start | bytes 626696 | tf_op jit(solution)/shard_map/ppermute | solution.py:13
  125.0 1.4 collective-permute-done.5
  126.5 0.7 slice_convert_fusion.10
  127.8 0.6 fusion.76
  132.3 4.2 %collective-permute-start.6 = (bf16[136,768]{1,0:T(8,128)(2,1)}, bf16[136,768]{1,0:T(8,128)(2,1)S(1)}, u32[]{:S(2)}, u32[]{:S(2)}) collective-permute-start(bf16[136,768]{1,0:T(8,128)(2,1)} %collective-permute-done.5), channel_id=1, source_target_pairs={{0,16},{16,32},{32,48},{48,64},{64,80},{80,96},{96,112},{112,128},... | collective-permute-start | bytes 626696 | tf_op jit(solution)/shard_map/ppermute | solution.py:13
  136.6 4.2 %collective-permute-start.15 = (bf16[136,768]{1,0:T(8,128)(2,1)S(1)}, bf16[136,768]{1,0:T(8,128)(2,1)}, u32[]{:S(2)}, u32[]{:S(2)}) collective-permute-start(bf16[136,768]{1,0:T(8,128)(2,1)S(1)} %collective-permute-done.14), channel_id=1, source_target_pairs={{16,0},{32,16},{48,32},{64,48},{80,64},{96,80},{112,96},{128,112},... | collective-permute-start | bytes 626696 | tf_op jit(solution)/shard_map/ppermute | solution.py:13
  140.8 1.2 fusion.4
  142.2 0.6 collective-permute-done.6
  142.8 0.5 fusion.83
  143.3 1.0 collective-permute-done.15
  144.4 0.7 slice_convert_fusion.1
  145.0 0.6 fusion.75
  149.5 5.2 %collective-permute-start.7 = (bf16[136,768]{1,0:T(8,128)(2,1)S(1)}, bf16[136,768]{1,0:T(8,128)(2,1)S(1)}, u32[]{:S(2)}, u32[]{:S(2)}) collective-permute-start(bf16[136,768]{1,0:T(8,128)(2,1)S(1)} %collective-permute-done.6), channel_id=1, source_target_pairs={{0,16},{16,32},{32,48},{48,64},{64,80},{80,96},{96,112},{112,128},... | collective-permute-start | bytes 626696 | tf_op jit(solution)/shard_map/ppermute | solution.py:13
  154.7 3.0 %collective-permute-start.16 = (bf16[136,768]{1,0:T(8,128)(2,1)}, bf16[136,768]{1,0:T(8,128)(2,1)S(1)}, u32[]{:S(2)}, u32[]{:S(2)}) collective-permute-start(bf16[136,768]{1,0:T(8,128)(2,1)} %collective-permute-done.15), channel_id=1, source_target_pairs={{16,0},{32,16},{48,32},{64,48},{80,64},{96,80},{112,96},{128,112},... | collective-permute-start | bytes 626696 | tf_op jit(solution)/shard_map/ppermute | solution.py:13
  158.0 1.2 fusion.12
  159.8 15.7 %collective-permute-start.8 = (f32[256,512]{1,0:T(8,128)S(1)}, f32[256,512]{1,0:T(8,128)S(1)}, u32[]{:S(2)}, u32[]{:S(2)}) collective-permute-start(f32[256,512]{1,0:T(8,128)S(1)} %fusion.6), channel_id=1, source_target_pairs={{0,128},{16,144},{32,160},{48,176},{64,192},{80,208},{96,224},{112... | collective-permute-start | bytes 1572872 | tf_op jit(solution)/shard_map/ppermute | solution.py:13
  178.3 1.9 collective-permute-start.17
  183.1 0.7 copy.21
  183.8 0.8 fusion.16
  184.7 5.9 %collective-permute-done.17 = f32[256,512]{1,0:T(8,128)S(1)} collective-permute-done((f32[256,512]{1,0:T(8,128)S(1)}, f32[256,512]{1,0:T(8,128)S(1)}, u32[]{:S(2)}, u32[]{:S(2)}) %collective-permute-start.17) | collective-permute-done | bytes 524320 | tf_op jit(solution)/shard_map/ppermute | solution.py:13
  190.7 0.9 fusion.22
  191.6 0.8 fusion.17
  (62 shorter events, 8.7 us)
Async XLA Ops:
  2.3 28.4 %all-to-all-start = ((bf16[8,16,1024]{2,0,1:T(8,128)(2,1)}), bf16[8,16,1024]{2,0,1:T(8,128)(2,1)S(1)}, u32[]{:S(2)}, u32[]{:S(2)}) async-start(bf16[8,16,1024]{2,0,1:T(8,128)(2,1)} %pad_maximum_fusion), calls=%async_computation | async-start | bytes 524288 | tf_op jit(solution)/shard_map/all_to_all | solution.py:95
  19.1 0.7 copy-start.1
  20.1 0.7 copy-start.2
  30.9 0.9 copy-start
  32.5 11.9 %collective-permute-start = (bf16[136,768]{1,0:T(8,128)(2,1)S(1)}, bf16[136,768]{1,0:T(8,128)(2,1)S(1)}, u32[]{:S(2)}, u32[]{:S(2)}) collective-permute-start(bf16[136,768]{1,0:T(8,128)(2,1)S(1)} %get-tuple-element.91), channel_id=1, source_target_pairs={{0,16},{16,32},{32,48},{48,64},{64,80},{80,96},{96,112},{112,128},... | collective-permute-start | bytes 626696 | tf_op jit(solution)/shard_map/ppermute | solution.py:13
  36.3 9.4 %collective-permute-start.9 = (bf16[136,768]{1,0:T(8,128)(2,1)S(1)}, bf16[136,768]{1,0:T(8,128)(2,1)S(1)}, u32[]{:S(2)}, u32[]{:S(2)}) collective-permute-start(bf16[136,768]{1,0:T(8,128)(2,1)S(1)} %get-tuple-element.90), channel_id=1, source_target_pairs={{16,0},{32,16},{48,32},{64,48},{80,64},{96,80},{112,96},{128,112},... | collective-permute-start | bytes 626696 | tf_op jit(solution)/shard_map/ppermute | solution.py:13
  50.4 11.5 %collective-permute-start.1 = (bf16[136,768]{1,0:T(8,128)(2,1)S(1)}, bf16[136,768]{1,0:T(8,128)(2,1)}, u32[]{:S(2)}, u32[]{:S(2)}) collective-permute-start(bf16[136,768]{1,0:T(8,128)(2,1)S(1)} %collective-permute-done), channel_id=1, source_target_pairs={{0,16},{16,32},{32,48},{48,64},{64,80},{80,96},{96,112},{112,128},... | collective-permute-start | bytes 626696 | tf_op jit(solution)/shard_map/ppermute | solution.py:13
  53.7 9.4 %collective-permute-start.10 = (bf16[136,768]{1,0:T(8,128)(2,1)S(1)}, bf16[136,768]{1,0:T(8,128)(2,1)S(1)}, u32[]{:S(2)}, u32[]{:S(2)}) collective-permute-start(bf16[136,768]{1,0:T(8,128)(2,1)S(1)} %collective-permute-done.9), channel_id=1, source_target_pairs={{16,0},{32,16},{48,32},{64,48},{80,64},{96,80},{112,96},{128,112},... | collective-permute-start | bytes 626696 | tf_op jit(solution)/shard_map/ppermute | solution.py:13
  67.5 10.6 %collective-permute-start.2 = (bf16[136,768]{1,0:T(8,128)(2,1)}, bf16[136,768]{1,0:T(8,128)(2,1)S(1)}, u32[]{:S(2)}, u32[]{:S(2)}) collective-permute-start(bf16[136,768]{1,0:T(8,128)(2,1)} %collective-permute-done.1), channel_id=1, source_target_pairs={{0,16},{16,32},{32,48},{48,64},{64,80},{80,96},{96,112},{112,128},... | collective-permute-start | bytes 626696 | tf_op jit(solution)/shard_map/ppermute | solution.py:13
  72.0 7.7 %collective-permute-start.11 = (bf16[136,768]{1,0:T(8,128)(2,1)S(1)}, bf16[136,768]{1,0:T(8,128)(2,1)S(1)}, u32[]{:S(2)}, u32[]{:S(2)}) collective-permute-start(bf16[136,768]{1,0:T(8,128)(2,1)S(1)} %collective-permute-done.10), channel_id=1, source_target_pairs={{16,0},{32,16},{48,32},{64,48},{80,64},{96,80},{112,96},{128,112},... | collective-permute-start | bytes 626696 | tf_op jit(solution)/shard_map/ppermute | solution.py:13
  84.2 9.9 %collective-permute-start.3 = (bf16[136,768]{1,0:T(8,128)(2,1)S(1)}, bf16[136,768]{1,0:T(8,128)(2,1)}, u32[]{:S(2)}, u32[]{:S(2)}) collective-permute-start(bf16[136,768]{1,0:T(8,128)(2,1)S(1)} %collective-permute-done.2), channel_id=1, source_target_pairs={{0,16},{16,32},{32,48},{48,64},{64,80},{80,96},{96,112},{112,128},... | collective-permute-start | bytes 626696 | tf_op jit(solution)/shard_map/ppermute | solution.py:13
  87.8 7.7 %collective-permute-start.12 = (bf16[136,768]{1,0:T(8,128)(2,1)S(1)}, bf16[136,768]{1,0:T(8,128)(2,1)S(1)}, u32[]{:S(2)}, u32[]{:S(2)}) collective-permute-start(bf16[136,768]{1,0:T(8,128)(2,1)S(1)} %collective-permute-done.11), channel_id=1, source_target_pairs={{16,0},{32,16},{48,32},{64,48},{80,64},{96,80},{112,96},{128,112},... | collective-permute-start | bytes 626696 | tf_op jit(solution)/shard_map/ppermute | solution.py:13
  100.0 10.4 %collective-permute-start.4 = (bf16[136,768]{1,0:T(8,128)(2,1)}, bf16[136,768]{1,0:T(8,128)(2,1)S(1)}, u32[]{:S(2)}, u32[]{:S(2)}) collective-permute-start(bf16[136,768]{1,0:T(8,128)(2,1)} %collective-permute-done.3), channel_id=1, source_target_pairs={{0,16},{16,32},{32,48},{48,64},{64,80},{80,96},{96,112},{112,128},... | collective-permute-start | bytes 626696 | tf_op jit(solution)/shard_map/ppermute | solution.py:13
  103.4 8.2 %collective-permute-start.13 = (bf16[136,768]{1,0:T(8,128)(2,1)S(1)}, bf16[136,768]{1,0:T(8,128)(2,1)S(1)}, u32[]{:S(2)}, u32[]{:S(2)}) collective-permute-start(bf16[136,768]{1,0:T(8,128)(2,1)S(1)} %collective-permute-done.12), channel_id=1, source_target_pairs={{16,0},{32,16},{48,32},{64,48},{80,64},{96,80},{112,96},{128,112},... | collective-permute-start | bytes 626696 | tf_op jit(solution)/shard_map/ppermute | solution.py:13
  116.1 10.4 %collective-permute-start.5 = (bf16[136,768]{1,0:T(8,128)(2,1)S(1)}, bf16[136,768]{1,0:T(8,128)(2,1)}, u32[]{:S(2)}, u32[]{:S(2)}) collective-permute-start(bf16[136,768]{1,0:T(8,128)(2,1)S(1)} %collective-permute-done.4), channel_id=1, source_target_pairs={{0,16},{16,32},{32,48},{48,64},{64,80},{80,96},{96,112},{112,128},... | collective-permute-start | bytes 626696 | tf_op jit(solution)/shard_map/ppermute | solution.py:13
  119.1 8.7 %collective-permute-start.14 = (bf16[136,768]{1,0:T(8,128)(2,1)S(1)}, bf16[136,768]{1,0:T(8,128)(2,1)S(1)}, u32[]{:S(2)}, u32[]{:S(2)}) collective-permute-start(bf16[136,768]{1,0:T(8,128)(2,1)S(1)} %collective-permute-done.13), channel_id=1, source_target_pairs={{16,0},{32,16},{48,32},{64,48},{80,64},{96,80},{112,96},{128,112},... | collective-permute-start | bytes 626696 | tf_op jit(solution)/shard_map/ppermute | solution.py:13
  132.3 10.5 %collective-permute-start.6 = (bf16[136,768]{1,0:T(8,128)(2,1)}, bf16[136,768]{1,0:T(8,128)(2,1)S(1)}, u32[]{:S(2)}, u32[]{:S(2)}) collective-permute-start(bf16[136,768]{1,0:T(8,128)(2,1)} %collective-permute-done.5), channel_id=1, source_target_pairs={{0,16},{16,32},{32,48},{48,64},{64,80},{80,96},{96,112},{112,128},... | collective-permute-start | bytes 626696 | tf_op jit(solution)/shard_map/ppermute | solution.py:13
  136.6 7.8 %collective-permute-start.15 = (bf16[136,768]{1,0:T(8,128)(2,1)S(1)}, bf16[136,768]{1,0:T(8,128)(2,1)}, u32[]{:S(2)}, u32[]{:S(2)}) collective-permute-start(bf16[136,768]{1,0:T(8,128)(2,1)S(1)} %collective-permute-done.14), channel_id=1, source_target_pairs={{16,0},{32,16},{48,32},{64,48},{80,64},{96,80},{112,96},{128,112},... | collective-permute-start | bytes 626696 | tf_op jit(solution)/shard_map/ppermute | solution.py:13
  149.5 10.1 %collective-permute-start.7 = (bf16[136,768]{1,0:T(8,128)(2,1)S(1)}, bf16[136,768]{1,0:T(8,128)(2,1)S(1)}, u32[]{:S(2)}, u32[]{:S(2)}) collective-permute-start(bf16[136,768]{1,0:T(8,128)(2,1)S(1)} %collective-permute-done.6), channel_id=1, source_target_pairs={{0,16},{16,32},{32,48},{48,64},{64,80},{80,96},{96,112},{112,128},... | collective-permute-start | bytes 626696 | tf_op jit(solution)/shard_map/ppermute | solution.py:13
  154.7 23.3 %collective-permute-start.16 = (bf16[136,768]{1,0:T(8,128)(2,1)}, bf16[136,768]{1,0:T(8,128)(2,1)S(1)}, u32[]{:S(2)}, u32[]{:S(2)}) collective-permute-start(bf16[136,768]{1,0:T(8,128)(2,1)} %collective-permute-done.15), channel_id=1, source_target_pairs={{16,0},{32,16},{48,32},{64,48},{80,64},{96,80},{112,96},{128,112},... | collective-permute-start | bytes 626696 | tf_op jit(solution)/shard_map/ppermute | solution.py:13
  159.8 22.9 %collective-permute-start.8 = (f32[256,512]{1,0:T(8,128)S(1)}, f32[256,512]{1,0:T(8,128)S(1)}, u32[]{:S(2)}, u32[]{:S(2)}) collective-permute-start(f32[256,512]{1,0:T(8,128)S(1)} %fusion.6), channel_id=1, source_target_pairs={{0,128},{16,144},{32,160},{48,176},{64,192},{80,208},{96,224},{112... | collective-permute-start | bytes 1572872 | tf_op jit(solution)/shard_map/ppermute | solution.py:13
  178.3 12.3 %collective-permute-start.17 = (f32[256,512]{1,0:T(8,128)S(1)}, f32[256,512]{1,0:T(8,128)S(1)}, u32[]{:S(2)}, u32[]{:S(2)}) collective-permute-start(f32[256,512]{1,0:T(8,128)S(1)} %fusion.13), channel_id=1, source_target_pairs={{128,0},{144,16},{160,32},{176,48},{192,64},{208,80},{224,96},{240... | collective-permute-start | bytes 1572872 | tf_op jit(solution)/shard_map/ppermute | solution.py:13

commit v5 on v4

--- a/solution.py
+++ b/solution.py
@@ -57,24 +57,26 @@
     moving = jnp.concatenate(
         [jnp.concatenate([left, right], axis=1), parts.astype(jnp.bfloat16)], axis=0
     )
-    acc = None
-    gain = None
+    received = []
     for _ in range(RELAY_BLOCKS):
         moving = passed_along(moving, "ctx", direction)
-        update = jnp.einsum(
-            "cd,ce->de",
-            moving[:rows, :split],
-            moving[:rows, split:],
-            preferred_element_type=jnp.float32,
-        )
-        coded = moving[rows : rows + 3, 0].astype(jnp.float32)
-        decay = (coded[0] + coded[1]) + coded[2]
-        if acc is None:
-            acc = update
-            gain = decay
-        else:
-            acc = acc + gain * update
-            gain = gain * decay
+        received.append(moving)
+    stacked = jnp.stack(received)
+    updates = jnp.einsum(
+        "kcd,kce->kde",
+        stacked[:, :rows, :split],
+        stacked[:, :rows, split:],
+        preferred_element_type=jnp.float32,
+    )
+    coded = stacked[:, rows : rows + 3, 0].astype(jnp.float32)
+    decays = (coded[:, 0] + coded[:, 1]) + coded[:, 2]
+    weights = [jnp.float32(1.0)]
+    for k in range(1, RELAY_BLOCKS + 1):
+        weights.append(weights[-1] * decays[k - 1])
+    gain = weights[RELAY_BLOCKS]
+    acc = updates[0]
+    for k in range(1, RELAY_BLOCKS):
+        acc = acc + weights[k] * updates[k]
     joined = passed_along(acc, "ctx", direction * RELAY_BLOCKS)
     return gain * joined + acc
 

time: 194 us -> 163 us (0.84)
  the two profiles are of different devices: /device:TPU:6 before, /device:TPU:120 now
where the time goes in v5:
time: 163 us; the launch traced here: 162 us
  starting transfers between devices  94 us (58%)
  waiting for transfers between devices  22.2 us (14%)
  between operations  16.3 us (10%)
  other arithmetic  14.8 us (9%)
  local copies, waits for them, and re-layouts  7.57 us (5%)
  matrix products  7.39 us (5%)
    ppermute x18, starting transfers between devices, passed_along(): return lax.ppermute(block, axis, route)  77.2 us
    ppermute x18, waiting for transfers between devices, passed_along(): return lax.ppermute(block, axis, route)  22.2 us
    all_to_all x1, starting transfers between devices, per_device(): lax.all_to_all(packed, 'head', split_axis=1, concat_axis=0, tiled=True)  16.8 us
    add x2, other arithmetic, relayed_partial(): acc = acc + weights[k] * updates[k]  4.63 us
    dot_general x2, matrix products, relayed_partial(): jnp.einsum('kcd,kce->kde', stacked[:, :rows, :split], stacked[:, :rows, s...  3.47 us
  transfers between devices with their start and end apart: 19, of which 9 were waited for; matrix products, arithmetic and copies ran while one was open for 15% of the time, Pallas kernels for 0%

profile of v5, /device:TPU:120, one launch (start us, length us, event | category | flops | bytes accessed | tf_op | source)
XLA Modules:
  0.0 162.2 jit_solution(15404154174393123493)
XLA Ops:
  0.6 1.7 %pad_maximum_fusion = bf16[8,16,1024]{2,0,1:T(8,128)(2,1)} fusion(bf16[8,16,512]{2,0,1:T(8,128)(2,1)} %bitcast.116, bf16[8,16,256]{2,0,1:T(8,128)(2,1)} %bitcast.117, bf16[8,16,256]{2,0,1:T(8,128)(2,1)} %bitcast.118), kind=kLoop, calls=%fused_computation.56 | loop fusion | flops 786432 | bytes 524288 | tf_op jit(solution)/shard_map/concatenate | solution.py:89
  2.3 16.8 %all-to-all-start = ((bf16[8,16,1024]{2,0,1:T(8,128)(2,1)}), bf16[8,16,1024]{2,0,1:T(8,128)(2,1)S(1)}, u32[]{:S(2)}, u32[]{:S(2)}) async-start(bf16[8,16,1024]{2,0,1:T(8,128)(2,1)} %pad_maximum_fusion), calls=%async_computation | async-start | bytes 524288 | tf_op jit(solution)/shard_map/all_to_all | solution.py:97
  19.1 0.7 copy.234
  19.9 0.1 reduce.3
  20.0 0.7 sub.43
  20.8 0.5 slice.206
  21.3 0.7 compare_bitcast_fusion
  22.0 0.6 slice.207
  22.6 1.0 reduce_window_sum.20
  23.6 0.6 slice.204
  29.2 0.6 slice.203
  29.9 2.0 %fusion.43 = (f32[128]{0:T(128)S(1)}, f32[128]{0:T(128)S(1)}) fusion(s32[]{:T(128)} %bitcast.11, f32[1,128]{1,0:T(1,128)S(1)} %reduce_window_sum.20, s32[129]{0:T(256)S(1)} %broadcast_add_fusion, f32[]{:T(128)} %bitcast.9, s32[]{:T(128)} %bitcast.8), kind=kLoop, calls=%fused_computation.97 | loop fusion | flops 768 | bytes 2060 | tf_op jit(solution)/shard_map/mul | solution.py:129
  31.9 0.2 fusion.10
  32.1 0.2 fusion.11
  32.3 0.2 fusion.50
  32.5 0.2 fusion.46
  32.7 0.1 multiply_convert_fusion
  32.8 0.1 maximum_maximum_fusion.1
  32.9 3.1 %collective-permute-start.9 = (bf16[136,768]{1,0:T(8,128)(2,1)S(1)}, bf16[136,768]{1,0:T(8,128)(2,1)S(1)}, u32[]{:S(2)}, u32[]{:S(2)}) collective-permute-start(bf16[136,768]{1,0:T(8,128)(2,1)S(1)} %get-tuple-element.90), channel_id=1, source_target_pairs={{16,0},{32,16},{48,32},{64,48},{80,64},{96,80},{112,96},{128,112},... | collective-permute-start | bytes 626696 | tf_op jit(solution)/shard_map/ppermute | solution.py:13
  36.1 0.2 fusion.39
  36.3 4.8 %collective-permute-start = (bf16[136,768]{1,0:T(8,128)(2,1)S(1)}, bf16[136,768]{1,0:T(8,128)(2,1)S(1)}, u32[]{:S(2)}, u32[]{:S(2)}) collective-permute-start(bf16[136,768]{1,0:T(8,128)(2,1)S(1)} %get-tuple-element.91), channel_id=1, source_target_pairs={{0,16},{16,32},{32,48},{48,64},{64,80},{80,96},{96,112},{112,128},... | collective-permute-start | bytes 626696 | tf_op jit(solution)/shard_map/ppermute | solution.py:13
  41.1 0.2 fusion.36
  41.3 3.1 %collective-permute-done.9 = bf16[136,768]{1,0:T(8,128)(2,1)S(1)} collective-permute-done((bf16[136,768]{1,0:T(8,128)(2,1)S(1)}, bf16[136,768]{1,0:T(8,128)(2,1)S(1)}, u32[]{:S(2)}, u32[]{:S(2)}) %collective-permute-start.9) | collective-permute-done | bytes 208928 | tf_op jit(solution)/shard_map/ppermute | solution.py:13
  44.4 1.9 %collective-permute-start.10 = (bf16[136,768]{1,0:T(8,128)(2,1)S(1)}, bf16[136,768]{1,0:T(8,128)(2,1)S(1)}, u32[]{:S(2)}, u32[]{:S(2)}) collective-permute-start(bf16[136,768]{1,0:T(8,128)(2,1)S(1)} %collective-permute-done.9), channel_id=1, source_target_pairs={{16,0},{32,16},{48,32},{64,48},{80,64},{96,80},{112,96},{128,112},... | collective-permute-start | bytes 626696 | tf_op jit(solution)/shard_map/ppermute | solution.py:13
  46.3 6.0 %collective-permute-start.1 = (bf16[136,768]{1,0:T(8,128)(2,1)S(1)}, bf16[136,768]{1,0:T(8,128)(2,1)S(1)}, u32[]{:S(2)}, u32[]{:S(2)}) collective-permute-start(bf16[136,768]{1,0:T(8,128)(2,1)S(1)} %collective-permute-done), channel_id=1, source_target_pairs={{0,16},{16,32},{32,48},{48,64},{64,80},{80,96},{96,112},{112,128},... | collective-permute-start | bytes 626696 | tf_op jit(solution)/shard_map/ppermute | solution.py:13
  52.4 2.6 %collective-permute-done.10 = bf16[136,768]{1,0:T(8,128)(2,1)S(1)} collective-permute-done((bf16[136,768]{1,0:T(8,128)(2,1)S(1)}, bf16[136,768]{1,0:T(8,128)(2,1)S(1)}, u32[]{:S(2)}, u32[]{:S(2)}) %collective-permute-start.10) | collective-permute-done | bytes 208928 | tf_op jit(solution)/shard_map/ppermute | solution.py:13
  55.0 1.9 %collective-permute-start.11 = (bf16[136,768]{1,0:T(8,128)(2,1)S(1)}, bf16[136,768]{1,0:T(8,128)(2,1)S(1)}, u32[]{:S(2)}, u32[]{:S(2)}) collective-permute-start(bf16[136,768]{1,0:T(8,128)(2,1)S(1)} %collective-permute-done.10), channel_id=1, source_target_pairs={{16,0},{32,16},{48,32},{64,48},{80,64},{96,80},{112,96},{128,112},... | collective-permute-start | bytes 626696 | tf_op jit(solution)/shard_map/ppermute | solution.py:13
  57.0 6.0 %collective-permute-start.2 = (bf16[136,768]{1,0:T(8,128)(2,1)S(1)}, bf16[136,768]{1,0:T(8,128)(2,1)S(1)}, u32[]{:S(2)}, u32[]{:S(2)}) collective-permute-start(bf16[136,768]{1,0:T(8,128)(2,1)S(1)} %collective-permute-done.1), channel_id=1, source_target_pairs={{0,16},{16,32},{32,48},{48,64},{64,80},{80,96},{96,112},{112,128},... | collective-permute-start | bytes 626696 | tf_op jit(solution)/shard_map/ppermute | solution.py:13
  63.0 1.8 %collective-permute-done.11 = bf16[136,768]{1,0:T(8,128)(2,1)S(1)} collective-permute-done((bf16[136,768]{1,0:T(8,128)(2,1)S(1)}, bf16[136,768]{1,0:T(8,128)(2,1)S(1)}, u32[]{:S(2)}, u32[]{:S(2)}) %collective-permute-start.11) | collective-permute-done | bytes 208928 | tf_op jit(solution)/shard_map/ppermute | solution.py:13
  64.8 1.9 %collective-permute-start.12 = (bf16[136,768]{1,0:T(8,128)(2,1)S(1)}, bf16[136,768]{1,0:T(8,128)(2,1)S(1)}, u32[]{:S(2)}, u32[]{:S(2)}) collective-permute-start(bf16[136,768]{1,0:T(8,128)(2,1)S(1)} %collective-permute-done.11), channel_id=1, source_target_pairs={{16,0},{32,16},{48,32},{64,48},{80,64},{96,80},{112,96},{128,112},... | collective-permute-start | bytes 626696 | tf_op jit(solution)/shard_map/ppermute | solution.py:13
  66.7 6.0 %collective-permute-start.3 = (bf16[136,768]{1,0:T(8,128)(2,1)S(1)}, bf16[136,768]{1,0:T(8,128)(2,1)S(1)}, u32[]{:S(2)}, u32[]{:S(2)}) collective-permute-start(bf16[136,768]{1,0:T(8,128)(2,1)S(1)} %collective-permute-done.2), channel_id=1, source_target_pairs={{0,16},{16,32},{32,48},{48,64},{64,80},{80,96},{96,112},{112,128},... | collective-permute-start | bytes 626696 | tf_op jit(solution)/shard_map/ppermute | solution.py:13
  72.8 1.8 %collective-permute-done.12 = bf16[136,768]{1,0:T(8,128)(2,1)S(1)} collective-permute-done((bf16[136,768]{1,0:T(8,128)(2,1)S(1)}, bf16[136,768]{1,0:T(8,128)(2,1)S(1)}, u32[]{:S(2)}, u32[]{:S(2)}) %collective-permute-start.12) | collective-permute-done | bytes 208928 | tf_op jit(solution)/shard_map/ppermute | solution.py:13
  74.6 1.9 %collective-permute-start.13 = (bf16[136,768]{1,0:T(8,128)(2,1)S(1)}, bf16[136,768]{1,0:T(8,128)(2,1)S(1)}, u32[]{:S(2)}, u32[]{:S(2)}) collective-permute-start(bf16[136,768]{1,0:T(8,128)(2,1)S(1)} %collective-permute-done.12), channel_id=1, source_target_pairs={{16,0},{32,16},{48,32},{64,48},{80,64},{96,80},{112,96},{128,112},... | collective-permute-start | bytes 626696 | tf_op jit(solution)/shard_map/ppermute | solution.py:13
  76.5 6.0 %collective-permute-start.4 = (bf16[136,768]{1,0:T(8,128)(2,1)S(1)}, bf16[136,768]{1,0:T(8,128)(2,1)S(1)}, u32[]{:S(2)}, u32[]{:S(2)}) collective-permute-start(bf16[136,768]{1,0:T(8,128)(2,1)S(1)} %collective-permute-done.3), channel_id=1, source_target_pairs={{0,16},{16,32},{32,48},{48,64},{64,80},{80,96},{96,112},{112,128},... | collective-permute-start | bytes 626696 | tf_op jit(solution)/shard_map/ppermute | solution.py:13
  82.6 1.8 %collective-permute-done.13 = bf16[136,768]{1,0:T(8,128)(2,1)S(1)} collective-permute-done((bf16[136,768]{1,0:T(8,128)(2,1)S(1)}, bf16[136,768]{1,0:T(8,128)(2,1)S(1)}, u32[]{:S(2)}, u32[]{:S(2)}) %collective-permute-start.13) | collective-permute-done | bytes 208928 | tf_op jit(solution)/shard_map/ppermute | solution.py:13
  84.4 1.9 %collective-permute-start.14 = (bf16[136,768]{1,0:T(8,128)(2,1)S(1)}, bf16[136,768]{1,0:T(8,128)(2,1)S(1)}, u32[]{:S(2)}, u32[]{:S(2)}) collective-permute-start(bf16[136,768]{1,0:T(8,128)(2,1)S(1)} %collective-permute-done.13), channel_id=1, source_target_pairs={{16,0},{32,16},{48,32},{64,48},{80,64},{96,80},{112,96},{128,112},... | collective-permute-start | bytes 626696 | tf_op jit(solution)/shard_map/ppermute | solution.py:13
  86.3 6.0 %collective-permute-start.5 = (bf16[136,768]{1,0:T(8,128)(2,1)S(1)}, bf16[136,768]{1,0:T(8,128)(2,1)S(1)}, u32[]{:S(2)}, u32[]{:S(2)}) collective-permute-start(bf16[136,768]{1,0:T(8,128)(2,1)S(1)} %collective-permute-done.4), channel_id=1, source_target_pairs={{0,16},{16,32},{32,48},{48,64},{64,80},{80,96},{96,112},{112,128},... | collective-permute-start | bytes 626696 | tf_op jit(solution)/shard_map/ppermute | solution.py:13
  92.4 1.8 %collective-permute-done.14 = bf16[136,768]{1,0:T(8,128)(2,1)S(1)} collective-permute-done((bf16[136,768]{1,0:T(8,128)(2,1)S(1)}, bf16[136,768]{1,0:T(8,128)(2,1)S(1)}, u32[]{:S(2)}, u32[]{:S(2)}) %collective-permute-start.14) | collective-permute-done | bytes 208928 | tf_op jit(solution)/shard_map/ppermute | solution.py:13
  94.2 1.9 %collective-permute-start.15 = (bf16[136,768]{1,0:T(8,128)(2,1)S(1)}, bf16[136,768]{1,0:T(8,128)(2,1)S(1)}, u32[]{:S(2)}, u32[]{:S(2)}) collective-permute-start(bf16[136,768]{1,0:T(8,128)(2,1)S(1)} %collective-permute-done.14), channel_id=1, source_target_pairs={{16,0},{32,16},{48,32},{64,48},{80,64},{96,80},{112,96},{128,112},... | collective-permute-start | bytes 626696 | tf_op jit(solution)/shard_map/ppermute | solution.py:13
  96.1 6.0 %collective-permute-start.6 = (bf16[136,768]{1,0:T(8,128)(2,1)S(1)}, bf16[136,768]{1,0:T(8,128)(2,1)}, u32[]{:S(2)}, u32[]{:S(2)}) collective-permute-start(bf16[136,768]{1,0:T(8,128)(2,1)S(1)} %collective-permute-done.5), channel_id=1, source_target_pairs={{0,16},{16,32},{32,48},{48,64},{64,80},{80,96},{96,112},{112,128},... | collective-permute-start | bytes 626696 | tf_op jit(solution)/shard_map/ppermute | solution.py:13
  102.2 2.2 %collective-permute-done.15 = bf16[136,768]{1,0:T(8,128)(2,1)S(1)} collective-permute-done((bf16[136,768]{1,0:T(8,128)(2,1)S(1)}, bf16[136,768]{1,0:T(8,128)(2,1)S(1)}, u32[]{:S(2)}, u32[]{:S(2)}) %collective-permute-start.15) | collective-permute-done | bytes 208928 | tf_op jit(solution)/shard_map/ppermute | solution.py:13
  104.4 1.9 %collective-permute-start.16 = (bf16[136,768]{1,0:T(8,128)(2,1)S(1)}, bf16[136,768]{1,0:T(8,128)(2,1)S(1)}, u32[]{:S(2)}, u32[]{:S(2)}) collective-permute-start(bf16[136,768]{1,0:T(8,128)(2,1)S(1)} %collective-permute-done.15), channel_id=1, source_target_pairs={{16,0},{32,16},{48,32},{64,48},{80,64},{96,80},{112,96},{128,112},... | collective-permute-start | bytes 626696 | tf_op jit(solution)/shard_map/ppermute | solution.py:13
  106.4 6.1 %collective-permute-start.7 = (bf16[136,768]{1,0:T(8,128)(2,1)}, bf16[136,768]{1,0:T(8,128)(2,1)}, u32[]{:S(2)}, u32[]{:S(2)}) collective-permute-start(bf16[136,768]{1,0:T(8,128)(2,1)} %collective-permute-done.6), channel_id=1, source_target_pairs={{0,16},{16,32},{32,48},{48,64},{64,80},{80,96},{96,112},{112,128},... | collective-permute-start | bytes 626696 | tf_op jit(solution)/shard_map/ppermute | solution.py:13
  112.5 1.0 bitcast_dynamic-update-slice_fusion.9
  113.5 0.8 collective-permute-done.16
  114.3 2.7 %fusion.12 = f32[8,256,512]{2,1,0:T(8,128)} fusion(bf16[8,136,768]{2,1,0:T(8,128)(2,1)S(1)} %bitcast_dynamic-update-slice_fusion), kind=kOutput, calls=%fused_computation.18 | convolution fusion | flops 268435456 | bytes 5767168 | tf_op jit(solution)/shard_map/kcd,kce->kde/dot_general | solution.py:65
  117.0 0.1 copy.251
  117.1 0.7 fusion.48
  123.0 3.3 %fusion.17 = f32[256,512]{1,0:T(8,128)S(1)} fusion(f32[8,256,512]{2,1,0:T(8,128)} %fusion.12, f32[]{:T(128)S(6)} %mul.307, f32[]{:T(128)S(6)} %mul.306, f32[]{:T(128)S(6)} %mul.305, f32[]{:T(128)S(6)} %mul.304, f32[]{:T(128)S(6)} %mul.303, f32[]{:T(128)S(6)} %mul.302, f32[]{:T(128)} %bitcast.44), kind=kLoop, calls=%fused_computation.24 | loop fusion | flops 1835008 | bytes 4718620 | tf_op jit(solution)/shard_map/add | solution.py:79
  126.3 11.7 %collective-permute-start.17 = (f32[256,512]{1,0:T(8,128)S(1)}, f32[256,512]{1,0:T(8,128)}, u32[]{:S(2)}, u32[]{:S(2)}) collective-permute-start(f32[256,512]{1,0:T(8,128)S(1)} %fusion.17), channel_id=1, source_target_pairs={{128,0},{144,16},{160,32},{176,48},{192,64},{208,80},{224,96},{240... | collective-permute-start | bytes 1572872 | tf_op jit(solution)/shard_map/ppermute | solution.py:13
  138.0 0.9 bitcast_dynamic-update-slice_fusion.8
  139.0 0.1 copy.250
  139.1 0.7 fusion.49
  144.8 0.7 fusion.14
  145.6 1.3 fusion.26
  146.9 1.9 %collective-permute-start.8 = (f32[256,512]{1,0:T(8,128)S(1)}, f32[256,512]{1,0:T(8,128)S(1)}, u32[]{:S(2)}, u32[]{:S(2)}) collective-permute-start(f32[256,512]{1,0:T(8,128)S(1)} %fusion.26), channel_id=1, source_target_pairs={{0,128},{16,144},{32,160},{48,176},{64,192},{80,208},{96,224},{112... | collective-permute-start | bytes 1572872 | tf_op jit(solution)/shard_map/ppermute | solution.py:13
  148.8 2.3 %add_convert_fusion = bf16[256,512]{1,0:T(8,128)(2,1)S(1)} fusion(f32[256,512]{1,0:T(8,128)} %collective-permute-done.17, f32[]{:T(128)S(6)} %mul.308, f32[8,256,512]{2,1,0:T(8,128)S(1)} %copy-done, f32[]{:T(128)S(6)} %mul.307, f32[]{:T(128)S(6)} %mul.306, f32[]{:T(128)S(6)} %mul.305, f32[]{:T(128)S(6)} %mul.304, f32[]{:T(128)S(6)} %mul.303, f32[]{:T(128)S(6)} %mul.302, ...), kind=kLoop, calls=%fused_computation.54 | loop fusion | flops 2228224 | bytes 4980768 | tf_op jit(solution)/shard_map/convert_element_type | solution.py:120
  151.1 0.9 fusion.8
  152.0 0.8 fusion.3
  152.9 6.3 %collective-permute-done.8 = f32[256,512]{1,0:T(8,128)S(1)} collective-permute-done((f32[256,512]{1,0:T(8,128)S(1)}, f32[256,512]{1,0:T(8,128)S(1)}, u32[]{:S(2)}, u32[]{:S(2)}) %collective-permute-start.8) | collective-permute-done | bytes 524320 | tf_op jit(solution)/shard_map/ppermute | solution.py:13
  159.2 1.2 add_convert_fusion.1
  160.4 0.2 fusion.7
  160.6 0.7 copy.241
  161.4 0.8 fusion.2
  (42 shorter events, 0.6 us)
Async XLA Ops:
  0.6 31.4 %copy-start.1 = (bf16[128,512]{1,0:T(8,128)(2,1)S(1)}, bf16[128,512]{1,0:T(8,128)(2,1)}, u32[]{:S(2)}) copy-start(bf16[128,512]{1,0:T(8,128)(2,1)} %param.13) | copy-start | bytes 393220
  2.3 29.6 %all-to-all-start = ((bf16[8,16,1024]{2,0,1:T(8,128)(2,1)}), bf16[8,16,1024]{2,0,1:T(8,128)(2,1)S(1)}, u32[]{:S(2)}, u32[]{:S(2)}) async-start(bf16[8,16,1024]{2,0,1:T(8,128)(2,1)} %pad_maximum_fusion), calls=%async_computation | async-start | bytes 524288 | tf_op jit(solution)/shard_map/all_to_all | solution.py:97
  32.9 11.5 %collective-permute-start.9 = (bf16[136,768]{1,0:T(8,128)(2,1)S(1)}, bf16[136,768]{1,0:T(8,128)(2,1)S(1)}, u32[]{:S(2)}, u32[]{:S(2)}) collective-permute-start(bf16[136,768]{1,0:T(8,128)(2,1)S(1)} %get-tuple-element.90), channel_id=1, source_target_pairs={{16,0},{32,16},{48,32},{64,48},{80,64},{96,80},{112,96},{128,112},... | collective-permute-start | bytes 626696 | tf_op jit(solution)/shard_map/ppermute | solution.py:13
  36.3 10.1 %collective-permute-start = (bf16[136,768]{1,0:T(8,128)(2,1)S(1)}, bf16[136,768]{1,0:T(8,128)(2,1)S(1)}, u32[]{:S(2)}, u32[]{:S(2)}) collective-permute-start(bf16[136,768]{1,0:T(8,128)(2,1)S(1)} %get-tuple-element.91), channel_id=1, source_target_pairs={{0,16},{16,32},{32,48},{48,64},{64,80},{80,96},{96,112},{112,128},... | collective-permute-start | bytes 626696 | tf_op jit(solution)/shard_map/ppermute | solution.py:13
  44.4 10.6 %collective-permute-start.10 = (bf16[136,768]{1,0:T(8,128)(2,1)S(1)}, bf16[136,768]{1,0:T(8,128)(2,1)S(1)}, u32[]{:S(2)}, u32[]{:S(2)}) collective-permute-start(bf16[136,768]{1,0:T(8,128)(2,1)S(1)} %collective-permute-done.9), channel_id=1, source_target_pairs={{16,0},{32,16},{48,32},{64,48},{80,64},{96,80},{112,96},{128,112},... | collective-permute-start | bytes 626696 | tf_op jit(solution)/shard_map/ppermute | solution.py:13
  46.3 10.6 %collective-permute-start.1 = (bf16[136,768]{1,0:T(8,128)(2,1)S(1)}, bf16[136,768]{1,0:T(8,128)(2,1)S(1)}, u32[]{:S(2)}, u32[]{:S(2)}) collective-permute-start(bf16[136,768]{1,0:T(8,128)(2,1)S(1)} %collective-permute-done), channel_id=1, source_target_pairs={{0,16},{16,32},{32,48},{48,64},{64,80},{80,96},{96,112},{112,128},... | collective-permute-start | bytes 626696 | tf_op jit(solution)/shard_map/ppermute | solution.py:13
  55.0 9.8 %collective-permute-start.11 = (bf16[136,768]{1,0:T(8,128)(2,1)S(1)}, bf16[136,768]{1,0:T(8,128)(2,1)S(1)}, u32[]{:S(2)}, u32[]{:S(2)}) collective-permute-start(bf16[136,768]{1,0:T(8,128)(2,1)S(1)} %collective-permute-done.10), channel_id=1, source_target_pairs={{16,0},{32,16},{48,32},{64,48},{80,64},{96,80},{112,96},{128,112},... | collective-permute-start | bytes 626696 | tf_op jit(solution)/shard_map/ppermute | solution.py:13
  57.0 9.8 %collective-permute-start.2 = (bf16[136,768]{1,0:T(8,128)(2,1)S(1)}, bf16[136,768]{1,0:T(8,128)(2,1)S(1)}, u32[]{:S(2)}, u32[]{:S(2)}) collective-permute-start(bf16[136,768]{1,0:T(8,128)(2,1)S(1)} %collective-permute-done.1), channel_id=1, source_target_pairs={{0,16},{16,32},{32,48},{48,64},{64,80},{80,96},{96,112},{112,128},... | collective-permute-start | bytes 626696 | tf_op jit(solution)/shard_map/ppermute | solution.py:13
  64.8 9.8 %collective-permute-start.12 = (bf16[136,768]{1,0:T(8,128)(2,1)S(1)}, bf16[136,768]{1,0:T(8,128)(2,1)S(1)}, u32[]{:S(2)}, u32[]{:S(2)}) collective-permute-start(bf16[136,768]{1,0:T(8,128)(2,1)S(1)} %collective-permute-done.11), channel_id=1, source_target_pairs={{16,0},{32,16},{48,32},{64,48},{80,64},{96,80},{112,96},{128,112},... | collective-permute-start | bytes 626696 | tf_op jit(solution)/shard_map/ppermute | solution.py:13
  66.7 9.8 %collective-permute-start.3 = (bf16[136,768]{1,0:T(8,128)(2,1)S(1)}, bf16[136,768]{1,0:T(8,128)(2,1)S(1)}, u32[]{:S(2)}, u32[]{:S(2)}) collective-permute-start(bf16[136,768]{1,0:T(8,128)(2,1)S(1)} %collective-permute-done.2), channel_id=1, source_target_pairs={{0,16},{16,32},{32,48},{48,64},{64,80},{80,96},{96,112},{112,128},... | collective-permute-start | bytes 626696 | tf_op jit(solution)/shard_map/ppermute | solution.py:13
  74.6 9.8 %collective-permute-start.13 = (bf16[136,768]{1,0:T(8,128)(2,1)S(1)}, bf16[136,768]{1,0:T(8,128)(2,1)S(1)}, u32[]{:S(2)}, u32[]{:S(2)}) collective-permute-start(bf16[136,768]{1,0:T(8,128)(2,1)S(1)} %collective-permute-done.12), channel_id=1, source_target_pairs={{16,0},{32,16},{48,32},{64,48},{80,64},{96,80},{112,96},{128,112},... | collective-permute-start | bytes 626696 | tf_op jit(solution)/shard_map/ppermute | solution.py:13
  76.5 9.8 %collective-permute-start.4 = (bf16[136,768]{1,0:T(8,128)(2,1)S(1)}, bf16[136,768]{1,0:T(8,128)(2,1)S(1)}, u32[]{:S(2)}, u32[]{:S(2)}) collective-permute-start(bf16[136,768]{1,0:T(8,128)(2,1)S(1)} %collective-permute-done.3), channel_id=1, source_target_pairs={{0,16},{16,32},{32,48},{48,64},{64,80},{80,96},{96,112},{112,128},... | collective-permute-start | bytes 626696 | tf_op jit(solution)/shard_map/ppermute | solution.py:13
  84.4 9.8 %collective-permute-start.14 = (bf16[136,768]{1,0:T(8,128)(2,1)S(1)}, bf16[136,768]{1,0:T(8,128)(2,1)S(1)}, u32[]{:S(2)}, u32[]{:S(2)}) collective-permute-start(bf16[136,768]{1,0:T(8,128)(2,1)S(1)} %collective-permute-done.13), channel_id=1, source_target_pairs={{16,0},{32,16},{48,32},{64,48},{80,64},{96,80},{112,96},{128,112},... | collective-permute-start | bytes 626696 | tf_op jit(solution)/shard_map/ppermute | solution.py:13
  86.3 9.8 %collective-permute-start.5 = (bf16[136,768]{1,0:T(8,128)(2,1)S(1)}, bf16[136,768]{1,0:T(8,128)(2,1)S(1)}, u32[]{:S(2)}, u32[]{:S(2)}) collective-permute-start(bf16[136,768]{1,0:T(8,128)(2,1)S(1)} %collective-permute-done.4), channel_id=1, source_target_pairs={{0,16},{16,32},{32,48},{48,64},{64,80},{80,96},{96,112},{112,128},... | collective-permute-start | bytes 626696 | tf_op jit(solution)/shard_map/ppermute | solution.py:13
  94.2 10.3 %collective-permute-start.15 = (bf16[136,768]{1,0:T(8,128)(2,1)S(1)}, bf16[136,768]{1,0:T(8,128)(2,1)S(1)}, u32[]{:S(2)}, u32[]{:S(2)}) collective-permute-start(bf16[136,768]{1,0:T(8,128)(2,1)S(1)} %collective-permute-done.14), channel_id=1, source_target_pairs={{16,0},{32,16},{48,32},{64,48},{80,64},{96,80},{112,96},{128,112},... | collective-permute-start | bytes 626696 | tf_op jit(solution)/shard_map/ppermute | solution.py:13
  96.1 10.3 %collective-permute-start.6 = (bf16[136,768]{1,0:T(8,128)(2,1)S(1)}, bf16[136,768]{1,0:T(8,128)(2,1)}, u32[]{:S(2)}, u32[]{:S(2)}) collective-permute-start(bf16[136,768]{1,0:T(8,128)(2,1)S(1)} %collective-permute-done.5), channel_id=1, source_target_pairs={{0,16},{16,32},{32,48},{48,64},{64,80},{80,96},{96,112},{112,128},... | collective-permute-start | bytes 626696 | tf_op jit(solution)/shard_map/ppermute | solution.py:13
  104.4 9.8 %collective-permute-start.16 = (bf16[136,768]{1,0:T(8,128)(2,1)S(1)}, bf16[136,768]{1,0:T(8,128)(2,1)S(1)}, u32[]{:S(2)}, u32[]{:S(2)}) collective-permute-start(bf16[136,768]{1,0:T(8,128)(2,1)S(1)} %collective-permute-done.15), channel_id=1, source_target_pairs={{16,0},{32,16},{48,32},{64,48},{80,64},{96,80},{112,96},{128,112},... | collective-permute-start | bytes 626696 | tf_op jit(solution)/shard_map/ppermute | solution.py:13
  106.4 31.6 %collective-permute-start.7 = (bf16[136,768]{1,0:T(8,128)(2,1)}, bf16[136,768]{1,0:T(8,128)(2,1)}, u32[]{:S(2)}, u32[]{:S(2)}) collective-permute-start(bf16[136,768]{1,0:T(8,128)(2,1)} %collective-permute-done.6), channel_id=1, source_target_pairs={{0,16},{16,32},{32,48},{48,64},{64,80},{80,96},{96,112},{112,128},... | collective-permute-start | bytes 626696 | tf_op jit(solution)/shard_map/ppermute | solution.py:13
  126.3 22.5 %collective-permute-start.17 = (f32[256,512]{1,0:T(8,128)S(1)}, f32[256,512]{1,0:T(8,128)}, u32[]{:S(2)}, u32[]{:S(2)}) collective-permute-start(f32[256,512]{1,0:T(8,128)S(1)} %fusion.17), channel_id=1, source_target_pairs={{128,0},{144,16},{160,32},{176,48},{192,64},{208,80},{224,96},{240... | collective-permute-start | bytes 1572872 | tf_op jit(solution)/shard_map/ppermute | solution.py:13
  145.6 3.3 %copy-start = (f32[8,256,512]{2,1,0:T(8,128)S(1)}, f32[8,256,512]{2,1,0:T(8,128)}, u32[]{:S(2)}) copy-start(f32[8,256,512]{2,1,0:T(8,128)} %fusion.12) | copy-start | bytes 12582916
  146.9 12.3 %collective-permute-start.8 = (f32[256,512]{1,0:T(8,128)S(1)}, f32[256,512]{1,0:T(8,128)S(1)}, u32[]{:S(2)}, u32[]{:S(2)}) collective-permute-start(f32[256,512]{1,0:T(8,128)S(1)} %fusion.26), channel_id=1, source_target_pairs={{0,128},{16,144},{32,160},{48,176},{64,192},{80,208},{96,224},{112... | collective-permute-start | bytes 1572872 | tf_op jit(solution)/shard_map/ppermute | solution.py:13

commit v6 on v4

--- a/solution.py
+++ b/solution.py
@@ -1,7 +1,7 @@
 import jax
 import jax.numpy as jnp
 from jax import lax
-from jax.sharding import PartitionSpec as P
+from jax.sharding import Mesh, PartitionSpec as P
 
 BLOCK = 128
 WINDOW_BLOCKS = 16
@@ -49,34 +49,84 @@
     return jnp.stack([high, middle, rest - middle])
 
 
-def relayed_partial(left, right, own_decay, direction):
-    rows = left.shape[0]
-    split = left.shape[1]
-    cols = split + right.shape[1]
+def coded_bundle(left, right, own_decay):
+    cols = left.shape[1] + right.shape[1]
     parts = jnp.zeros((GAIN_ROWS, cols), jnp.float32).at[:3, :].set(pieces_of(own_decay)[:, None])
-    moving = jnp.concatenate(
+    return jnp.concatenate(
         [jnp.concatenate([left, right], axis=1), parts.astype(jnp.bfloat16)], axis=0
     )
-    acc = None
-    gain = None
-    for _ in range(RELAY_BLOCKS):
-        moving = passed_along(moving, "ctx", direction)
-        update = jnp.einsum(
+
+
+def row_updates(bundles, which, rows, split):
+    updates = [
+        jnp.einsum(
             "cd,ce->de",
-            moving[:rows, :split],
-            moving[:rows, split:],
+            bundles[k, which, :rows, :split],
+            bundles[k, which, :rows, split:],
             preferred_element_type=jnp.float32,
         )
-        coded = moving[rows : rows + 3, 0].astype(jnp.float32)
-        decay = (coded[0] + coded[1]) + coded[2]
-        if acc is None:
-            acc = update
-            gain = decay
-        else:
-            acc = acc + gain * update
-            gain = gain * decay
-    joined = passed_along(acc, "ctx", direction * RELAY_BLOCKS)
-    return gain * joined + acc
+        for k in range(bundles.shape[0])
+    ]
+    coded = bundles[:, 0, rows : rows + 3, 0].astype(jnp.float32)
+    decays = (coded[:, 0] + coded[:, 1]) + coded[:, 2]
+    return updates, decays
+
+
+def shift_x(block, distance):
+    return passed_along(block, "cx", distance)
+
+
+def weighted_sum(weights, updates):
+    total = weights[0] * updates[0]
+    for k in range(1, len(updates)):
+        total = total + weights[k] * updates[k]
+    return total
+
+
+def forward_states(updates, decays, y):
+    count = len(updates)
+    w_pre = [None] * count
+    w_suf = [None] * count
+    run_pre = jnp.float32(1.0)
+    run_suf = jnp.float32(1.0)
+    for c in range(count - 1, -1, -1):
+        before = c < y
+        w_pre[c] = jnp.where(before, run_pre, 0.0)
+        w_suf[c] = jnp.where(before, 0.0, run_suf)
+        run_pre = run_pre * jnp.where(before, decays[c], 1.0)
+        run_suf = run_suf * jnp.where(before, 1.0, decays[c])
+    pre = weighted_sum(w_pre, updates)
+    suf = weighted_sum(w_suf, updates)
+    gain_pre = run_pre
+    gain_suf = run_suf
+    gain_row = gain_pre * gain_suf
+    row = gain_suf * pre + suf
+    from_two_back = shift_x(suf, 1)
+    through = shift_x(gain_row * from_two_back + row, 1)
+    return gain_pre * through + pre
+
+
+def backward_states(updates, decays, y):
+    count = len(updates)
+    w_pre = [None] * count
+    w_suf = [None] * count
+    run_pre = jnp.float32(1.0)
+    run_suf = jnp.float32(1.0)
+    for c in range(count):
+        after = c > y
+        w_pre[c] = jnp.where(after, 0.0, run_pre)
+        w_suf[c] = jnp.where(after, run_suf, 0.0)
+        run_pre = run_pre * jnp.where(after, 1.0, decays[c])
+        run_suf = run_suf * jnp.where(after, decays[c], 1.0)
+    pre = weighted_sum(w_pre, updates)
+    suf = weighted_sum(w_suf, updates)
+    gain_pre = run_pre
+    gain_suf = run_suf
+    gain_row = gain_pre * gain_suf
+    row = pre + gain_pre * suf
+    from_two_ahead = shift_x(pre, -1)
+    through = shift_x(row + gain_row * from_two_ahead, -1)
+    return suf + gain_suf * through
 
 
 def per_device(queries, keys, values, grad_out, log_decay, doc_lengths):
@@ -99,7 +149,7 @@
     tok_dev = key_rows.shape[0]
     block_count = tok_dev // BLOCK
     score_scaling = (key_dim * BLOCK) ** (-0.5)
-    me = lax.axis_index("ctx")
+    me = lax.axis_index("cx") * lax.axis_size("cy") + lax.axis_index("cy")
     doc_ids = document_ids(doc_lengths, me * tok_dev, tok_dev)
     weights, per_head_decay_rate, tail_decay, block_decay = decay_tables(
         log_decay[0], doc_ids, BLOCK, score_scaling
@@ -112,8 +162,14 @@
     queried = (query_block_list * (per_head_decay_rate * score_scaling)[:, :, None]).astype(
         jnp.bfloat16
     )
-    states = relayed_partial(keyed_blocks[0], value_block_list[0], block_decay[0], 1)[None]
-    ends = relayed_partial(queried[0], gradient_block_list[0], block_decay[0], -1)[None]
+    forward_bundle = coded_bundle(keyed_blocks[0], value_block_list[0], block_decay[0])
+    backward_bundle = coded_bundle(queried[0], gradient_block_list[0], block_decay[0])
+    row_bundles = lax.all_gather(jnp.stack([forward_bundle, backward_bundle]), "cy")
+    y = lax.axis_index("cy")
+    forward_updates, row_decays = row_updates(row_bundles, 0, BLOCK, key_dim)
+    backward_updates, _ = row_updates(row_bundles, 1, BLOCK, key_dim)
+    states = forward_states(forward_updates, row_decays, y)[None]
+    ends = backward_states(backward_updates, row_decays, y)[None]
     lowered_state = states.astype(jnp.bfloat16)
     back_low = ends.astype(jnp.bfloat16)
     scores = jnp.einsum(
@@ -165,18 +221,25 @@
 
 
 def solution(mesh):
+    ctx_size = mesh.shape["ctx"]
+    row_len = 8 if ctx_size % 8 == 0 else 1
+    grid = Mesh(
+        mesh.devices.reshape(ctx_size // row_len, row_len, mesh.shape["head"]),
+        ("cx", "cy", "head"),
+    )
+    ctx = ("cx", "cy")
     placed = (
-        P(("ctx", "head"), None),
-        P(("ctx", "head"), None),
-        P(("ctx", "head"), None),
-        P("ctx", "head"),
-        P("head", "ctx"),
+        P(ctx + ("head",), None),
+        P(ctx + ("head",), None),
+        P(ctx + ("head",), None),
+        P(ctx, "head"),
+        P("head", ctx),
         P(),
     )
     return jax.shard_map(
         per_device,
-        mesh=mesh,
+        mesh=grid,
         in_specs=placed,
-        out_specs=(P("ctx", "head"), P("ctx", "head"), P("ctx", "head"), P("ctx", "head")),
+        out_specs=(P(ctx, "head"), P(ctx, "head"), P(ctx, "head"), P(ctx, "head")),
         check_vma=False,
     )

time: 194 us -> 188 us (0.969)
  the two profiles are of different devices: /device:TPU:6 before, /device:TPU:8 now
where the time goes in v6:
time: 188 us; the launch traced here: 187 us
  waiting for transfers between devices  63.1 us (34%)
  between operations  38.9 us (21%)
  matrix products  34.6 us (18%)
  starting transfers between devices  28.6 us (15%)
  other arithmetic  15.9 us (8%)
  local copies, waits for them, and re-layouts  6.2 us (3%)
    all_gather x1, waiting for transfers between devices, per_device(): lax.all_gather(jnp.stack([forward_bundle, backward_bundle]), 'cy')  50.6 us
    dot_general x16, matrix products, row_updates(): jnp.einsum('cd,ce->de', bundles[k, which, :rows, :split], bundles[k, whic...  27.9 us
    all_to_all x1, starting transfers between devices, per_device(): lax.all_to_all(packed, 'head', split_axis=1, concat_axis=0, tiled=True)  16.8 us
    ppermute x4, waiting for transfers between devices, passed_along(): return lax.ppermute(block, axis, route)  12.5 us
    ppermute x4, starting transfers between devices, passed_along(): return lax.ppermute(block, axis, route)  11.8 us
    add x1, other arithmetic, backward_states(): through = shift_x(row + gain_row * from_two_ahead, -1)  4.07 us
  transfers between devices with their start and end apart: 6, of which 4 were waited for; matrix products, arithmetic and copies ran while one was open for 13% of the time, Pallas kernels for 0%

profile of v6, /device:TPU:8, one launch (start us, length us, event | category | flops | bytes accessed | tf_op | source)
XLA Modules:
  0.0 187.2 jit_solution(13575131493181104859)
XLA Ops:
  7.2 1.7 pad_maximum_fusion.1
  8.9 16.8 %all-to-all-start = ((bf16[8,16,1024]{2,0,1:T(8,128)(2,1)}), bf16[8,16,1024]{2,0,1:T(8,128)(2,1)S(1)}, u32[]{:S(2)}, u32[]{:S(2)}) async-start(bf16[8,16,1024]{2,0,1:T(8,128)(2,1)} %pad_maximum_fusion.1), calls=%async_computation | async-start | bytes 524288 | tf_op jit(solution)/shard_map/all_to_all | solution.py:145
  25.7 0.0 all-gather.3.cloned.1.call-start
  25.7 0.7 copy.25
  26.5 0.1 reduce-window.9
  26.5 0.1 reduce.3
  26.6 0.7 sub.43
  27.3 0.1 convert_reduce_fusion
  27.4 0.5 slice.222
  27.9 0.7 compare_bitcast_fusion
  28.6 0.6 slice.223
  29.2 1.0 reduce_window_sum.20
  30.2 0.6 slice.220
  35.7 0.1 slice_bitcast_fusion.64
  35.8 0.6 slice.219
  36.4 0.1 select_maximum_fusion
  36.5 2.0 %compare_select_fusion = (f32[128]{0:T(128)S(1)}, f32[128]{0:T(128)S(1)}) fusion(f32[]{:T(128)} %bitcast.9, s32[]{:T(128)} %bitcast.8, f32[1,128]{1,0:T(1,128)S(1)} %reduce_window_sum.20, s32[129]{0:T(256)S(1)} %broadcast_add_fusion, s32[]{:T(128)} %bitcast.11), kind=kLoop, calls=%fused_computation.92 | loop fusion | flops 768 | bytes 2060 | tf_op jit(solution)/shard_map/mul | solution.py:37
  38.5 0.1 multiply_convert_fusion.1
  38.6 1.0 maximum_bitcast_fusion
  39.7 0.8 pad_maximum_fusion
  40.4 0.0 all-gather.3.cloned.1.call-update
  40.5 0.2 fusion.10
  40.7 0.2 fusion.11
  40.9 0.9 fusion.33
  41.7 0.9 fusion.43
  42.7 0.9 fusion.40
  43.5 50.6 %all-gather.3.cloned.1.call-done = bf16[16,136,768]{2,1,0:T(8,128)(2,1)} async-done(((bf16[2,136,768]{2,1,0:T(8,128)(2,1)}), bf16[16,136,768]{2,1,0:T(8,128)(2,1)}) %all-gather.3.cloned.1.call-update) | async-done | bytes 3342352 | tf_op jit(solution)/shard_map/all_gather | solution.py:167
  94.1 0.7 slice.271
  94.9 0.1 copy.32
  95.0 0.7 fusion.42
  105.4 2.0 %fusion.13 = f32[256,512]{1,0:T(8,128)} fusion(bf16[8,2,136,768]{3,2,1,0:T(8,128)(2,1)} %bitcast.175), kind=kOutput, calls=%fused_computation.33 | convolution fusion | flops 33554432 | bytes 720896 | tf_op jit(solution)/shard_map/cd,ce->de/dot_general | solution.py:62
  107.3 2.0 %fusion.14 = f32[256,512]{1,0:T(8,128)} fusion(bf16[8,2,136,768]{3,2,1,0:T(8,128)(2,1)} %bitcast.176), kind=kOutput, calls=%fused_computation.35 | convolution fusion | flops 33554432 | bytes 720896 | tf_op jit(solution)/shard_map/cd,ce->de/dot_general | solution.py:62
  109.3 2.0 %fusion.15 = f32[256,512]{1,0:T(8,128)} fusion(bf16[8,2,136,768]{3,2,1,0:T(8,128)(2,1)} %bitcast.177), kind=kOutput, calls=%fused_computation.37 | convolution fusion | flops 33554432 | bytes 720896 | tf_op jit(solution)/shard_map/cd,ce->de/dot_general | solution.py:62
  111.3 2.0 %fusion.16 = f32[256,512]{1,0:T(8,128)} fusion(bf16[8,2,136,768]{3,2,1,0:T(8,128)(2,1)} %bitcast.178), kind=kOutput, calls=%fused_computation.39 | convolution fusion | flops 33554432 | bytes 720896 | tf_op jit(solution)/shard_map/cd,ce->de/dot_general | solution.py:62
  113.3 2.0 %fusion.17 = f32[256,512]{1,0:T(8,128)} fusion(bf16[8,2,136,768]{3,2,1,0:T(8,128)(2,1)} %bitcast.179), kind=kOutput, calls=%fused_computation.41 | convolution fusion | flops 33554432 | bytes 720896 | tf_op jit(solution)/shard_map/cd,ce->de/dot_general | solution.py:62
  115.3 2.0 %fusion.18 = f32[256,512]{1,0:T(8,128)} fusion(bf16[8,2,136,768]{3,2,1,0:T(8,128)(2,1)} %bitcast.180), kind=kOutput, calls=%fused_computation.43 | convolution fusion | flops 33554432 | bytes 720896 | tf_op jit(solution)/shard_map/cd,ce->de/dot_general | solution.py:62
  117.3 2.0 %fusion.19 = f32[256,512]{1,0:T(8,128)} fusion(bf16[8,2,136,768]{3,2,1,0:T(8,128)(2,1)} %bitcast.181), kind=kOutput, calls=%fused_computation.45 | convolution fusion | flops 33554432 | bytes 720896 | tf_op jit(solution)/shard_map/cd,ce->de/dot_general | solution.py:62
  120.0 1.2 fusion.21
  121.2 1.2 fusion.22
  122.4 1.2 fusion.23
  123.6 1.2 fusion.24
  124.8 1.2 fusion.25
  126.0 1.2 fusion.26
  127.3 3.5 %multiply_add_fusion.1 = (f32[256,512]{1,0:T(8,128)}, f32[256,512]{1,0:T(8,128)}) fusion(f32[256,512]{1,0:T(8,128)} %fusion.13, f32[256,512]{1,0:T(8,128)} %fusion.14, f32[256,512]{1,0:T(8,128)} %fusion.15, f32[256,512]{1,0:T(8,128)} %fusion.16, f32[256,512]{1,0:T(8,128)} %fusion.17, f32[256,512]{1,0:T(8,128)} %fusion.18, f32[256,512]{1,0:T(8,128)} %fusion.19, ...), kind=kOutput, calls=%fused_computation.20 | convolution fusion | flops 35520512 | bytes 4915232 | tf_op jit(solution)/shard_map/cd,ce->de/dot_general | solution.py:62
  130.7 2.5 %collective-permute-start.2 = (f32[256,512]{1,0:T(8,128)}, f32[256,512]{1,0:T(8,128)}, u32[]{:S(2)}, u32[]{:S(2)}) collective-permute-start(f32[256,512]{1,0:T(8,128)} %get-tuple-element.62), channel_id=1, source_target_pairs={{128,0},{256,128},{384,256},{512,384},{640,512},{768,640},{896,768... | collective-permute-start | bytes 1572872 | tf_op jit(solution)/shard_map/ppermute | solution.py:13
  136.8 1.2 fusion.27
  138.0 0.8 copy-done
  138.8 2.2 %multiply_add_fusion.4 = (f32[256,512]{1,0:T(8,128)}, f32[256,512]{1,0:T(8,128)}) fusion(f32[256,512]{1,0:T(8,128)S(1)} %fusion.21, f32[256,512]{1,0:T(8,128)S(1)} %fusion.22, f32[256,512]{1,0:T(8,128)S(1)} %fusion.23, f32[256,512]{1,0:T(8,128)S(1)} %fusion.24, f32[256,512]{1,0:T(8,128)S(1)} %fusion.25, f32[256,512]{1,0:T(8,128)S(1)} %fusion.26, ...), kind=kOutput, calls=%fused_computation.25 | convolution fusion | flops 35520512 | bytes 4915232 | tf_op jit(solution)/shard_map/cd,ce->de/dot_general | solution.py:62
  141.0 3.3 %collective-permute-start = (f32[256,512]{1,0:T(8,128)}, f32[256,512]{1,0:T(8,128)}, u32[]{:S(2)}, u32[]{:S(2)}) collective-permute-start(f32[256,512]{1,0:T(8,128)} %get-tuple-element.60), channel_id=1, source_target_pairs={{0,128},{128,256},{256,384},{384,512},{512,640},{640,768},{768,896... | collective-permute-start | bytes 1572872 | tf_op jit(solution)/shard_map/ppermute | solution.py:13
  144.4 2.1 %collective-permute-done.2 = f32[256,512]{1,0:T(8,128)} collective-permute-done((f32[256,512]{1,0:T(8,128)}, f32[256,512]{1,0:T(8,128)}, u32[]{:S(2)}, u32[]{:S(2)}) %collective-permute-start.2) | collective-permute-done | bytes 524320 | tf_op jit(solution)/shard_map/ppermute | solution.py:13
  146.4 4.1 %multiply_add_fusion = (f32[256,512]{1,0:T(8,128)}, f32[256,512]{1,0:T(8,128)}) fusion(f32[256,512]{1,0:T(8,128)} %collective-permute-done.2, f32[256,512]{1,0:T(8,128)} %get-tuple-element.62, f32[]{:T(128)S(6)} %mul.531, f32[]{:T(128)S(6)} %mul.528, f32[256,512]{1,0:T(8,128)} %get-tuple-element.63, f32[]{:T(128)S(6)} %select_n.251, f32[256,512]{1,0:T(8,128)} %fusion.13, ...), kind=kLoop, calls=%fused_computation.19 | loop fusion | flops 2490368 | bytes 6291496 | tf_op jit(solution)/shard_map/add | solution.py:128
  150.5 3.7 %collective-permute-start.3 = (f32[256,512]{1,0:T(8,128)}, f32[256,512]{1,0:T(8,128)}, u32[]{:S(2)}, u32[]{:S(2)}) collective-permute-start(f32[256,512]{1,0:T(8,128)} %get-tuple-element.40), channel_id=1, source_target_pairs={{128,0},{256,128},{384,256},{512,384},{640,512},{768,640},{896,768... | collective-permute-start | bytes 1572872 | tf_op jit(solution)/shard_map/ppermute | solution.py:13
  154.2 0.9 fusion.30
  160.6 2.2 %add_add_fusion = (f32[256,512]{1,0:T(8,128)S(1)}, f32[256,512]{1,0:T(8,128)S(1)}) fusion(f32[256,512]{1,0:T(8,128)} %get-tuple-element.60, f32[256,512]{1,0:T(8,128)} %collective-permute-done, f32[]{:T(128)S(6)} %mul.434, f32[]{:T(128)S(6)} %mul.435, f32[256,512]{1,0:T(8,128)} %get-tuple-element.61, f32[]{:T(128)S(6)} %select_n.234, ...), kind=kLoop, calls=%fused_computation.23 | loop fusion | flops 2490368 | bytes 6291496 | tf_op jit(solution)/shard_map/add | solution.py:105
  162.9 2.3 %collective-permute-start.1 = (f32[256,512]{1,0:T(8,128)S(1)}, f32[256,512]{1,0:T(8,128)S(1)}, u32[]{:S(2)}, u32[]{:S(2)}) collective-permute-start(f32[256,512]{1,0:T(8,128)S(1)} %get-tuple-element.42), channel_id=1, source_target_pairs={{0,128},{128,256},{256,384},{384,512},{512,640},{640,768},{768,896... | collective-permute-start | bytes 1572872 | tf_op jit(solution)/shard_map/ppermute | solution.py:13
  165.2 0.2 collective-permute-done.3
  165.3 1.1 add_convert_fusion
  166.5 0.9 fusion.8
  167.4 0.8 fusion.3
  168.2 10.2 %collective-permute-done.1 = f32[256,512]{1,0:T(8,128)S(1)} collective-permute-done((f32[256,512]{1,0:T(8,128)S(1)}, f32[256,512]{1,0:T(8,128)S(1)}, u32[]{:S(2)}, u32[]{:S(2)}) %collective-permute-start.1) | collective-permute-done | bytes 524320 | tf_op jit(solution)/shard_map/ppermute | solution.py:13
  178.5 0.1 add_convert_fusion.1
  178.6 0.2 fusion.7
  178.8 0.7 copy.29
  179.5 0.8 fusion.2
  (25 shorter events, 0.1 us)
Async XLA Ops:
  7.2 33.5 %copy-start.2 = (bf16[128,512]{1,0:T(8,128)(2,1)S(1)}, bf16[128,512]{1,0:T(8,128)(2,1)}, u32[]{:S(2)}) copy-start(bf16[128,512]{1,0:T(8,128)(2,1)} %param.13) | copy-start | bytes 393220
  8.9 29.6 %all-to-all-start = ((bf16[8,16,1024]{2,0,1:T(8,128)(2,1)}), bf16[8,16,1024]{2,0,1:T(8,128)(2,1)S(1)}, u32[]{:S(2)}, u32[]{:S(2)}) async-start(bf16[8,16,1024]{2,0,1:T(8,128)(2,1)} %pad_maximum_fusion.1), calls=%async_computation | async-start | bytes 524288 | tf_op jit(solution)/shard_map/all_to_all | solution.py:145
  25.7 68.5 %all-gather.3.cloned.1.call-start = ((), (), s32[]{:S(2)}) async-start(), calls=%async_computation.1 | async-start | bytes 3760128 | tf_op jit(solution)/shard_map/all_gather | solution.py:167
  40.9 78.4 %copy-start.7 = (bf16[128,128]{1,0:T(8,128)(2,1)}, bf16[128,128]{1,0:T(8,128)(2,1)S(1)}, u32[]{:S(2)}) copy-start(bf16[128,128]{1,0:T(8,128)(2,1)S(1)} %fusion.11) | copy-start | bytes 98308
  130.7 15.7 %collective-permute-start.2 = (f32[256,512]{1,0:T(8,128)}, f32[256,512]{1,0:T(8,128)}, u32[]{:S(2)}, u32[]{:S(2)}) collective-permute-start(f32[256,512]{1,0:T(8,128)} %get-tuple-element.62), channel_id=1, source_target_pairs={{128,0},{256,128},{384,256},{512,384},{640,512},{768,640},{896,768... | collective-permute-start | bytes 1572872 | tf_op jit(solution)/shard_map/ppermute | solution.py:13
  138.0 0.8 copy-start
  141.0 19.6 %collective-permute-start = (f32[256,512]{1,0:T(8,128)}, f32[256,512]{1,0:T(8,128)}, u32[]{:S(2)}, u32[]{:S(2)}) collective-permute-start(f32[256,512]{1,0:T(8,128)} %get-tuple-element.60), channel_id=1, source_target_pairs={{0,128},{128,256},{256,384},{384,512},{512,640},{640,768},{768,896... | collective-permute-start | bytes 1572872 | tf_op jit(solution)/shard_map/ppermute | solution.py:13
  144.3 9.8 %copy-start.8 = (bf16[128,128]{1,0:T(8,128)(2,1)S(1)}, bf16[128,128]{1,0:T(8,128)(2,1)}, u32[]{:S(2)}) copy-start(bf16[128,128]{1,0:T(8,128)(2,1)} %copy-done.7) | copy-start | bytes 98308
  150.5 14.8 %collective-permute-start.3 = (f32[256,512]{1,0:T(8,128)}, f32[256,512]{1,0:T(8,128)}, u32[]{:S(2)}, u32[]{:S(2)}) collective-permute-start(f32[256,512]{1,0:T(8,128)} %get-tuple-element.40), channel_id=1, source_target_pairs={{128,0},{256,128},{384,256},{512,384},{640,512},{768,640},{896,768... | collective-permute-start | bytes 1572872 | tf_op jit(solution)/shard_map/ppermute | solution.py:13
  160.6 4.8 %copy-start.1 = (f32[256,512]{1,0:T(8,128)S(1)}, f32[256,512]{1,0:T(8,128)}, u32[]{:S(2)}) copy-start(f32[256,512]{1,0:T(8,128)} %get-tuple-element.41) | copy-start | bytes 1572868
  160.6 5.9 %copy-start.5 = (f32[128,256]{1,0:T(8,128)S(1)}, f32[128,256]{1,0:T(8,128)}, u32[]{:S(2)}) copy-start(f32[128,256]{1,0:T(8,128)} %fusion.33) | copy-start | bytes 393220
  160.6 6.7 %copy-start.4 = (f32[128,512]{1,0:T(8,128)S(1)}, f32[128,512]{1,0:T(8,128)}, u32[]{:S(2)}) copy-start(f32[128,512]{1,0:T(8,128)} %fusion.43) | copy-start | bytes 786436
  162.9 15.7 %copy-start.6 = (f32[128,256]{0,1:T(8,128)S(1)}, f32[128,256]{0,1:T(8,128)}, u32[]{:S(2)}) copy-start(f32[128,256]{0,1:T(8,128)} %fusion.30) | copy-start | bytes 393220
  162.9 16.7 %copy-start.3 = (f32[128,512]{1,0:T(8,128)S(1)}, f32[128,512]{1,0:T(8,128)}, u32[]{:S(2)}) copy-start(f32[128,512]{1,0:T(8,128)} %fusion.40) | copy-start | bytes 786436
  162.9 15.6 %collective-permute-start.1 = (f32[256,512]{1,0:T(8,128)S(1)}, f32[256,512]{1,0:T(8,128)S(1)}, u32[]{:S(2)}, u32[]{:S(2)}) collective-permute-start(f32[256,512]{1,0:T(8,128)S(1)} %get-tuple-element.42), channel_id=1, source_target_pairs={{0,128},{128,256},{256,384},{384,512},{512,640},{640,768},{768,896... | collective-permute-start | bytes 1572872 | tf_op jit(solution)/shard_map/ppermute | solution.py:13
Sparse Core Ops, SparseCore 0:
  40.6 53.5 all-gather.2

commit v7 on v5

--- a/solution.py
+++ b/solution.py
@@ -40,6 +40,7 @@
 
 RELAY_BLOCKS = WINDOW_BLOCKS // 2
 GAIN_ROWS = 8
+DIRECT_BLOCKS = 2
 
 
 def pieces_of(decay):
@@ -58,9 +59,12 @@
         [jnp.concatenate([left, right], axis=1), parts.astype(jnp.bfloat16)], axis=0
     )
     received = []
-    for _ in range(RELAY_BLOCKS):
+    own = moving
+    for _ in range(RELAY_BLOCKS - DIRECT_BLOCKS):
         moving = passed_along(moving, "ctx", direction)
         received.append(moving)
+    for k in range(RELAY_BLOCKS - DIRECT_BLOCKS + 1, RELAY_BLOCKS + 1):
+        received.append(passed_along(own, "ctx", direction * k))
     stacked = jnp.stack(received)
     updates = jnp.einsum(
         "kcd,kce->kde",

time: 163 us -> 185 us (1.13)
  the two profiles are of different devices: /device:TPU:120 before, /device:TPU:104 now
where the time goes in v7:
time: 185 us; the launch traced here: 184 us
  starting transfers between devices  86.3 us (47%)
  waiting for transfers between devices  49.5 us (27%)
  between operations  16.2 us (9%)
  other arithmetic  15.3 us (8%)
  local copies, waits for them, and re-layouts  9.42 us (5%)
  matrix products  7.38 us (4%)
    ppermute x18, starting transfers between devices, passed_along(): return lax.ppermute(block, axis, route)  69.5 us
    ppermute x18, waiting for transfers between devices, passed_along(): return lax.ppermute(block, axis, route)  49.5 us
    all_to_all x1, starting transfers between devices, per_device(): lax.all_to_all(packed, 'head', split_axis=1, concat_axis=0, tiled=True)  16.8 us
    add x2, other arithmetic, relayed_partial(): acc = acc + weights[k] * updates[k]  4.52 us
    unnamed x23, local copies, waits for them, and re-layouts  3.98 us
  transfers between devices with their start and end apart: 19, of which 10 were waited for; matrix products, arithmetic and copies ran while one was open for 14% of the time, Pallas kernels for 0%

profile of v7, /device:TPU:104, one launch (start us, length us, event | category | flops | bytes accessed | tf_op | source)
XLA Modules:
  0.0 184.1 jit_solution(18213435985513299263)
XLA Ops:
  0.6 1.7 pad_maximum_fusion
  2.3 16.8 %all-to-all-start = ((bf16[8,16,1024]{2,0,1:T(8,128)(2,1)}), bf16[8,16,1024]{2,0,1:T(8,128)(2,1)S(1)}, u32[]{:S(2)}, u32[]{:S(2)}) async-start(bf16[8,16,1024]{2,0,1:T(8,128)(2,1)} %pad_maximum_fusion), calls=%async_computation | async-start | bytes 524288 | tf_op jit(solution)/shard_map/all_to_all | solution.py:101
  19.1 0.7 copy.234
  19.9 0.1 reduce.3
  20.0 0.7 sub.43
  20.8 0.5 slice.206
  21.3 0.7 compare_bitcast_fusion
  22.0 0.6 slice.207
  22.6 1.0 reduce_window_sum.20
  23.6 0.6 slice.204
  29.2 0.6 slice.203
  29.9 2.0 %fusion.43 = (f32[128]{0:T(128)S(1)}, f32[128]{0:T(128)S(1)}) fusion(s32[]{:T(128)} %bitcast.11, f32[1,128]{1,0:T(1,128)S(1)} %reduce_window_sum.20, s32[129]{0:T(256)S(1)} %broadcast_add_fusion, f32[]{:T(128)} %bitcast.9, s32[]{:T(128)} %bitcast.8), kind=kLoop, calls=%fused_computation.97 | loop fusion | flops 768 | bytes 2060 | tf_op jit(solution)/shard_map/mul | solution.py:133
  32.0 0.8 maximum_maximum_fusion.1
  32.9 3.1 %collective-permute-start.9 = (bf16[136,768]{1,0:T(8,128)(2,1)S(1)}, bf16[136,768]{1,0:T(8,128)(2,1)S(1)}, u32[]{:S(2)}, u32[]{:S(2)}) collective-permute-start(bf16[136,768]{1,0:T(8,128)(2,1)S(1)} %get-tuple-element.90), channel_id=1, source_target_pairs={{16,0},{32,16},{48,32},{64,48},{80,64},{96,80},{112,96},{128,112},... | collective-permute-start | bytes 626696 | tf_op jit(solution)/shard_map/ppermute | solution.py:13
  36.0 2.7 %collective-permute-start.15 = (bf16[136,768]{1,0:T(8,128)(2,1)S(1)}, bf16[136,768]{1,0:T(8,128)(2,1)S(1)}, u32[]{:S(2)}, u32[]{:S(2)}) collective-permute-start(bf16[136,768]{1,0:T(8,128)(2,1)S(1)} %get-tuple-element.90), channel_id=1, source_target_pairs={{112,0},{128,16},{144,32},{160,48},{176,64},{192,80},{208,96},{224... | collective-permute-start | bytes 626696 | tf_op jit(solution)/shard_map/ppermute | solution.py:13
  38.7 2.4 %collective-permute-start.16 = (bf16[136,768]{1,0:T(8,128)(2,1)S(1)}, bf16[136,768]{1,0:T(8,128)(2,1)S(1)}, u32[]{:S(2)}, u32[]{:S(2)}) collective-permute-start(bf16[136,768]{1,0:T(8,128)(2,1)S(1)} %get-tuple-element.90), channel_id=1, source_target_pairs={{128,0},{144,16},{160,32},{176,48},{192,64},{208,80},{224,96},{240... | collective-permute-start | bytes 626696 | tf_op jit(solution)/shard_map/ppermute | solution.py:13
  41.1 0.2 fusion.10
  41.3 0.2 fusion.11
  41.5 3.9 %collective-permute-start = (bf16[136,768]{1,0:T(8,128)(2,1)}, bf16[136,768]{1,0:T(8,128)(2,1)S(1)}, u32[]{:S(2)}, u32[]{:S(2)}) collective-permute-start(bf16[136,768]{1,0:T(8,128)(2,1)} %get-tuple-element.91), channel_id=1, source_target_pairs={{0,16},{16,32},{32,48},{48,64},{64,80},{80,96},{96,112},{112,128},... | collective-permute-start | bytes 626696 | tf_op jit(solution)/shard_map/ppermute | solution.py:13
  45.4 2.9 %collective-permute-start.6 = (bf16[136,768]{1,0:T(8,128)(2,1)}, bf16[136,768]{1,0:T(8,128)(2,1)}, u32[]{:S(2)}, u32[]{:S(2)}) collective-permute-start(bf16[136,768]{1,0:T(8,128)(2,1)} %get-tuple-element.91), channel_id=1, source_target_pairs={{0,112},{16,128},{32,144},{48,160},{64,176},{80,192},{96,208},{112... | collective-permute-start | bytes 626696 | tf_op jit(solution)/shard_map/ppermute | solution.py:13
  48.3 0.2 fusion.50
  48.5 0.2 fusion.46
  48.7 0.2 fusion.39
  48.9 0.2 fusion.36
  49.1 3.4 %collective-permute-start.7 = (bf16[136,768]{1,0:T(8,128)(2,1)}, bf16[136,768]{1,0:T(8,128)(2,1)}, u32[]{:S(2)}, u32[]{:S(2)}) collective-permute-start(bf16[136,768]{1,0:T(8,128)(2,1)} %get-tuple-element.91), channel_id=1, source_target_pairs={{0,128},{16,144},{32,160},{48,176},{64,192},{80,208},{96,224},{112... | collective-permute-start | bytes 626696 | tf_op jit(solution)/shard_map/ppermute | solution.py:13
  52.5 3.1 %collective-permute-start.10 = (bf16[136,768]{1,0:T(8,128)(2,1)S(1)}, bf16[136,768]{1,0:T(8,128)(2,1)S(1)}, u32[]{:S(2)}, u32[]{:S(2)}) collective-permute-start(bf16[136,768]{1,0:T(8,128)(2,1)S(1)} %collective-permute-done.9), channel_id=1, source_target_pairs={{16,0},{32,16},{48,32},{64,48},{80,64},{96,80},{112,96},{128,112},... | collective-permute-start | bytes 626696 | tf_op jit(solution)/shard_map/ppermute | solution.py:13
  55.7 5.9 %collective-permute-done.10 = bf16[136,768]{1,0:T(8,128)(2,1)S(1)} collective-permute-done((bf16[136,768]{1,0:T(8,128)(2,1)S(1)}, bf16[136,768]{1,0:T(8,128)(2,1)S(1)}, u32[]{:S(2)}, u32[]{:S(2)}) %collective-permute-start.10) | collective-permute-done | bytes 208928 | tf_op jit(solution)/shard_map/ppermute | solution.py:13
  61.6 4.7 %collective-permute-start.1 = (bf16[136,768]{1,0:T(8,128)(2,1)S(1)}, bf16[136,768]{1,0:T(8,128)(2,1)S(1)}, u32[]{:S(2)}, u32[]{:S(2)}) collective-permute-start(bf16[136,768]{1,0:T(8,128)(2,1)S(1)} %collective-permute-done), channel_id=1, source_target_pairs={{0,16},{16,32},{32,48},{48,64},{64,80},{80,96},{96,112},{112,128},... | collective-permute-start | bytes 626696 | tf_op jit(solution)/shard_map/ppermute | solution.py:13
  66.3 3.4 %collective-permute-done.1 = bf16[136,768]{1,0:T(8,128)(2,1)S(1)} collective-permute-done((bf16[136,768]{1,0:T(8,128)(2,1)S(1)}, bf16[136,768]{1,0:T(8,128)(2,1)S(1)}, u32[]{:S(2)}, u32[]{:S(2)}) %collective-permute-start.1) | collective-permute-done | bytes 208928 | tf_op jit(solution)/shard_map/ppermute | solution.py:13
  69.6 1.9 %collective-permute-start.11 = (bf16[136,768]{1,0:T(8,128)(2,1)S(1)}, bf16[136,768]{1,0:T(8,128)(2,1)S(1)}, u32[]{:S(2)}, u32[]{:S(2)}) collective-permute-start(bf16[136,768]{1,0:T(8,128)(2,1)S(1)} %collective-permute-done.10), channel_id=1, source_target_pairs={{16,0},{32,16},{48,32},{64,48},{80,64},{96,80},{112,96},{128,112},... | collective-permute-start | bytes 626696 | tf_op jit(solution)/shard_map/ppermute | solution.py:13
  71.6 6.1 %collective-permute-done.11 = bf16[136,768]{1,0:T(8,128)(2,1)S(1)} collective-permute-done((bf16[136,768]{1,0:T(8,128)(2,1)S(1)}, bf16[136,768]{1,0:T(8,128)(2,1)S(1)}, u32[]{:S(2)}, u32[]{:S(2)}) %collective-permute-start.11) | collective-permute-done | bytes 208928 | tf_op jit(solution)/shard_map/ppermute | solution.py:13
  77.7 6.0 %collective-permute-start.2 = (bf16[136,768]{1,0:T(8,128)(2,1)S(1)}, bf16[136,768]{1,0:T(8,128)(2,1)S(1)}, u32[]{:S(2)}, u32[]{:S(2)}) collective-permute-start(bf16[136,768]{1,0:T(8,128)(2,1)S(1)} %collective-permute-done.1), channel_id=1, source_target_pairs={{0,16},{16,32},{32,48},{48,64},{64,80},{80,96},{96,112},{112,128},... | collective-permute-start | bytes 626696 | tf_op jit(solution)/shard_map/ppermute | solution.py:13
  83.7 3.3 %collective-permute-done.2 = bf16[136,768]{1,0:T(8,128)(2,1)S(1)} collective-permute-done((bf16[136,768]{1,0:T(8,128)(2,1)S(1)}, bf16[136,768]{1,0:T(8,128)(2,1)S(1)}, u32[]{:S(2)}, u32[]{:S(2)}) %collective-permute-start.2) | collective-permute-done | bytes 208928 | tf_op jit(solution)/shard_map/ppermute | solution.py:13
  87.0 1.9 %collective-permute-start.12 = (bf16[136,768]{1,0:T(8,128)(2,1)S(1)}, bf16[136,768]{1,0:T(8,128)(2,1)S(1)}, u32[]{:S(2)}, u32[]{:S(2)}) collective-permute-start(bf16[136,768]{1,0:T(8,128)(2,1)S(1)} %collective-permute-done.11), channel_id=1, source_target_pairs={{16,0},{32,16},{48,32},{64,48},{80,64},{96,80},{112,96},{128,112},... | collective-permute-start | bytes 626696 | tf_op jit(solution)/shard_map/ppermute | solution.py:13
  88.9 6.2 %collective-permute-done.12 = bf16[136,768]{1,0:T(8,128)(2,1)S(1)} collective-permute-done((bf16[136,768]{1,0:T(8,128)(2,1)S(1)}, bf16[136,768]{1,0:T(8,128)(2,1)S(1)}, u32[]{:S(2)}, u32[]{:S(2)}) %collective-permute-start.12) | collective-permute-done | bytes 208928 | tf_op jit(solution)/shard_map/ppermute | solution.py:13
  95.2 6.0 %collective-permute-start.3 = (bf16[136,768]{1,0:T(8,128)(2,1)S(1)}, bf16[136,768]{1,0:T(8,128)(2,1)S(1)}, u32[]{:S(2)}, u32[]{:S(2)}) collective-permute-start(bf16[136,768]{1,0:T(8,128)(2,1)S(1)} %collective-permute-done.2), channel_id=1, source_target_pairs={{0,16},{16,32},{32,48},{48,64},{64,80},{80,96},{96,112},{112,128},... | collective-permute-start | bytes 626696 | tf_op jit(solution)/shard_map/ppermute | solution.py:13
  101.2 3.3 %collective-permute-done.3 = bf16[136,768]{1,0:T(8,128)(2,1)S(1)} collective-permute-done((bf16[136,768]{1,0:T(8,128)(2,1)S(1)}, bf16[136,768]{1,0:T(8,128)(2,1)S(1)}, u32[]{:S(2)}, u32[]{:S(2)}) %collective-permute-start.3) | collective-permute-done | bytes 208928 | tf_op jit(solution)/shard_map/ppermute | solution.py:13
  104.5 1.9 %collective-permute-start.13 = (bf16[136,768]{1,0:T(8,128)(2,1)S(1)}, bf16[136,768]{1,0:T(8,128)(2,1)S(1)}, u32[]{:S(2)}, u32[]{:S(2)}) collective-permute-start(bf16[136,768]{1,0:T(8,128)(2,1)S(1)} %collective-permute-done.12), channel_id=1, source_target_pairs={{16,0},{32,16},{48,32},{64,48},{80,64},{96,80},{112,96},{128,112},... | collective-permute-start | bytes 626696 | tf_op jit(solution)/shard_map/ppermute | solution.py:13
  106.4 6.2 %collective-permute-done.13 = bf16[136,768]{1,0:T(8,128)(2,1)S(1)} collective-permute-done((bf16[136,768]{1,0:T(8,128)(2,1)S(1)}, bf16[136,768]{1,0:T(8,128)(2,1)S(1)}, u32[]{:S(2)}, u32[]{:S(2)}) %collective-permute-start.13) | collective-permute-done | bytes 208928 | tf_op jit(solution)/shard_map/ppermute | solution.py:13
  112.6 6.0 %collective-permute-start.4 = (bf16[136,768]{1,0:T(8,128)(2,1)S(1)}, bf16[136,768]{1,0:T(8,128)(2,1)}, u32[]{:S(2)}, u32[]{:S(2)}) collective-permute-start(bf16[136,768]{1,0:T(8,128)(2,1)S(1)} %collective-permute-done.3), channel_id=1, source_target_pairs={{0,16},{16,32},{32,48},{48,64},{64,80},{80,96},{96,112},{112,128},... | collective-permute-start | bytes 626696 | tf_op jit(solution)/shard_map/ppermute | solution.py:13
  118.7 3.3 %collective-permute-done.4 = bf16[136,768]{1,0:T(8,128)(2,1)} collective-permute-done((bf16[136,768]{1,0:T(8,128)(2,1)S(1)}, bf16[136,768]{1,0:T(8,128)(2,1)}, u32[]{:S(2)}, u32[]{:S(2)}) %collective-permute-start.4) | collective-permute-done | bytes 208928 | tf_op jit(solution)/shard_map/ppermute | solution.py:13
  122.0 1.9 %collective-permute-start.14 = (bf16[136,768]{1,0:T(8,128)(2,1)S(1)}, bf16[136,768]{1,0:T(8,128)(2,1)S(1)}, u32[]{:S(2)}, u32[]{:S(2)}) collective-permute-start(bf16[136,768]{1,0:T(8,128)(2,1)S(1)} %collective-permute-done.13), channel_id=1, source_target_pairs={{16,0},{32,16},{48,32},{64,48},{80,64},{96,80},{112,96},{128,112},... | collective-permute-start | bytes 626696 | tf_op jit(solution)/shard_map/ppermute | solution.py:13
  123.9 0.9 bitcast_dynamic-update-slice_fusion.11
  124.8 5.4 %collective-permute-done.14 = bf16[136,768]{1,0:T(8,128)(2,1)S(1)} collective-permute-done((bf16[136,768]{1,0:T(8,128)(2,1)S(1)}, bf16[136,768]{1,0:T(8,128)(2,1)S(1)}, u32[]{:S(2)}, u32[]{:S(2)}) %collective-permute-start.14) | collective-permute-done | bytes 208928 | tf_op jit(solution)/shard_map/ppermute | solution.py:13
  130.2 6.0 %collective-permute-start.5 = (bf16[136,768]{1,0:T(8,128)(2,1)}, bf16[136,768]{1,0:T(8,128)(2,1)}, u32[]{:S(2)}, u32[]{:S(2)}) collective-permute-start(bf16[136,768]{1,0:T(8,128)(2,1)} %collective-permute-done.4), channel_id=1, source_target_pairs={{0,16},{16,32},{32,48},{48,64},{64,80},{80,96},{96,112},{112,128},... | collective-permute-start | bytes 626696 | tf_op jit(solution)/shard_map/ppermute | solution.py:13
  136.4 2.7 %fusion.12 = f32[8,256,512]{2,1,0:T(8,128)} fusion(bf16[8,136,768]{2,1,0:T(8,128)(2,1)S(1)} %bitcast_dynamic-update-slice_fusion), kind=kOutput, calls=%fused_computation.18 | convolution fusion | flops 268435456 | bytes 5767168 | tf_op jit(solution)/shard_map/kcd,kce->kde/dot_general | solution.py:69
  139.2 0.7 fusion.48
  145.0 3.2 %fusion.17 = f32[256,512]{1,0:T(8,128)S(1)} fusion(f32[8,256,512]{2,1,0:T(8,128)} %fusion.12, f32[]{:T(128)S(6)} %mul.307, f32[]{:T(128)S(6)} %mul.306, f32[]{:T(128)S(6)} %mul.305, f32[]{:T(128)S(6)} %mul.304, f32[]{:T(128)S(6)} %mul.303, f32[]{:T(128)S(6)} %mul.302, f32[]{:T(128)} %bitcast.44), kind=kLoop, calls=%fused_computation.24 | loop fusion | flops 1835008 | bytes 4718620 | tf_op jit(solution)/shard_map/add | solution.py:83
  148.2 9.7 %collective-permute-start.17 = (f32[256,512]{1,0:T(8,128)S(1)}, f32[256,512]{1,0:T(8,128)}, u32[]{:S(2)}, u32[]{:S(2)}) collective-permute-start(f32[256,512]{1,0:T(8,128)S(1)} %fusion.17), channel_id=1, source_target_pairs={{128,0},{144,16},{160,32},{176,48},{192,64},{208,80},{224,96},{240... | collective-permute-start | bytes 1572872 | tf_op jit(solution)/shard_map/ppermute | solution.py:13
  157.9 0.9 bitcast_dynamic-update-slice_fusion.10
  158.9 0.9 bitcast_dynamic-update-slice_fusion.9
  159.9 0.9 bitcast_dynamic-update-slice_fusion.8
  160.9 0.7 fusion.49
  166.7 0.7 fusion.14
  167.4 1.3 fusion.26
  168.7 1.9 %collective-permute-start.8 = (f32[256,512]{1,0:T(8,128)S(1)}, f32[256,512]{1,0:T(8,128)S(1)}, u32[]{:S(2)}, u32[]{:S(2)}) collective-permute-start(f32[256,512]{1,0:T(8,128)S(1)} %fusion.26), channel_id=1, source_target_pairs={{0,128},{16,144},{32,160},{48,176},{64,192},{80,208},{96,224},{112... | collective-permute-start | bytes 1572872 | tf_op jit(solution)/shard_map/ppermute | solution.py:13
  170.7 2.2 %add_convert_fusion = bf16[256,512]{1,0:T(8,128)(2,1)S(1)} fusion(f32[256,512]{1,0:T(8,128)} %collective-permute-done.17, f32[]{:T(128)S(6)} %mul.308, f32[8,256,512]{2,1,0:T(8,128)S(1)} %copy-done, f32[]{:T(128)S(6)} %mul.307, f32[]{:T(128)S(6)} %mul.306, f32[]{:T(128)S(6)} %mul.305, f32[]{:T(128)S(6)} %mul.304, f32[]{:T(128)S(6)} %mul.303, f32[]{:T(128)S(6)} %mul.302, ...), kind=kLoop, calls=%fused_computation.54 | loop fusion | flops 2228224 | bytes 4980768 | tf_op jit(solution)/shard_map/convert_element_type | solution.py:124
  172.9 0.9 fusion.8
  173.7 0.8 fusion.3
  174.6 6.4 %collective-permute-done.8 = f32[256,512]{1,0:T(8,128)S(1)} collective-permute-done((f32[256,512]{1,0:T(8,128)S(1)}, f32[256,512]{1,0:T(8,128)S(1)}, u32[]{:S(2)}, u32[]{:S(2)}) %collective-permute-start.8) | collective-permute-done | bytes 524320 | tf_op jit(solution)/shard_map/ppermute | solution.py:13
  181.0 1.2 add_convert_fusion.1
  182.2 0.2 fusion.7
  182.5 0.7 copy.241
  183.2 0.8 fusion.2
  (42 shorter events, 0.9 us)
Async XLA Ops:
  0.6 31.4 %copy-start.1 = (bf16[128,512]{1,0:T(8,128)(2,1)S(1)}, bf16[128,512]{1,0:T(8,128)(2,1)}, u32[]{:S(2)}) copy-start(bf16[128,512]{1,0:T(8,128)(2,1)} %param.13) | copy-start | bytes 393220
  2.3 29.6 %all-to-all-start = ((bf16[8,16,1024]{2,0,1:T(8,128)(2,1)}), bf16[8,16,1024]{2,0,1:T(8,128)(2,1)S(1)}, u32[]{:S(2)}, u32[]{:S(2)}) async-start(bf16[8,16,1024]{2,0,1:T(8,128)(2,1)} %pad_maximum_fusion), calls=%async_computation | async-start | bytes 524288 | tf_op jit(solution)/shard_map/all_to_all | solution.py:101
  32.9 16.2 %collective-permute-start.9 = (bf16[136,768]{1,0:T(8,128)(2,1)S(1)}, bf16[136,768]{1,0:T(8,128)(2,1)S(1)}, u32[]{:S(2)}, u32[]{:S(2)}) collective-permute-start(bf16[136,768]{1,0:T(8,128)(2,1)S(1)} %get-tuple-element.90), channel_id=1, source_target_pairs={{16,0},{32,16},{48,32},{64,48},{80,64},{96,80},{112,96},{128,112},... | collective-permute-start | bytes 626696 | tf_op jit(solution)/shard_map/ppermute | solution.py:13
  36.0 100.3 %collective-permute-start.15 = (bf16[136,768]{1,0:T(8,128)(2,1)S(1)}, bf16[136,768]{1,0:T(8,128)(2,1)S(1)}, u32[]{:S(2)}, u32[]{:S(2)}) collective-permute-start(bf16[136,768]{1,0:T(8,128)(2,1)S(1)} %get-tuple-element.90), channel_id=1, source_target_pairs={{112,0},{128,16},{144,32},{160,48},{176,64},{192,80},{208,96},{224... | collective-permute-start | bytes 626696 | tf_op jit(solution)/shard_map/ppermute | solution.py:13
  38.7 97.6 %collective-permute-start.16 = (bf16[136,768]{1,0:T(8,128)(2,1)S(1)}, bf16[136,768]{1,0:T(8,128)(2,1)S(1)}, u32[]{:S(2)}, u32[]{:S(2)}) collective-permute-start(bf16[136,768]{1,0:T(8,128)(2,1)S(1)} %get-tuple-element.90), channel_id=1, source_target_pairs={{128,0},{144,16},{160,32},{176,48},{192,64},{208,80},{224,96},{240... | collective-permute-start | bytes 626696 | tf_op jit(solution)/shard_map/ppermute | solution.py:13
  41.5 11.0 %collective-permute-start = (bf16[136,768]{1,0:T(8,128)(2,1)}, bf16[136,768]{1,0:T(8,128)(2,1)S(1)}, u32[]{:S(2)}, u32[]{:S(2)}) collective-permute-start(bf16[136,768]{1,0:T(8,128)(2,1)} %get-tuple-element.91), channel_id=1, source_target_pairs={{0,16},{16,32},{32,48},{48,64},{64,80},{80,96},{96,112},{112,128},... | collective-permute-start | bytes 626696 | tf_op jit(solution)/shard_map/ppermute | solution.py:13
  45.4 113.5 %collective-permute-start.6 = (bf16[136,768]{1,0:T(8,128)(2,1)}, bf16[136,768]{1,0:T(8,128)(2,1)}, u32[]{:S(2)}, u32[]{:S(2)}) collective-permute-start(bf16[136,768]{1,0:T(8,128)(2,1)} %get-tuple-element.91), channel_id=1, source_target_pairs={{0,112},{16,128},{32,144},{48,160},{64,176},{80,192},{96,208},{112... | collective-permute-start | bytes 626696 | tf_op jit(solution)/shard_map/ppermute | solution.py:13
  49.1 110.8 %collective-permute-start.7 = (bf16[136,768]{1,0:T(8,128)(2,1)}, bf16[136,768]{1,0:T(8,128)(2,1)}, u32[]{:S(2)}, u32[]{:S(2)}) collective-permute-start(bf16[136,768]{1,0:T(8,128)(2,1)} %get-tuple-element.91), channel_id=1, source_target_pairs={{0,128},{16,144},{32,160},{48,176},{64,192},{80,208},{96,224},{112... | collective-permute-start | bytes 626696 | tf_op jit(solution)/shard_map/ppermute | solution.py:13
  52.5 9.0 %collective-permute-start.10 = (bf16[136,768]{1,0:T(8,128)(2,1)S(1)}, bf16[136,768]{1,0:T(8,128)(2,1)S(1)}, u32[]{:S(2)}, u32[]{:S(2)}) collective-permute-start(bf16[136,768]{1,0:T(8,128)(2,1)S(1)} %collective-permute-done.9), channel_id=1, source_target_pairs={{16,0},{32,16},{48,32},{64,48},{80,64},{96,80},{112,96},{128,112},... | collective-permute-start | bytes 626696 | tf_op jit(solution)/shard_map/ppermute | solution.py:13
  61.6 8.1 %collective-permute-start.1 = (bf16[136,768]{1,0:T(8,128)(2,1)S(1)}, bf16[136,768]{1,0:T(8,128)(2,1)S(1)}, u32[]{:S(2)}, u32[]{:S(2)}) collective-permute-start(bf16[136,768]{1,0:T(8,128)(2,1)S(1)} %collective-permute-done), channel_id=1, source_target_pairs={{0,16},{16,32},{32,48},{48,64},{64,80},{80,96},{96,112},{112,128},... | collective-permute-start | bytes 626696 | tf_op jit(solution)/shard_map/ppermute | solution.py:13
  69.6 8.0 %collective-permute-start.11 = (bf16[136,768]{1,0:T(8,128)(2,1)S(1)}, bf16[136,768]{1,0:T(8,128)(2,1)S(1)}, u32[]{:S(2)}, u32[]{:S(2)}) collective-permute-start(bf16[136,768]{1,0:T(8,128)(2,1)S(1)} %collective-permute-done.10), channel_id=1, source_target_pairs={{16,0},{32,16},{48,32},{64,48},{80,64},{96,80},{112,96},{128,112},... | collective-permute-start | bytes 626696 | tf_op jit(solution)/shard_map/ppermute | solution.py:13
  77.7 9.3 %collective-permute-start.2 = (bf16[136,768]{1,0:T(8,128)(2,1)S(1)}, bf16[136,768]{1,0:T(8,128)(2,1)S(1)}, u32[]{:S(2)}, u32[]{:S(2)}) collective-permute-start(bf16[136,768]{1,0:T(8,128)(2,1)S(1)} %collective-permute-done.1), channel_id=1, source_target_pairs={{0,16},{16,32},{32,48},{48,64},{64,80},{80,96},{96,112},{112,128},... | collective-permute-start | bytes 626696 | tf_op jit(solution)/shard_map/ppermute | solution.py:13
  87.0 8.2 %collective-permute-start.12 = (bf16[136,768]{1,0:T(8,128)(2,1)S(1)}, bf16[136,768]{1,0:T(8,128)(2,1)S(1)}, u32[]{:S(2)}, u32[]{:S(2)}) collective-permute-start(bf16[136,768]{1,0:T(8,128)(2,1)S(1)} %collective-permute-done.11), channel_id=1, source_target_pairs={{16,0},{32,16},{48,32},{64,48},{80,64},{96,80},{112,96},{128,112},... | collective-permute-start | bytes 626696 | tf_op jit(solution)/shard_map/ppermute | solution.py:13
  95.2 9.3 %collective-permute-start.3 = (bf16[136,768]{1,0:T(8,128)(2,1)S(1)}, bf16[136,768]{1,0:T(8,128)(2,1)S(1)}, u32[]{:S(2)}, u32[]{:S(2)}) collective-permute-start(bf16[136,768]{1,0:T(8,128)(2,1)S(1)} %collective-permute-done.2), channel_id=1, source_target_pairs={{0,16},{16,32},{32,48},{48,64},{64,80},{80,96},{96,112},{112,128},... | collective-permute-start | bytes 626696 | tf_op jit(solution)/shard_map/ppermute | solution.py:13
  104.5 8.2 %collective-permute-start.13 = (bf16[136,768]{1,0:T(8,128)(2,1)S(1)}, bf16[136,768]{1,0:T(8,128)(2,1)S(1)}, u32[]{:S(2)}, u32[]{:S(2)}) collective-permute-start(bf16[136,768]{1,0:T(8,128)(2,1)S(1)} %collective-permute-done.12), channel_id=1, source_target_pairs={{16,0},{32,16},{48,32},{64,48},{80,64},{96,80},{112,96},{128,112},... | collective-permute-start | bytes 626696 | tf_op jit(solution)/shard_map/ppermute | solution.py:13
  112.6 9.3 %collective-permute-start.4 = (bf16[136,768]{1,0:T(8,128)(2,1)S(1)}, bf16[136,768]{1,0:T(8,128)(2,1)}, u32[]{:S(2)}, u32[]{:S(2)}) collective-permute-start(bf16[136,768]{1,0:T(8,128)(2,1)S(1)} %collective-permute-done.3), channel_id=1, source_target_pairs={{0,16},{16,32},{32,48},{48,64},{64,80},{80,96},{96,112},{112,128},... | collective-permute-start | bytes 626696 | tf_op jit(solution)/shard_map/ppermute | solution.py:13
  122.0 8.3 %collective-permute-start.14 = (bf16[136,768]{1,0:T(8,128)(2,1)S(1)}, bf16[136,768]{1,0:T(8,128)(2,1)S(1)}, u32[]{:S(2)}, u32[]{:S(2)}) collective-permute-start(bf16[136,768]{1,0:T(8,128)(2,1)S(1)} %collective-permute-done.13), channel_id=1, source_target_pairs={{16,0},{32,16},{48,32},{64,48},{80,64},{96,80},{112,96},{128,112},... | collective-permute-start | bytes 626696 | tf_op jit(solution)/shard_map/ppermute | solution.py:13
  130.2 27.7 %collective-permute-start.5 = (bf16[136,768]{1,0:T(8,128)(2,1)}, bf16[136,768]{1,0:T(8,128)(2,1)}, u32[]{:S(2)}, u32[]{:S(2)}) collective-permute-start(bf16[136,768]{1,0:T(8,128)(2,1)} %collective-permute-done.4), channel_id=1, source_target_pairs={{0,16},{16,32},{32,48},{48,64},{64,80},{80,96},{96,112},{112,128},... | collective-permute-start | bytes 626696 | tf_op jit(solution)/shard_map/ppermute | solution.py:13
  148.2 22.4 %collective-permute-start.17 = (f32[256,512]{1,0:T(8,128)S(1)}, f32[256,512]{1,0:T(8,128)}, u32[]{:S(2)}, u32[]{:S(2)}) collective-permute-start(f32[256,512]{1,0:T(8,128)S(1)} %fusion.17), channel_id=1, source_target_pairs={{128,0},{144,16},{160,32},{176,48},{192,64},{208,80},{224,96},{240... | collective-permute-start | bytes 1572872 | tf_op jit(solution)/shard_map/ppermute | solution.py:13
  167.4 3.3 %copy-start = (f32[8,256,512]{2,1,0:T(8,128)S(1)}, f32[8,256,512]{2,1,0:T(8,128)}, u32[]{:S(2)}) copy-start(f32[8,256,512]{2,1,0:T(8,128)} %fusion.12) | copy-start | bytes 12582916
  168.7 12.3 %collective-permute-start.8 = (f32[256,512]{1,0:T(8,128)S(1)}, f32[256,512]{1,0:T(8,128)S(1)}, u32[]{:S(2)}, u32[]{:S(2)}) collective-permute-start(f32[256,512]{1,0:T(8,128)S(1)} %fusion.26), channel_id=1, source_target_pairs={{0,128},{16,144},{32,160},{48,176},{64,192},{80,208},{96,224},{112... | collective-permute-start | bytes 1572872 | tf_op jit(solution)/shard_map/ppermute | solution.py:13
